TPU v7x, 256 devices: a whole 4x4x8 slice. The times are simulated.
256 devices in a mesh: gx: 8 (over x, core), gy: 32 (over y, z).
Axes of the slice: x: 4, y: 4, z: 8, core: 2. Of those that a mesh axis runs over, the one named last changes fastest.
Arguments:
- hidden_in: bfloat16 [8192, 4096], P('gx', 'gy')
- norm_gain: bfloat16 [4096], P('gy'), may hold values from 0.099609375 to 1.8984375
- query_proj: bfloat16 [4096, 4096], P('gx', 'gy')
- kv_proj: bfloat16 [1024, 4096], P(None, 'gy')
- prompt_lengths: int32 [8], replicated, may hold values from 1 to 4096, 8192 in all
- cache_slot: int32 [512], replicated, may hold values from 0 to 511, as said below
Outputs:
- attention: bfloat16 [8192, 4096], P('gy', 'gx')
- kv_cache: bfloat16 [512, 16, 1024], P('gy', None, 'gx')
Inputs may be any that keep to these rules, and one draw needn't show every extreme that they name: `prompt_lengths`: the 8 prompts sum to 8192 tokens; the longest has exactly 4096. `cache_slot`: A permutation of the 512 slots; slot s is held by index s // 16 of gy. The 16 pages of one token block go to any one index at most 1 times, and every index receives exactly 16 pages.
All inputs are finite; a program needn't handle non-finite values.
Results may differ from a plain program's by a relative error of at most 0.0066.
The roundings to bfloat16 on the way count: a program that leaves them out, or rounds other values in their place, can miss the bound.
Values may be sent and summed in bfloat16 or wider, within the bound.
No kernel may reach another device: no remote copies, remote signals or barrier semaphores. Data moves between devices by JAX's collectives and lax.ppermute only.
A program may use at most 128 MiB of HBM per device.

v0:
```python
import math

import jax
import jax.numpy as jnp
from jax import lax
from jax.sharding import PartitionSpec as P

D = 4096
H = 32
KVH = 4
HD = 128
PAGES_DEV = 16


epsilon = 1e-06
rope_base = 5000000.0
masked_out = -1e30


def token_places(prompt_lengths, token_index):
    prompt_ends = jnp.cumsum(prompt_lengths)
    prompt_starts = prompt_ends - prompt_lengths
    segment = jnp.sum((token_index[:, None] >= prompt_ends[None, :]).astype(jnp.int32), axis=1)
    chosen = segment[:, None] == jnp.arange(prompt_lengths.shape[0], dtype=jnp.int32)[None, :]
    opening = jnp.sum(jnp.where(chosen, prompt_starts[None, :], 0), axis=1)
    return (segment, token_index - opening)


def rotate(vectors, places):
    half_size = vectors.shape[-1] // 2
    frequency = rope_base ** (-(jnp.arange(half_size, dtype=jnp.float32) * 2.0) / vectors.shape[-1])
    angles = places.astype(jnp.float32)[:, None] * frequency[None, :]
    cos_part = jnp.cos(angles)[:, None, :]
    sin_part = jnp.sin(angles)[:, None, :]
    leading = vectors[..., :half_size]
    trailing = vectors[..., half_size:]
    return jnp.concatenate(
        [leading * cos_part - trailing * sin_part, trailing * cos_part + leading * sin_part],
        axis=-1,
    )


def local(hidden_in, norm_gain, query_proj, kv_proj, prompt_lengths, cache_slot):
    count_gx = lax.axis_size("gx")
    count_gy = lax.axis_size("gy")
    where_gx = lax.axis_index("gx")
    where_gy = lax.axis_index("gy")
    local_rows = hidden_in.shape[0]
    block_tokens = local_rows * count_gx // count_gy
    all_tokens = block_tokens * count_gy
    heads_here = query_proj.shape[0] // HD
    group_size = H // KVH
    kv_head = where_gx * heads_here // group_size
    contract = (((1,), (1,)), ((), ()))
    kv_width = 2 * HD
    kv_start = kv_head * 2 * HD
    kv_rows = lax.dynamic_slice_in_dim(kv_proj, kv_start, kv_width, 0)
    widened = hidden_in.astype(jnp.float32)
    squares = jnp.sum(widened * widened, axis=1)
    totals = lax.psum(squares, "gy")
    normed = (
        widened * lax.rsqrt(totals / D + epsilon)[:, None] * norm_gain.astype(jnp.float32)[None, :]
    ).astype(jnp.bfloat16)
    gathered = lax.all_gather(normed, "gx", axis=0, tiled=True)
    stacked = jnp.concatenate([query_proj, kv_rows], axis=0)
    projected = lax.psum_scatter(
        lax.dot_general(gathered, stacked, contract, preferred_element_type=jnp.float32),
        "gy",
        scatter_dimension=0,
        tiled=True,
    )
    every_index = jnp.arange(all_tokens, dtype=jnp.int32)
    segment_all, place_all = token_places(prompt_lengths, every_index)
    first_query = where_gy * block_tokens
    token_index = first_query + jnp.arange(block_tokens, dtype=jnp.int32)
    segment_own = lax.dynamic_slice_in_dim(segment_all, first_query, block_tokens, 0)
    place_own = lax.dynamic_slice_in_dim(place_all, first_query, block_tokens, 0)
    query_cols = heads_here * HD
    queries = rotate(
        projected[:, :query_cols].reshape(block_tokens, heads_here, HD), place_own
    ).astype(jnp.bfloat16)
    keys = rotate(projected[:, query_cols : query_cols + HD][:, None, :], place_own)[
        :, 0, :
    ].astype(jnp.bfloat16)
    values = projected[:, query_cols + HD :].astype(jnp.bfloat16)
    cache_cols = jnp.where(where_gx % 2 == 0, keys, values)
    score_scale = 1.0 / math.sqrt(HD)
    last_query = first_query + block_tokens - 1
    first_segment = segment_own[0]
    initial = (
        jnp.full((heads_here, block_tokens), masked_out, jnp.float32),
        jnp.zeros((heads_here, block_tokens), jnp.float32),
        jnp.zeros((heads_here, block_tokens, HD), jnp.float32),
    )
    key_piece = lax.all_gather(keys, "gy", axis=0, tiled=True)
    value_piece = lax.all_gather(values, "gy", axis=0, tiled=True)
    block_count = key_piece.shape[0] // block_tokens
    key_blocks = key_piece.reshape(block_count, block_tokens, HD)
    value_blocks = value_piece.reshape(block_count, block_tokens, HD)

    def one_block(current, inputs):
        key_rows, value_rows, offset = inputs
        block_begin = offset * block_tokens
        key_segment = lax.dynamic_slice_in_dim(segment_all, block_begin, block_tokens, 0)
        skipped = jnp.logical_or(
            block_begin > last_query, key_segment[block_tokens - 1] < first_segment
        )

        def compute(previous):
            running_max, running_sum, running_acc = previous
            key_index = block_begin + jnp.arange(block_tokens, dtype=jnp.int32)
            allowed = (key_segment[None, :] == segment_own[:, None]) & (
                key_index[None, :] <= token_index[:, None]
            )
            scores = (
                jnp.einsum("qhd,kd->hqk", queries, key_rows, preferred_element_type=jnp.float32)
                * score_scale
            )
            scores = jnp.where(allowed[None], scores, masked_out)
            new_max = jnp.maximum(running_max, jnp.max(scores, axis=2))
            weights = jnp.where(allowed[None], jnp.exp(scores - new_max[..., None]), 0.0)
            factor = jnp.exp(running_max - new_max)
            new_sum = running_sum * factor + jnp.sum(weights, axis=2)
            update = jnp.einsum(
                "hqk,kd->hqd",
                weights.astype(jnp.bfloat16),
                value_rows,
                preferred_element_type=jnp.float32,
            )
            return (new_max, new_sum, running_acc * factor[..., None] + update)

        return (lax.cond(skipped, lambda previous: previous, compute, current), None)

    offsets = jnp.arange(block_count, dtype=jnp.int32)
    result, unused = lax.scan(one_block, initial, (key_blocks, value_blocks, offsets))
    final_max, final_sum, final_acc = result
    attention = (
        (final_acc / final_sum[..., None])
        .transpose(1, 0, 2)
        .reshape(block_tokens, query_cols)
        .astype(jnp.bfloat16)
    )
    pages_dev = PAGES_DEV
    page_len = block_tokens // pages_dev
    width_cols = cache_cols.shape[1]
    my_pages = cache_cols.reshape(pages_dev, page_len * width_cols)
    capacity = max(1, pages_dev // count_gy)
    slots_all = count_gy * capacity
    owners = (cache_slot // pages_dev).reshape(count_gy, pages_dev)
    page_range = jnp.arange(pages_dev, dtype=jnp.int32)
    earlier = page_range[None, :] < page_range[:, None]
    same_owner = owners[:, :, None] == owners[:, None, :]
    ranks = jnp.sum((same_owner & earlier[None]).astype(jnp.int32), axis=2)
    my_owner = lax.dynamic_index_in_dim(owners, where_gy, 0, keepdims=False)
    my_rank = lax.dynamic_index_in_dim(ranks, where_gy, 0, keepdims=False)
    target = my_owner * capacity + my_rank
    slot_range = jnp.arange(slots_all, dtype=jnp.int32)
    send_map = (slot_range[:, None] == target[None, :]).astype(jnp.bfloat16)
    outgoing = jnp.dot(send_map, my_pages, preferred_element_type=jnp.float32).astype(jnp.bfloat16)
    incoming = lax.all_to_all(outgoing, "gy", split_axis=0, concat_axis=0, tiled=True)
    wanted = where_gy * pages_dev + page_range
    matches = cache_slot[None, :] == wanted[:, None]
    page_ids = jnp.arange(cache_slot.shape[0], dtype=jnp.int32)
    source_page = jnp.sum(jnp.where(matches, page_ids[None, :], 0), axis=1)
    source_rank = jnp.sum(jnp.where(matches, ranks.reshape(-1)[None, :], 0), axis=1)
    source_slot = source_page // pages_dev * capacity + source_rank
    take_map = (source_slot[:, None] == slot_range[None, :]).astype(jnp.bfloat16)
    cache_block = jnp.dot(take_map, incoming, preferred_element_type=jnp.float32)
    cache_block = cache_block.astype(jnp.bfloat16).reshape(pages_dev, page_len, width_cols)
    return (attention, cache_block)


def solution(mesh):
    return jax.shard_map(
        local,
        mesh=mesh,
        in_specs=(P("gx", "gy"), P("gy"), P("gx", "gy"), P(None, "gy"), P(), P()),
        out_specs=(P("gy", "gx"), P("gy", None, "gx")),
        check_vma=False,
    )
```

profile of v0, /device:TPU:144, one launch (start us, length us, event | category | flops | bytes accessed | tf_op | source)
XLA Modules:
  0.0 692.0 jit_solution(10577667807313542377)
XLA Ops:
  7.2 1.2 fusion.19
  8.4 58.0 %psum.7 = f32[1024]{0:T(1024)S(1)} all-reduce(f32[1024]{0:T(1024)S(1)} %fusion.19), channel_id=1, replica_groups=mesh['gx'=8,'gy'=32] {'gy'}, use_global_device_ids=true, to_apply=%region_1.2 | all-reduce | flops 1024 | bytes 8192 | tf_op jit(solution)/shard_map/psum | solution.py:60
  67.1 1.9 fusion.21
  69.0 39.9 %all-gather.5.cloned.1.call-done = bf16[8192,128]{1,0:T(8,128)(2,1)} async-done(((bf16[1024,128]{1,0:T(8,128)(2,1)}), bf16[8192,128]{1,0:T(8,128)(2,1)}) %all-gather.5.cloned.1.call-update) | async-done | bytes 2097168 | tf_op jit(solution)/shard_map/all_gather | solution.py:64
  109.0 13.3 %fusion.23 = f32[8192,768]{0,1:T(8,128)} fusion(bf16[8192,128]{1,0:T(8,128)(2,1)} %all-gather.5.cloned.1.call-done, bf16[256,128]{1,0:T(8,128)(2,1)S(1)} %constant_dynamic-slice_fusion, bf16[512,128]{1,0:T(8,128)(2,1)} %param.12), kind=kOutput, calls=%fused_computation.42 | convolution fusion | flops 1611005952 | bytes 27459584 | tf_op jit(solution)/shard_map/dot_general | solution.py:67
  123.6 265.1 %reduce-scatter.2.cloned.1.call-done = f32[256,768]{0,1:T(8,128)} async-done(((f32[8192,768]{0,1:T(8,128)}), f32[256,768]{0,1:T(8,128)}) %reduce-scatter.2.cloned.1.call-update) | async-done | bytes 786448 | tf_op jit(solution)/shard_map/reduce_scatter | solution.py:66
  390.0 1.5 bitcast_select_fusion
  397.0 9.8 %all-to-all-start = ((bf16[32,2,1024]{2,1,0:T(2,128)(2,1)}), bf16[32,2,1024]{2,1,0:T(2,128)(2,1)S(1)}, u32[]{:S(2)}, u32[]{:S(2)}) async-start(bf16[32,2,1024]{2,1,0:T(2,128)(2,1)} %reshape.266), calls=%async_computation.1 | async-start | bytes 262144 | tf_op jit(solution)/shard_map/all_to_all | solution.py:160
  407.1 4.2 all-to-all-done
  412.3 53.4 %all-gather.7.cloned.1.call-done = bf16[8192,128]{0,1:T(8,128)(2,1)} async-done(((bf16[256,128]{0,1:T(8,128)(2,1)}), bf16[8192,128]{0,1:T(8,128)(2,1)}) %all-gather.7.cloned.1.call-update) | async-done | bytes 2097168 | tf_op jit(solution)/shard_map/all_gather | solution.py:96
  465.7 3.2 copy.72
  468.9 72.9 %all-gather.9.cloned.1.call-done = bf16[8192,1,128]{0,2,1:T(8,128)(2,1)} async-done(((bf16[256,1,128]{0,2,1:T(8,128)(2,1)}), bf16[8192,1,128]{0,2,1:T(8,128)(2,1)}) %all-gather.9.cloned.1.call-update) | async-done | bytes 2097168 | tf_op jit(solution)/shard_map/all_gather | solution.py:95
  541.8 4.1 copy.71
  546.0 138.6 %while.15 = (s32[]{:T(128)}, f32[4,256]{1,0:T(4,128)S(1)}, f32[4,256]{1,0:T(4,128)S(1)}, f32[4,256,128]{2,1,0:T(8,128)S(1)}, s32[32]{0:T(128)S(1)}, /*index=5*/s...) while((s32[]{:T(128)}, f32[4,256]{1,0:T(4,128)S(1)}, ...), condition=%wide.region_11.12_spmd.clone, body=%wide.region_6.11_spmd.clone.sunk | while | flops 137038352 | bytes 4926361 | solution.py:135
  562.1 2.1 conditional.3
  562.2 1.2 fusion.46
  567.4 2.1 conditional.3
  567.5 1.2 fusion.46
  572.7 2.1 conditional.3
  572.8 1.2 fusion.46
  578.0 2.1 conditional.3
  578.1 1.2 fusion.46
  583.3 2.1 conditional.3
  583.4 1.2 fusion.46
  588.6 2.1 conditional.3
  588.7 1.2 fusion.46
  593.9 2.1 conditional.3
  594.0 1.2 fusion.46
  599.2 2.1 conditional.3
  599.3 1.2 fusion.46
  604.5 2.1 conditional.3
  604.6 1.2 fusion.46
  609.8 2.1 conditional.3
  609.9 1.2 fusion.46
  615.1 2.1 conditional.3
  615.2 1.2 fusion.46
  620.4 2.1 conditional.3
  620.5 1.2 fusion.46
  625.7 2.1 conditional.3
  625.8 1.2 fusion.46
  631.0 2.1 conditional.3
  631.2 1.2 fusion.46
  636.3 2.1 conditional.3
  636.5 1.2 fusion.46
  641.6 2.1 conditional.3
  641.8 1.2 fusion.46
  646.9 2.1 conditional.3
  647.1 1.2 fusion.46
  (353 shorter events, 66.6 us)
Async XLA Ops:
  7.2 61.9 %copy-start = (bf16[1024,128]{1,0:T(8,128)(2,1)S(1)}, bf16[1024,128]{1,0:T(8,128)(2,1)}, u32[]{:S(2)}) copy-start(bf16[1024,128]{1,0:T(8,128)(2,1)} %param.13) | copy-start | bytes 786436
  7.2 101.8 %all-gather.5.cloned.1.call-start = ((), (), s32[]{:S(2)}) async-start(), calls=%async_computation.2 | async-start | bytes 2359296 | tf_op jit(solution)/shard_map/all_gather | solution.py:64
  68.9 319.8 %reduce-scatter.2.cloned.1.call-start = ((), (), s32[]{:S(2)}) async-start(), calls=%async_computation.3 | async-start | bytes 25952256 | tf_op jit(solution)/shard_map/reduce_scatter | solution.py:66
  122.3 0.7 copy-start.2
  122.3 270.6 %copy-start.1 = (s32[512]{0:T(512)S(1)}, s32[512]{0:T(512)}, u32[]{:S(2)}) copy-start(s32[512]{0:T(512)} %param.15) | copy-start | bytes 6148
  122.3 343.4 %all-gather.7.cloned.1.call-start = ((), (), s32[]{:S(2)}) async-start(), calls=%async_computation.4 | async-start | bytes 2162688 | tf_op jit(solution)/shard_map/all_gather | solution.py:96
  388.7 5.6 slice-start
  391.6 150.2 %all-gather.9.cloned.1.call-start = ((), (), s32[]{:S(2)}) async-start(), calls=%async_computation.5 | async-start | bytes 2162688 | tf_op jit(solution)/shard_map/all_gather | solution.py:95
  397.0 14.3 %all-to-all-start = ((bf16[32,2,1024]{2,1,0:T(2,128)(2,1)}), bf16[32,2,1024]{2,1,0:T(2,128)(2,1)S(1)}, u32[]{:S(2)}, u32[]{:S(2)}) async-start(bf16[32,2,1024]{2,1,0:T(2,128)(2,1)} %reshape.266), calls=%async_computation.1 | async-start | bytes 262144 | tf_op jit(solution)/shard_map/all_to_all | solution.py:160
Sparse Core Ops, SparseCore 0:
  69.1 39.8 all-gather.4
  122.5 266.2 reduce-scatter.1
  391.7 73.9 all-gather.6
  468.0 73.7 all-gather.8
where the time goes:
time: 694 us; the launch traced here: 692 us
  waiting for transfers between devices  436 us (63%)
  loops' own time  63.5 us (9%)
  blocking collectives  58 us (8%)
  local copies, waits for them, and re-layouts  52.8 us (8%)
  matrix products  42.2 us (6%)
  other arithmetic  16 us (2%)
  between operations  14 us (2%)
  starting transfers between devices  9.95 us (1%)
    reduce_scatter x1, waiting for transfers between devices, local(): lax.psum_scatter(lax.dot_general(gathered, stacked, contract, preferred_e...  265 us
    all_gather x1, waiting for transfers between devices, local(): key_piece = lax.all_gather(keys, 'gy', axis=0, tiled=True)  72.9 us
    another operation x1, loops' own time, local(): lax.scan(one_block, initial, (key_blocks, value_blocks, offsets))  62.1 us
    psum x1, blocking collectives, local(): totals = lax.psum(squares, 'gy')  58 us
    all_gather x1, waiting for transfers between devices, local(): value_piece = lax.all_gather(values, 'gy', axis=0, tiled=True)  53.4 us
    all_gather x1, waiting for transfers between devices, local(): gathered = lax.all_gather(normed, 'gx', axis=0, tiled=True)  39.9 us
    dot_general x17, matrix products, compute(): jnp.einsum('qhd,kd->hqk', queries, key_rows, preferred_element_type=jnp.f...  19.9 us
    slice x32, local copies, waits for them, and re-layouts, one_block(): key_segment[block_tokens - 1] < first_segment  18.9 us
  transfers between devices with their start and end apart: 5, of which 5 were waited for; matrix products, arithmetic and copies ran while one was open for 1% of the time, Pallas kernels for 0%

commit v1 on v0

v1 whole, which is shorter than its diff:
```python
import math

import jax
import jax.numpy as jnp
from jax import lax
from jax.sharding import PartitionSpec as P

D = 4096
H = 32
KVH = 4
HD = 128
PAGES_DEV = 16
MOST = 4096


epsilon = 1e-06
rope_base = 5000000.0
masked_out = -1e30


def token_places(prompt_lengths, token_index):
    prompt_ends = jnp.cumsum(prompt_lengths)
    prompt_starts = prompt_ends - prompt_lengths
    segment = jnp.sum((token_index[:, None] >= prompt_ends[None, :]).astype(jnp.int32), axis=1)
    chosen = segment[:, None] == jnp.arange(prompt_lengths.shape[0], dtype=jnp.int32)[None, :]
    opening = jnp.sum(jnp.where(chosen, prompt_starts[None, :], 0), axis=1)
    return (segment, token_index - opening)


def rotate(vectors, places):
    half_size = vectors.shape[-1] // 2
    frequency = rope_base ** (-(jnp.arange(half_size, dtype=jnp.float32) * 2.0) / vectors.shape[-1])
    angles = places.astype(jnp.float32)[:, None] * frequency[None, :]
    cos_part = jnp.cos(angles)[:, None, :]
    sin_part = jnp.sin(angles)[:, None, :]
    leading = vectors[..., :half_size]
    trailing = vectors[..., half_size:]
    return jnp.concatenate(
        [leading * cos_part - trailing * sin_part, trailing * cos_part + leading * sin_part],
        axis=-1,
    )


def local(hidden_in, norm_gain, query_proj, kv_proj, prompt_lengths, cache_slot):
    count_gx = lax.axis_size("gx")
    count_gy = lax.axis_size("gy")
    where_gx = lax.axis_index("gx")
    where_gy = lax.axis_index("gy")
    local_rows, local_feats = hidden_in.shape
    features = local_feats * count_gy
    block_tokens = local_rows * count_gx // count_gy
    all_tokens = block_tokens * count_gy
    blocks_per_slab = local_rows // block_tokens
    sub = block_tokens // count_gy
    heads_here = query_proj.shape[0] // HD
    query_cols = heads_here * HD
    is_key = where_gx % 2 == 0

    kv_rows = lax.dynamic_slice_in_dim(kv_proj, where_gx * HD, HD, 0)
    stacked = jnp.concatenate([query_proj, kv_rows], axis=0)
    weights_full = lax.all_gather(stacked, "gy", axis=1, tiled=True)
    gain_full = lax.all_gather(norm_gain, "gy", axis=0, tiled=True)

    pieces = hidden_in.reshape(blocks_per_slab, count_gy, sub, local_feats)
    pieces = lax.all_to_all(pieces, "gy", 1, 1, tiled=True)
    rows_here = lax.all_gather(pieces, "gx", axis=0, tiled=False)
    rows_here = rows_here.transpose(0, 1, 3, 2, 4).reshape(block_tokens, features)
    widened = rows_here.astype(jnp.float32)
    squares = jnp.sum(widened * widened, axis=1)
    normed = (
        widened * lax.rsqrt(squares / features + epsilon)[:, None]
        * gain_full.astype(jnp.float32)[None, :]
    ).astype(jnp.bfloat16)
    contract = (((1,), (1,)), ((), ()))
    projected = lax.dot_general(normed, weights_full, contract, preferred_element_type=jnp.float32)

    order = jnp.arange(block_tokens, dtype=jnp.int32)
    my_tokens = (order // sub) * block_tokens + where_gy * sub + order % sub
    unused_segment, my_places = token_places(prompt_lengths, my_tokens)
    queries = rotate(
        projected[:, :query_cols].reshape(block_tokens, heads_here, HD), my_places
    ).astype(jnp.bfloat16)
    half_raw = projected[:, query_cols:]
    rotated = rotate(half_raw[:, None, :], my_places)[:, 0, :]
    mine = jnp.where(is_key, rotated, half_raw).astype(jnp.bfloat16)

    queries = lax.all_to_all(
        queries.reshape(count_gy, sub, query_cols), "gy", 0, 0, tiled=True
    ).reshape(block_tokens, heads_here, HD)
    mine_all = lax.all_gather(mine.reshape(count_gy, sub, HD), "gy", axis=0, tiled=False)
    mine_all = mine_all.transpose(1, 0, 2, 3).reshape(all_tokens, HD)
    other_all = lax.ppermute(mine_all, "gx", [(p, p ^ 1) for p in range(count_gx)])
    keys = jnp.where(is_key, mine_all, other_all)
    values = jnp.where(is_key, other_all, mine_all)

    every_index = jnp.arange(all_tokens, dtype=jnp.int32)
    segment_all, unused_places = token_places(prompt_lengths, every_index)
    first_query = where_gy * block_tokens
    token_index = first_query + order
    segment_own = lax.dynamic_slice_in_dim(segment_all, first_query, block_tokens, 0)
    window_blocks = min(count_gy, MOST // block_tokens + 1)
    window = window_blocks * block_tokens
    window_start = jnp.clip(where_gy - (window_blocks - 1), 0, count_gy - window_blocks) * block_tokens
    key_rows = lax.dynamic_slice_in_dim(keys, window_start, window, 0)
    value_rows = lax.dynamic_slice_in_dim(values, window_start, window, 0)
    key_segment = lax.dynamic_slice_in_dim(segment_all, window_start, window, 0)
    key_index = window_start + jnp.arange(window, dtype=jnp.int32)
    allowed = (key_segment[None, :] == segment_own[:, None]) & (
        key_index[None, :] <= token_index[:, None]
    )
    score_scale = 1.0 / math.sqrt(HD)
    scores = (
        jnp.einsum("qhd,kd->hqk", queries, key_rows, preferred_element_type=jnp.float32)
        * score_scale
    )
    scores = jnp.where(allowed[None], scores, masked_out)
    row_max = jnp.max(scores, axis=2, keepdims=True)
    weights = jnp.where(allowed[None], jnp.exp(scores - row_max), 0.0)
    totals = jnp.sum(weights, axis=2)
    mixed = jnp.einsum(
        "hqk,kd->hqd", weights.astype(jnp.bfloat16), value_rows, preferred_element_type=jnp.float32
    )
    attention = (
        (mixed / totals[..., None])
        .astype(jnp.bfloat16)
        .transpose(1, 0, 2)
        .reshape(block_tokens, query_cols)
    )

    cache_cols = lax.dynamic_slice_in_dim(mine_all, first_query, block_tokens, 0)
    pages_dev = PAGES_DEV
    page_len = block_tokens // pages_dev
    page_range = jnp.arange(pages_dev, dtype=jnp.int32)
    width_cols = cache_cols.shape[1]
    my_pages = cache_cols.reshape(pages_dev, page_len * width_cols)
    capacity = max(1, pages_dev // count_gy)
    slots_all = count_gy * capacity
    owners = (cache_slot // pages_dev).reshape(count_gy, pages_dev)
    earlier = page_range[None, :] < page_range[:, None]
    same_owner = owners[:, :, None] == owners[:, None, :]
    ranks = jnp.sum((same_owner & earlier[None]).astype(jnp.int32), axis=2)
    my_owner = lax.dynamic_index_in_dim(owners, where_gy, 0, keepdims=False)
    my_rank = lax.dynamic_index_in_dim(ranks, where_gy, 0, keepdims=False)
    target = my_owner * capacity + my_rank
    slot_range = jnp.arange(slots_all, dtype=jnp.int32)
    send_map = (slot_range[:, None] == target[None, :]).astype(jnp.bfloat16)
    outgoing = jnp.dot(send_map, my_pages, preferred_element_type=jnp.float32).astype(jnp.bfloat16)
    incoming = lax.all_to_all(outgoing, "gy", split_axis=0, concat_axis=0, tiled=True)
    wanted = where_gy * pages_dev + page_range
    matches = cache_slot[None, :] == wanted[:, None]
    page_ids = jnp.arange(cache_slot.shape[0], dtype=jnp.int32)
    source_page = jnp.sum(jnp.where(matches, page_ids[None, :], 0), axis=1)
    source_rank = jnp.sum(jnp.where(matches, ranks.reshape(-1)[None, :], 0), axis=1)
    source_slot = source_page // pages_dev * capacity + source_rank
    take_map = (source_slot[:, None] == slot_range[None, :]).astype(jnp.bfloat16)
    cache_block = jnp.dot(take_map, incoming, preferred_element_type=jnp.float32)
    cache_block = cache_block.astype(jnp.bfloat16).reshape(pages_dev, page_len, width_cols)
    return (attention, cache_block)


def solution(mesh):
    return jax.shard_map(
        local,
        mesh=mesh,
        in_specs=(P("gx", "gy"), P("gy"), P("gx", "gy"), P(None, "gy"), P(), P()),
        out_specs=(P("gy", "gx"), P("gy", None, "gx")),
        check_vma=False,
    )
```

time: 694 us -> 318 us (0.46)
  the two profiles are of different devices: /device:TPU:144 before, /device:TPU:2 now
where the time goes in v1:
time: 318 us; the launch traced here: 317 us
  waiting for transfers between devices  164 us (52%)
  blocking collectives  60.2 us (19%)
  other arithmetic  37.6 us (12%)
  matrix products  21.2 us (7%)
  between operations  14 us (4%)
  starting transfers between devices  10.9 us (3%)
  local copies, waits for them, and re-layouts  9.22 us (3%)
    all_gather x1, waiting for transfers between devices, local(): lax.all_gather(mine.reshape(count_gy, sub, HD), 'gy', axis=0, tiled=False)  77.7 us
    all_gather x1, waiting for transfers between devices, local(): weights_full = lax.all_gather(stacked, 'gy', axis=1, tiled=True)  67.4 us
    all_gather x1, blocking collectives, local(): gain_full = lax.all_gather(norm_gain, 'gy', axis=0, tiled=True)  36.5 us
    all_to_all x1, blocking collectives, local(): pieces = lax.all_to_all(pieces, 'gy', 1, 1, tiled=True)  23.7 us
    sub x1, other arithmetic, local(): weights = jnp.where(allowed[None], jnp.exp(scores - row_max), 0.0)  18.1 us
    dot_general x1, matrix products, local(): jnp.einsum('qhd,kd->hqk', queries, key_rows, preferred_element_type=jnp.f...  9.99 us
    all_to_all x1, waiting for transfers between devices, local(): lax.all_to_all(queries.reshape(count_gy, sub, query_cols), 'gy', 0, 0, ti...  9.77 us
    all_to_all x1, waiting for transfers between devices, local(): lax.all_to_all(outgoing, 'gy', split_axis=0, concat_axis=0, tiled=True)  9.12 us
  transfers between devices with their start and end apart: 6, of which 4 were waited for; matrix products, arithmetic and copies ran while one was open for 7% of the time, Pallas kernels for 0%

profile of v1, /device:TPU:2, one launch (start us, length us, event | category | flops | bytes accessed | tf_op | source)
XLA Modules:
  0.0 317.1 jit_solution(16310074648877330027)
XLA Ops:
  7.2 1.0 copy.44
  8.3 23.7 %all_to_all.22 = bf16[4,32,8,128]{3,2,0,1:T(8,128)(2,1)S(1)} all-to-all(bf16[4,32,8,128]{3,2,0,1:T(8,128)(2,1)S(1)} %copy.44), channel_id=1, replica_groups=mesh['gx'=8,'gy'=32] {'gy'}, dimensions={1} | all-to-all | bytes 524288 | tf_op jit(solution)/shard_map/all_to_all | solution.py:65
  32.0 0.7 copy.45
  32.8 1.6 pad_maximum_fusion.1
  34.5 36.5 %all-gather.1 = bf16[32,1,128]{2,1,0:T(2,128)(2,1)S(1)} all-gather(bf16[1,1,128]{2,1,0:T(2,128)(2,1)} %bitcast.75), channel_id=1, replica_groups=mesh['gx'=8,'gy'=32] {'gy'}, dimensions={0}, use_global_device_ids=true | all-gather | bytes 8448 | tf_op jit(solution)/shard_map/all_gather | solution.py:62
  71.0 0.8 reduce-window.8
  71.8 0.1 convert_reduce_fusion.2
  71.9 0.7 bitcast_subtract_fusion
  72.6 0.1 select_reduce_fusion
  72.7 2.1 multiply_reduce_fusion
  74.8 0.1 rsqrt.11
  74.9 4.1 %bitcast_convert_fusion = f32[8,4,32,8,128]{4,3,2,1,0:T(8,128)} fusion(bf16[32,32,8,128]{3,2,1,0:T(8,128)(2,1)} %all-gather.10.cloned.1.call-done), kind=kLoop, calls=%fused_computation.103 | loop fusion | flops 1048576 | bytes 6291456 | tf_op jit(solution)/shard_map/convert_element_type | solution.py:68
  79.0 67.4 %all-gather.6.cloned.1.call-done = bf16[640,4096]{1,0:T(8,128)(2,1)} async-done(((bf16[640,128]{1,0:T(8,128)(2,1)}), bf16[640,4096]{1,0:T(8,128)(2,1)}) %all-gather.6.cloned.1.call-update) | async-done | bytes 5242896 | tf_op jit(solution)/shard_map/all_gather | solution.py:61
  146.4 5.6 %fusion.8 = f32[256,640]{1,0:T(8,128)S(1)} fusion(bf16[640,4096]{1,0:T(8,128)(2,1)} %all-gather.6.cloned.1.call-done, f32[256,4096]{1,0:T(8,128)} %bitcast.62, f32[4096]{0:T(1024)S(1)} %bitcast.71, f32[256]{0:T(256)S(1)} %rsqrt.11), kind=kOutput, calls=%fused_computation.15 | convolution fusion | flops 1345323008 | bytes 10109952 | tf_op jit(solution)/shard_map/dot_general | solution.py:75
  152.0 0.6 fusion.37
  152.6 0.7 fusion.43
  153.4 0.1 convert_reduce_fusion
  153.5 0.1 dynamic_slice.25
  153.7 1.2 multiply_cosine_fusion
  154.9 77.7 %all-gather.8.cloned.1.call-done = bf16[32,32,8,128]{3,2,1,0:T(8,128)(2,1)} async-done(((bf16[1,32,8,128]{3,2,1,0:T(8,128)(2,1)}), bf16[32,32,8,128]{3,2,1,0:T(8,128)(2,1)}) %all-gather.8.cloned.1.call-update) | async-done | bytes 2097168 | tf_op jit(solution)/shard_map/all_gather | solution.py:90
  232.6 2.2 copy.46
  234.8 0.1 collective-permute-start
  234.9 4.4 %compare_and_fusion = pred[256,4352]{0,1:T(8,128)(4,1)} fusion(s32[256]{0:T(256)S(1)} %iota_add_fusion.1, s32[256]{0:T(256)S(1)} %dynamic_slice.26, s32[4352]{0:T(1024)S(1)} %iota_add_fusion, s32[4352]{0:T(1024)S(1)} %dynamic_slice.25), kind=kLoop, calls=%fused_computation.9 | loop fusion | flops 3342336 | bytes 1150976 | tf_op jit(solution)/shard_map/and | solution.py:108
  239.3 0.2 reshape.312
  239.5 1.4 subtract_convert_fusion
  240.9 0.4 pad_maximum_fusion
  241.3 0.8 convert_element_type.69
  242.1 5.6 %all-to-all-start.1 = ((bf16[32,8,512]{2,1,0:T(8,128)(2,1)}), bf16[32,8,512]{2,1,0:T(8,128)(2,1)S(1)}, u32[]{:S(2)}, u32[]{:S(2)}) async-start(bf16[32,8,512]{2,1,0:T(8,128)(2,1)} %convert_element_type.69), calls=%async_computation.1 | async-start | bytes 524288 | tf_op jit(solution)/shard_map/all_to_all | solution.py:87
  247.7 0.1 eq.103
  247.9 0.1 convert_reduce_fusion.1
  248.1 0.1 broadcast_in_dim.96
  248.1 0.2 add_reduce_fusion
  248.4 0.2 fusion.7
  248.6 0.5 broadcast.313
  249.1 0.7 reduce.4
  249.8 0.7 reshape.327
  250.5 9.8 %all-to-all-done.1 = bf16[32,8,512]{2,1,0:T(8,128)(2,1)S(1)} async-done(((bf16[32,8,512]{2,1,0:T(8,128)(2,1)}), bf16[32,8,512]{2,1,0:T(8,128)(2,1)S(1)}, u32[]{:S(2)}, u32[]{:S(2)}) %all-to-all-start.1) | async-done | bytes 262176 | tf_op jit(solution)/shard_map/all_to_all | solution.py:87
  260.3 5.1 %all-to-all-start.2 = ((bf16[32,2,1024]{2,1,0:T(2,128)(2,1)}), bf16[32,2,1024]{2,1,0:T(2,128)(2,1)S(1)}, u32[]{:S(2)}, u32[]{:S(2)}) async-start(bf16[32,2,1024]{2,1,0:T(2,128)(2,1)} %reshape.327), calls=%async_computation.2 | async-start | bytes 262144 | tf_op jit(solution)/shard_map/all_to_all | solution.py:148
  265.4 0.2 fusion.44
  265.6 0.8 reshape.313
  266.3 9.1 %all-to-all-done.2 = bf16[32,2,1024]{2,1,0:T(2,128)(2,1)S(1)} async-done(((bf16[32,2,1024]{2,1,0:T(2,128)(2,1)}), bf16[32,2,1024]{2,1,0:T(2,128)(2,1)S(1)}, u32[]{:S(2)}, u32[]{:S(2)}) %all-to-all-start.2) | async-done | bytes 131104 | tf_op jit(solution)/shard_map/all_to_all | solution.py:148
  275.5 0.1 reshape.328
  275.6 0.2 fusion.20
  275.8 0.6 copy.60
  276.4 10.0 %fusion.22 = f32[4352,256,4]{1,0,2:T(8,128)} fusion(pred[]{:T(512)S(6)} %eq.96, bf16[8192,128]{1,0:T(8,128)(2,1)} %collective-permute-done, s32[]{:T(128)S(6)} %select_n.101, bf16[8192,128]{1,0:T(8,128)(2,1)S(1)} %bitcast.66, bf16[256,4,128]{2,1,0:T(4,128)(2,1)} %reshape.313), kind=kOutput, calls=%fused_computation.23 | convolution fusion | flops 1141407744 | bytes 20316164 | tf_op jit(solution)/shard_map/qhd,kd->hqk/dot_general | solution.py:113
  286.4 18.1 %fusion.60 = (f32[4,256]{1,0:T(4,128)S(1)}, bf16[4,256,4352]{1,2,0:T(8,128)(2,1)}) fusion(f32[4352,256,4]{1,0,2:T(8,128)} %fusion.22, pred[256,4352]{0,1:T(8,128)(4,1)S(1)} %copy-done.1), kind=kOutput, calls=%fused_computation.107 | output fusion | flops 35655936 | bytes 27856896 | tf_op jit(solution)/shard_map/sub | solution.py:118
  304.5 5.3 %fusion.17 = bf16[256,4,128]{0,2,1:T(8,128)(2,1)S(1)} fusion(bf16[4,256,4352]{1,2,0:T(8,128)(2,1)} %get-tuple-element.23, pred[]{:T(512)S(6)} %eq.96, bf16[8192,128]{1,0:T(8,128)(2,1)} %collective-permute-done, s32[]{:T(128)S(6)} %select_n.101, bf16[8192,128]{1,0:T(8,128)(2,1)S(1)} %bitcast.67, f32[256,4]{0,1:T(4,128)S(1)} %bitcast.77), kind=kOutput, calls=%fused_computation.20 | convolution fusion | flops 1141669888 | bytes 11407365 | tf_op jit(solution)/shard_map/hqk,kd->hqd/dot_general | solution.py:120
  309.8 0.8 copy.55
  (33 shorter events, 0.6 us)
Async XLA Ops:
  7.2 25.7 %copy-start = (bf16[1024,128]{1,0:T(8,128)(2,1)S(1)}, bf16[1024,128]{1,0:T(8,128)(2,1)}, u32[]{:S(2)}) copy-start(bf16[1024,128]{1,0:T(8,128)(2,1)} %param.9) | copy-start | bytes 786436
  7.2 65.5 %all-gather.10.cloned.1.call-start = ((), (), s32[]{:S(2)}) async-start(), calls=%async_computation.5 | async-start | bytes 2359296 | tf_op jit(solution)/shard_map/all_gather | solution.py:66
  32.8 113.6 %all-gather.6.cloned.1.call-start = ((), (), s32[]{:S(2)}) async-start(), calls=%async_computation.3 | async-start | bytes 5406720 | tf_op jit(solution)/shard_map/all_gather | solution.py:61
  34.4 198.2 %all-gather.8.cloned.1.call-start = ((), (), s32[]{:S(2)}) async-start(), calls=%async_computation.4 | async-start | bytes 2162688 | tf_op jit(solution)/shard_map/all_gather | solution.py:90
  146.4 7.3 %copy-start.2 = (s32[512]{0:T(512)S(1)}, s32[512]{0:T(512)}, u32[]{:S(2)}) copy-start(s32[512]{0:T(512)} %param.11) | copy-start | bytes 6148
  234.8 41.6 %collective-permute-start = (bf16[8192,128]{1,0:T(8,128)(2,1)S(1)}, bf16[8192,128]{1,0:T(8,128)(2,1)}, u32[]{:S(2)}, u32[]{:S(2)}) collective-permute-start(bf16[8192,128]{1,0:T(8,128)(2,1)S(1)} %bitcast.64), channel_id=1, source_target_pairs={{0,32},{32,0},{64,96},{96,64},{128,160},{160,128},{192,224},{224,1... | collective-permute-start | bytes 6291464 | tf_op jit(solution)/shard_map/ppermute | solution.py:92
  242.1 18.1 %all-to-all-start.1 = ((bf16[32,8,512]{2,1,0:T(8,128)(2,1)}), bf16[32,8,512]{2,1,0:T(8,128)(2,1)S(1)}, u32[]{:S(2)}, u32[]{:S(2)}) async-start(bf16[32,8,512]{2,1,0:T(8,128)(2,1)} %convert_element_type.69), calls=%async_computation.1 | async-start | bytes 524288 | tf_op jit(solution)/shard_map/all_to_all | solution.py:87
  260.3 15.2 %all-to-all-start.2 = ((bf16[32,2,1024]{2,1,0:T(2,128)(2,1)}), bf16[32,2,1024]{2,1,0:T(2,128)(2,1)S(1)}, u32[]{:S(2)}, u32[]{:S(2)}) async-start(bf16[32,2,1024]{2,1,0:T(2,128)(2,1)} %reshape.327), calls=%async_computation.2 | async-start | bytes 262144 | tf_op jit(solution)/shard_map/all_to_all | solution.py:148
  276.4 10.0 %copy-start.1 = (pred[256,4352]{0,1:T(8,128)(4,1)S(1)}, pred[256,4352]{0,1:T(8,128)(4,1)}, u32[]{:S(2)}) copy-start(pred[256,4352]{0,1:T(8,128)(4,1)} %compare_and_fusion) | copy-start | bytes 3342340
Sparse Core Ops, SparseCore 0:
  32.9 22.5 all-gather.9
  57.9 88.4 all-gather.5
  153.5 79.0 all-gather.7

commit v2 on v1

--- a/solution.py
+++ b/solution.py
@@ -57,13 +57,19 @@
     is_key = where_gx % 2 == 0
 
     kv_rows = lax.dynamic_slice_in_dim(kv_proj, where_gx * HD, HD, 0)
-    stacked = jnp.concatenate([query_proj, kv_rows], axis=0)
-    weights_full = lax.all_gather(stacked, "gy", axis=1, tiled=True)
-    gain_full = lax.all_gather(norm_gain, "gy", axis=0, tiled=True)
+    gain_rows = jnp.concatenate(
+        [norm_gain[None, :], jnp.zeros((7, local_feats), norm_gain.dtype)], axis=0
+    )
+    stacked = jnp.concatenate([query_proj, kv_rows, gain_rows], axis=0)
+    gathered = lax.all_gather(stacked, "gy", axis=1, tiled=True)
+    weight_rows = query_cols + HD
+    weights_full = gathered[:weight_rows]
+    gain_full = gathered[weight_rows]
 
     pieces = hidden_in.reshape(blocks_per_slab, count_gy, sub, local_feats)
     pieces = lax.all_to_all(pieces, "gy", 1, 1, tiled=True)
-    rows_here = lax.all_gather(pieces, "gx", axis=0, tiled=False)
+    spread = jnp.broadcast_to(pieces[None], (count_gx,) + pieces.shape)
+    rows_here = lax.all_to_all(spread, "gx", 0, 0, tiled=True)
     rows_here = rows_here.transpose(0, 1, 3, 2, 4).reshape(block_tokens, features)
     widened = rows_here.astype(jnp.float32)
     squares = jnp.sum(widened * widened, axis=1)
@@ -84,25 +90,36 @@
     rotated = rotate(half_raw[:, None, :], my_places)[:, 0, :]
     mine = jnp.where(is_key, rotated, half_raw).astype(jnp.bfloat16)
 
-    queries = lax.all_to_all(
-        queries.reshape(count_gy, sub, query_cols), "gy", 0, 0, tiled=True
-    ).reshape(block_tokens, heads_here, HD)
-    mine_all = lax.all_gather(mine.reshape(count_gy, sub, HD), "gy", axis=0, tiled=False)
-    mine_all = mine_all.transpose(1, 0, 2, 3).reshape(all_tokens, HD)
-    other_all = lax.ppermute(mine_all, "gx", [(p, p ^ 1) for p in range(count_gx)])
-    keys = jnp.where(is_key, mine_all, other_all)
-    values = jnp.where(is_key, other_all, mine_all)
+    other = lax.ppermute(mine, "gx", [(p, p ^ 1) for p in range(count_gx)])
+    both = jnp.concatenate(
+        [jnp.where(is_key, mine, other), jnp.where(is_key, other, mine)], axis=1
+    ).reshape(count_gy, sub, 2 * HD)
+    window_blocks = min(count_gy, MOST // block_tokens + 1)
+    window = window_blocks * block_tokens
+    first_blocks = [min(max(b - (window_blocks - 1), 0), count_gy - window_blocks) for b in range(count_gy)]
+    chosen = jnp.asarray(
+        [[f + w for w in range(window_blocks)] for f in first_blocks], dtype=jnp.int32
+    )
+    kv_parcel = jnp.take(both, chosen, axis=0).reshape(count_gy, window_blocks * sub * 2 * HD)
+    q_parcel = queries.reshape(count_gy, sub * query_cols)
+    parcel = jnp.concatenate([q_parcel, kv_parcel], axis=1)
+    arrived = lax.all_to_all(parcel, "gy", 0, 0, tiled=True)
+    queries = arrived[:, : sub * query_cols].reshape(block_tokens, heads_here, HD)
+    kv_rows_all = (
+        arrived[:, sub * query_cols :]
+        .reshape(count_gy, window_blocks, sub, 2 * HD)
+        .transpose(1, 0, 2, 3)
+        .reshape(window, 2 * HD)
+    )
+    key_rows = kv_rows_all[:, :HD]
+    value_rows = kv_rows_all[:, HD:]
 
     every_index = jnp.arange(all_tokens, dtype=jnp.int32)
     segment_all, unused_places = token_places(prompt_lengths, every_index)
     first_query = where_gy * block_tokens
     token_index = first_query + order
     segment_own = lax.dynamic_slice_in_dim(segment_all, first_query, block_tokens, 0)
-    window_blocks = min(count_gy, MOST // block_tokens + 1)
-    window = window_blocks * block_tokens
     window_start = jnp.clip(where_gy - (window_blocks - 1), 0, count_gy - window_blocks) * block_tokens
-    key_rows = lax.dynamic_slice_in_dim(keys, window_start, window, 0)
-    value_rows = lax.dynamic_slice_in_dim(values, window_start, window, 0)
     key_segment = lax.dynamic_slice_in_dim(segment_all, window_start, window, 0)
     key_index = window_start + jnp.arange(window, dtype=jnp.int32)
     allowed = (key_segment[None, :] == segment_own[:, None]) & (
@@ -127,7 +144,8 @@
         .reshape(block_tokens, query_cols)
     )
 
-    cache_cols = lax.dynamic_slice_in_dim(mine_all, first_query, block_tokens, 0)
+    own_block = lax.dynamic_slice_in_dim(kv_rows_all, first_query - window_start, block_tokens, 0)
+    cache_cols = jnp.where(is_key, own_block[:, :HD], own_block[:, HD:])
     pages_dev = PAGES_DEV
     page_len = block_tokens // pages_dev
     page_range = jnp.arange(pages_dev, dtype=jnp.int32)

time: 318 us -> 257 us (0.81)
  waiting for transfers between devices: 164 us -> 110 us
  blocking collectives: 60.2 us -> 23.8 us
  local copies, waits for them, and re-layouts: 9.22 us -> 29.1 us
  starting transfers between devices: 10.9 us -> 20.9 us
    all_gather x3 -> x1, waiting for transfers between devices: 145 us -> 31.5 us  [local(): gathered = lax.all_gather(stacked, 'gy', axis=1, tiled=True)]
    all_to_all x1 -> x2, waiting for transfers between devices: 9.77 us -> 78.7 us  [the longest x1 54 us: local(): arrived = lax.all_to_all(parcel, 'gy', 0, 0, tiled=True)]
    all_gather x1 -> x0, blocking collectives: 36.5 us -> none  [local(): gain_full = lax.all_gather(norm_gain, 'gy', axis=0, tiled=True)]
    unnamed x10 -> x18, local copies, waits for them, and re-layouts: 2.34 us -> 19.2 us
    all_to_all x1, waiting for transfers between devices: 9.12 us -> 0.01 us  [local(): lax.all_to_all(outgoing, 'gy', split_axis=0, concat_axis=0, tiled=True)]
    all_to_all x1 -> x2, starting transfers between devices: 5.58 us -> 14.5 us  [the longest x1 9.72 us: local(): arrived = lax.all_to_all(parcel, 'gy', 0, 0, tiled=True)]
    all_to_all x0 -> x2, other arithmetic: none -> 5.05 us  [local(): arrived = lax.all_to_all(parcel, 'gy', 0, 0, tiled=True)]
  transfers between devices with their start and end apart: 6 -> 5, of which waited for: 4 -> 3; matrix products, arithmetic and copies ran while one was open for 7% -> 15% of each run, Pallas kernels for 0% -> 0%
where the time goes in v2:
time: 257 us; the launch traced here: 255 us
  waiting for transfers between devices  110 us (43%)
  other arithmetic  37.5 us (15%)
  local copies, waits for them, and re-layouts  29.1 us (11%)
  blocking collectives  23.8 us (9%)
  starting transfers between devices  20.9 us (8%)
  matrix products  19.6 us (8%)
  between operations  14.3 us (6%)
    all_to_all x1, waiting for transfers between devices, local(): arrived = lax.all_to_all(parcel, 'gy', 0, 0, tiled=True)  54 us
    all_gather x1, waiting for transfers between devices, local(): gathered = lax.all_gather(stacked, 'gy', axis=1, tiled=True)  31.5 us
    all_to_all x1, waiting for transfers between devices, local(): rows_here = lax.all_to_all(spread, 'gx', 0, 0, tiled=True)  24.8 us
    all_to_all x1, blocking collectives, local(): pieces = lax.all_to_all(pieces, 'gy', 1, 1, tiled=True)  23.8 us
    unnamed x18, local copies, waits for them, and re-layouts  19.2 us
    sub x1, other arithmetic, local(): weights = jnp.where(allowed[None], jnp.exp(scores - row_max), 0.0)  18.6 us
    all_to_all x1, starting transfers between devices, local(): arrived = lax.all_to_all(parcel, 'gy', 0, 0, tiled=True)  9.72 us
    dot_general x1, matrix products, local(): jnp.einsum('qhd,kd->hqk', queries, key_rows, preferred_element_type=jnp.f...  8.6 us
  transfers between devices with their start and end apart: 5, of which 3 were waited for; matrix products, arithmetic and copies ran while one was open for 15% of the time, Pallas kernels for 0%

profile of v2, /device:TPU:2, one launch (start us, length us, event | category | flops | bytes accessed | tf_op | source)
XLA Modules:
  0.0 255.4 jit_solution(8031653901322891832)
XLA Ops:
  7.2 0.9 copy-done
  8.2 1.7 maximum_maximum_fusion
  10.0 1.0 copy.46
  11.0 23.8 %all_to_all.34 = bf16[4,32,8,128]{3,2,0,1:T(8,128)(2,1)S(1)} all-to-all(bf16[4,32,8,128]{3,2,0,1:T(8,128)(2,1)S(1)} %copy.46), channel_id=1, replica_groups=mesh['gx'=8,'gy'=32] {'gy'}, dimensions={1} | all-to-all | bytes 524288 | tf_op jit(solution)/shard_map/all_to_all | solution.py:70
  34.8 1.8 broadcast_in_dim.71
  36.7 4.8 %all-to-all-start.1 = ((bf16[8,4,32,8,128]{4,3,2,1,0:T(8,128)(2,1)}), bf16[8,4,32,8,128]{4,3,2,1,0:T(8,128)(2,1)S(1)}, u32[]{:S(2)}, u32[]{:S(2)}) async-start(bf16[8,4,32,8,128]{4,3,2,1,0:T(8,128)(2,1)} %broadcast_in_dim.71), calls=%async_computation.1 | async-start | bytes 4194304 | tf_op jit(solution)/shard_map/all_to_all | solution.py:72
  41.5 0.2 reduce-window.8
  41.9 0.5 multiply_cosine_fusion.1
  42.5 24.8 %all-to-all-done.1 = bf16[8,4,32,8,128]{4,3,2,1,0:T(8,128)(2,1)S(1)} async-done(((bf16[8,4,32,8,128]{4,3,2,1,0:T(8,128)(2,1)}), bf16[8,4,32,8,128]{4,3,2,1,0:T(8,128)(2,1)S(1)}, u32[]{:S(2)}, u32[]{:S(2)}) %all-to-all-start.1) | async-done | bytes 2097184 | tf_op jit(solution)/shard_map/all_to_all | solution.py:72
  67.2 0.5 multiply_reduce_fusion
  67.8 2.5 convert_element_type.74
  70.3 31.5 %all-gather.2.cloned.1.call-done = bf16[648,4096]{1,0:T(8,128)(2,1)} async-done(((bf16[648,128]{1,0:T(8,128)(2,1)}), bf16[648,4096]{1,0:T(8,128)(2,1)}) %all-gather.2.cloned.1.call-update) | async-done | bytes 5308432 | tf_op jit(solution)/shard_map/all_gather | solution.py:64
  101.8 0.8 slice_convert_fusion
  102.7 5.6 %fusion.7 = f32[256,640]{1,0:T(8,128)S(1)} fusion(bf16[648,4096]{1,0:T(8,128)(2,1)} %all-gather.2.cloned.1.call-done, f32[256,4096]{1,0:T(8,128)} %bitcast.72, f32[4096]{0:T(1024)S(1)} %bitcast.76, f32[256]{0:T(256)S(1)} %rsqrt.11), kind=kOutput, calls=%fused_computation.10 | convolution fusion | flops 1345323008 | bytes 10109952 | tf_op jit(solution)/shard_map/dot_general | solution.py:81
  108.4 0.6 fusion.28
  109.2 0.2 reshape.329
  109.4 0.5 subtract_convert_fusion
  109.8 0.4 pad_maximum_fusion
  110.2 0.2 convert_element_type.66
  110.4 2.4 gather_fusion
  112.9 2.4 select_n.129
  115.3 1.8 maximum_bitcast_fusion
  117.1 0.5 broadcast.328
  117.6 3.3 %reduce.4 = bf16[32,38912]{1,0:T(8,128)(2,1)} reduce(bf16[32,1,38912]{2,0,1:T(8,128)(2,1)S(1)} %maximum_bitcast_fusion, bf16[]{:T(256)} %broadcast.328), dimensions={1}, to_apply=%copy.48.reduce_sub_computation | reduce | bytes 4980738 | tf_op jit(solution)/shard_map/all_to_all | solution.py:106
  120.8 4.8 %reshape.352 = bf16[32,2,19456]{2,1,0:T(2,128)(2,1)} reshape(bf16[32,38912]{1,0:T(8,128)(2,1)} %reduce.4) | data formatting | bytes 4980736
  125.7 9.7 %all-to-all-start.2 = ((bf16[32,2,19456]{2,1,0:T(2,128)(2,1)}), bf16[32,2,19456]{2,1,0:T(2,128)(2,1)S(1)}, u32[]{:S(2)}, u32[]{:S(2)}) async-start(bf16[32,2,19456]{2,1,0:T(2,128)(2,1)} %reshape.352), calls=%async_computation.2 | async-start | bytes 4980736 | tf_op jit(solution)/shard_map/all_to_all | solution.py:106
  135.4 0.1 convert_reduce_fusion
  135.9 0.1 convert_reduce_fusion.1
  136.2 0.2 add_reduce_fusion
  136.4 0.2 fusion.34
  136.6 4.3 %compare_and_fusion = pred[256,4352]{0,1:T(8,128)(4,1)} fusion(s32[256]{0:T(256)S(1)} %iota_add_fusion.1, s32[256]{0:T(256)S(1)} %dynamic_slice.20, s32[4352]{0:T(1024)S(1)} %iota_add_fusion, s32[4352]{0:T(1024)S(1)} %dynamic_slice.19), kind=kLoop, calls=%fused_computation.12 | loop fusion | flops 3342336 | bytes 1150976 | tf_op jit(solution)/shard_map/and | solution.py:125
  140.9 54.0 %all-to-all-done.2 = bf16[32,2,19456]{2,1,0:T(2,128)(2,1)S(1)} async-done(((bf16[32,2,19456]{2,1,0:T(2,128)(2,1)}), bf16[32,2,19456]{2,1,0:T(2,128)(2,1)S(1)}, u32[]{:S(2)}, u32[]{:S(2)}) %all-to-all-start.2) | async-done | bytes 2490400 | tf_op jit(solution)/shard_map/all_to_all | solution.py:106
  194.9 6.8 %reshape.353 = bf16[32,1,38912]{2,1,0:T(2,128)(2,1)} reshape(bf16[32,2,19456]{2,1,0:T(2,128)(2,1)S(1)} %all-to-all-done.2) | data formatting | bytes 4980736
  201.7 3.9 %copy.73 = bf16[32,1,38912]{2,0,1:T(8,128)(2,1)S(1)} copy(bf16[32,1,38912]{2,1,0:T(2,128)(2,1)} %reshape.353) | data formatting | bytes 4980736
  205.6 0.1 slice.66
  205.8 0.4 copy.64
  206.2 0.2 copy.49
  206.4 0.2 reshape.333
  206.6 8.6 %fusion.22 = f32[4352,256,4]{1,0,2:T(8,128)} fusion(bf16[4352,256]{1,0:T(8,128)(2,1)S(1)} %bitcast.69, bf16[256,4,128]{2,1,0:T(4,128)(2,1)S(1)} %reshape.333), kind=kOutput, calls=%fused_computation.28 | convolution fusion | flops 1140850688 | bytes 19202048 | tf_op jit(solution)/shard_map/qhd,kd->hqk/dot_general | solution.py:130
  215.3 0.2 fusion.9
  215.5 0.7 reduce.5
  216.1 0.7 reshape.354
  216.9 6.2 %all-to-all-start.3 = ((bf16[32,2,1024]{2,1,0:T(2,128)(2,1)}), bf16[32,2,1024]{2,1,0:T(2,128)(2,1)S(1)}, u32[]{:S(2)}, u32[]{:S(2)}) async-start(bf16[32,2,1024]{2,1,0:T(2,128)(2,1)} %reshape.354), calls=%async_computation.3 | async-start | bytes 262144 | tf_op jit(solution)/shard_map/all_to_all | solution.py:166
  223.1 18.6 %fusion.48 = (f32[4,256]{1,0:T(4,128)S(1)}, bf16[4,256,4352]{1,2,0:T(8,128)(2,1)}) fusion(f32[4352,256,4]{1,0,2:T(8,128)} %fusion.22, pred[256,4352]{0,1:T(8,128)(4,1)} %compare_and_fusion), kind=kOutput, calls=%fused_computation.104 | output fusion | flops 35655936 | bytes 27856896 | tf_op jit(solution)/shard_map/sub | solution.py:135
  241.8 5.0 %fusion.18 = bf16[256,4,128]{0,2,1:T(8,128)(2,1)S(1)} fusion(bf16[4,256,4352]{1,2,0:T(8,128)(2,1)} %get-tuple-element.25, bf16[4352,256]{1,0:T(8,128)(2,1)S(1)} %bitcast.71, f32[256,4]{0,1:T(4,128)S(1)} %bitcast.81), kind=kOutput, calls=%fused_computation.24 | convolution fusion | flops 1141112832 | bytes 10293248 | tf_op jit(solution)/shard_map/hqk,kd->hqd/dot_general | solution.py:137
  246.8 0.8 copy.58
  247.7 0.2 fusion.21
  247.9 0.6 copy.65
  (48 shorter events, 1.5 us)
Async XLA Ops:
  7.2 1.0 copy-start
  7.2 94.7 %all-gather.2.cloned.1.call-start = ((), (), s32[]{:S(2)}) async-start(), calls=%async_computation.4 | async-start | bytes 5474304 | tf_op jit(solution)/shard_map/all_gather | solution.py:64
  9.9 31.6 %copy-start.4 = (s32[8]{0:T(128)S(1)}, s32[8]{0:T(128)}, u32[]{:S(2)}) copy-start(s32[8]{0:T(128)} %param.11) | copy-start | bytes 100
  10.0 31.8 %copy-start.3 = (s32[544]{0:T(1024)S(1)}, s32[544]{0:T(1024)}, u32[]{:S(2)}) copy-start(s32[544]{0:T(1024)} %constant.149) | copy-start | bytes 6532
  36.7 30.5 %all-to-all-start.1 = ((bf16[8,4,32,8,128]{4,3,2,1,0:T(8,128)(2,1)}), bf16[8,4,32,8,128]{4,3,2,1,0:T(8,128)(2,1)S(1)}, u32[]{:S(2)}, u32[]{:S(2)}) async-start(bf16[8,4,32,8,128]{4,3,2,1,0:T(8,128)(2,1)} %broadcast_in_dim.71), calls=%async_computation.1 | async-start | bytes 4194304 | tf_op jit(solution)/shard_map/all_to_all | solution.py:72
  109.1 1.3 collective-permute-start
  120.8 14.9 %copy-start.2 = (s32[512]{0:T(512)S(1)}, s32[512]{0:T(512)}, u32[]{:S(2)}) copy-start(s32[512]{0:T(512)} %param.12) | copy-start | bytes 6148
  125.7 69.2 %all-to-all-start.2 = ((bf16[32,2,19456]{2,1,0:T(2,128)(2,1)}), bf16[32,2,19456]{2,1,0:T(2,128)(2,1)S(1)}, u32[]{:S(2)}, u32[]{:S(2)}) async-start(bf16[32,2,19456]{2,1,0:T(2,128)(2,1)} %reshape.352), calls=%async_computation.2 | async-start | bytes 4980736 | tf_op jit(solution)/shard_map/all_to_all | solution.py:106
  216.9 30.7 %all-to-all-start.3 = ((bf16[32,2,1024]{2,1,0:T(2,128)(2,1)}), bf16[32,2,1024]{2,1,0:T(2,128)(2,1)S(1)}, u32[]{:S(2)}, u32[]{:S(2)}) async-start(bf16[32,2,1024]{2,1,0:T(2,128)(2,1)} %reshape.354), calls=%async_computation.3 | async-start | bytes 262144 | tf_op jit(solution)/shard_map/all_to_all | solution.py:166
  241.8 6.8 %copy-start.1 = (bf16[1024,128]{1,0:T(8,128)(2,1)S(1)}, bf16[1024,128]{1,0:T(8,128)(2,1)}, u32[]{:S(2)}) copy-start(bf16[1024,128]{1,0:T(8,128)(2,1)} %param.10) | copy-start | bytes 786436
Sparse Core Ops, SparseCore 0:
  11.0 90.7 all-gather.1

commit v3 on v2

--- a/solution.py
+++ b/solution.py
@@ -90,38 +90,34 @@
     rotated = rotate(half_raw[:, None, :], my_places)[:, 0, :]
     mine = jnp.where(is_key, rotated, half_raw).astype(jnp.bfloat16)
 
-    other = lax.ppermute(mine, "gx", [(p, p ^ 1) for p in range(count_gx)])
-    both = jnp.concatenate(
-        [jnp.where(is_key, mine, other), jnp.where(is_key, other, mine)], axis=1
-    ).reshape(count_gy, sub, 2 * HD)
     window_blocks = min(count_gy, MOST // block_tokens + 1)
     window = window_blocks * block_tokens
     first_blocks = [min(max(b - (window_blocks - 1), 0), count_gy - window_blocks) for b in range(count_gy)]
     chosen = jnp.asarray(
         [[f + w for w in range(window_blocks)] for f in first_blocks], dtype=jnp.int32
     )
-    kv_parcel = jnp.take(both, chosen, axis=0).reshape(count_gy, window_blocks * sub * 2 * HD)
+    strided = mine.reshape(count_gy, sub, HD)
+    kv_parcel = jnp.take(strided, chosen, axis=0).reshape(count_gy, window_blocks * sub * HD)
     q_parcel = queries.reshape(count_gy, sub * query_cols)
     parcel = jnp.concatenate([q_parcel, kv_parcel], axis=1)
     arrived = lax.all_to_all(parcel, "gy", 0, 0, tiled=True)
     queries = arrived[:, : sub * query_cols].reshape(block_tokens, heads_here, HD)
-    kv_rows_all = (
-        arrived[:, sub * query_cols :]
-        .reshape(count_gy, window_blocks, sub, 2 * HD)
-        .transpose(1, 0, 2, 3)
-        .reshape(window, 2 * HD)
-    )
-    key_rows = kv_rows_all[:, :HD]
-    value_rows = kv_rows_all[:, HD:]
+    mine_window = arrived[:, sub * query_cols :].reshape(count_gy, window_blocks, sub, HD)
+    other_window = lax.ppermute(mine_window, "gx", [(p, p ^ 1) for p in range(count_gx)])
+    key_rows = jnp.where(is_key, mine_window, other_window).reshape(window, HD)
+    value_rows = jnp.where(is_key, other_window, mine_window).reshape(window, HD)
 
-    every_index = jnp.arange(all_tokens, dtype=jnp.int32)
-    segment_all, unused_places = token_places(prompt_lengths, every_index)
     first_query = where_gy * block_tokens
     token_index = first_query + order
-    segment_own = lax.dynamic_slice_in_dim(segment_all, first_query, block_tokens, 0)
-    window_start = jnp.clip(where_gy - (window_blocks - 1), 0, count_gy - window_blocks) * block_tokens
-    key_segment = lax.dynamic_slice_in_dim(segment_all, window_start, window, 0)
-    key_index = window_start + jnp.arange(window, dtype=jnp.int32)
+    segment_own, unused_places = token_places(prompt_lengths, token_index)
+    window_first = jnp.clip(where_gy - (window_blocks - 1), 0, count_gy - window_blocks)
+    source_range = jnp.arange(count_gy, dtype=jnp.int32)[:, None, None]
+    block_range = jnp.arange(window_blocks, dtype=jnp.int32)[None, :, None]
+    sub_range = jnp.arange(sub, dtype=jnp.int32)[None, None, :]
+    key_index = (
+        (window_first + block_range) * block_tokens + source_range * sub + sub_range
+    ).reshape(window)
+    key_segment, unused_places = token_places(prompt_lengths, key_index)
     allowed = (key_segment[None, :] == segment_own[:, None]) & (
         key_index[None, :] <= token_index[:, None]
     )
@@ -144,8 +140,9 @@
         .reshape(block_tokens, query_cols)
     )
 
-    own_block = lax.dynamic_slice_in_dim(kv_rows_all, first_query - window_start, block_tokens, 0)
-    cache_cols = jnp.where(is_key, own_block[:, :HD], own_block[:, HD:])
+    cache_cols = lax.dynamic_index_in_dim(
+        mine_window, where_gy - window_first, 1, keepdims=False
+    ).reshape(block_tokens, HD)
     pages_dev = PAGES_DEV
     page_len = block_tokens // pages_dev
     page_range = jnp.arange(pages_dev, dtype=jnp.int32)

time: 257 us -> 228 us (0.89)
  waiting for transfers between devices: 110 us -> 91.3 us
  local copies, waits for them, and re-layouts: 29.1 us -> 23.2 us
    all_to_all x1, waiting for transfers between devices: 54 us -> 25.2 us  [local(): arrived = lax.all_to_all(parcel, 'gy', 0, 0, tiled=True)]
    all_to_all x1, waiting for transfers between devices: 0.01 us -> 9.57 us  [local(): lax.all_to_all(outgoing, 'gy', split_axis=0, concat_axis=0, tiled=True)]
    unnamed x18 -> x23, local copies, waits for them, and re-layouts: 19.2 us -> 14.6 us
    all_to_all x2, other arithmetic: 5.05 us -> 1.8 us  [local(): arrived = lax.all_to_all(parcel, 'gy', 0, 0, tiled=True)]
  transfers between devices with their start and end apart: 5 -> 5, of which waited for: 3 -> 4; matrix products, arithmetic and copies ran while one was open for 15% -> 7% of each run, Pallas kernels for 0% -> 0%
where the time goes in v3:
time: 228 us; the launch traced here: 227 us
  waiting for transfers between devices  91.3 us (40%)
  other arithmetic  35 us (15%)
  blocking collectives  23.8 us (10%)
  local copies, waits for them, and re-layouts  23.2 us (10%)
  starting transfers between devices  20.1 us (9%)
  matrix products  19.5 us (9%)
  between operations  14.4 us (6%)
    all_gather x1, waiting for transfers between devices, local(): gathered = lax.all_gather(stacked, 'gy', axis=1, tiled=True)  31.7 us
    all_to_all x1, waiting for transfers between devices, local(): arrived = lax.all_to_all(parcel, 'gy', 0, 0, tiled=True)  25.2 us
    all_to_all x1, waiting for transfers between devices, local(): rows_here = lax.all_to_all(spread, 'gx', 0, 0, tiled=True)  24.8 us
    all_to_all x1, blocking collectives, local(): pieces = lax.all_to_all(pieces, 'gy', 1, 1, tiled=True)  23.8 us
    sub x1, other arithmetic, local(): weights = jnp.where(allowed[None], jnp.exp(scores - row_max), 0.0)  18.1 us
    unnamed x23, local copies, waits for them, and re-layouts  14.6 us
    all_to_all x1, starting transfers between devices, local(): arrived = lax.all_to_all(parcel, 'gy', 0, 0, tiled=True)  9.68 us
    all_to_all x1, waiting for transfers between devices, local(): lax.all_to_all(outgoing, 'gy', split_axis=0, concat_axis=0, tiled=True)  9.57 us
  transfers between devices with their start and end apart: 5, of which 4 were waited for; matrix products, arithmetic and copies ran while one was open for 7% of the time, Pallas kernels for 0%

profile of v3, /device:TPU:2, one launch (start us, length us, event | category | flops | bytes accessed | tf_op | source)
XLA Modules:
  0.0 227.4 jit_solution(1769382629200644866)
XLA Ops:
  7.3 0.8 copy-done
  8.1 1.7 maximum_maximum_fusion
  9.9 1.0 copy.42
  10.9 23.8 %all_to_all.34 = bf16[4,32,8,128]{3,2,0,1:T(8,128)(2,1)S(1)} all-to-all(bf16[4,32,8,128]{3,2,0,1:T(8,128)(2,1)S(1)} %copy.42), channel_id=1, replica_groups=mesh['gx'=8,'gy'=32] {'gy'}, dimensions={1} | all-to-all | bytes 524288 | tf_op jit(solution)/shard_map/all_to_all | solution.py:70
  34.8 1.8 broadcast_in_dim.67
  36.6 4.7 %all-to-all-start.1 = ((bf16[8,4,32,8,128]{4,3,2,1,0:T(8,128)(2,1)}), bf16[8,4,32,8,128]{4,3,2,1,0:T(8,128)(2,1)S(1)}, u32[]{:S(2)}, u32[]{:S(2)}) async-start(bf16[8,4,32,8,128]{4,3,2,1,0:T(8,128)(2,1)} %broadcast_in_dim.67), calls=%async_computation.1 | async-start | bytes 4194304 | tf_op jit(solution)/shard_map/all_to_all | solution.py:72
  41.4 0.2 reduce-window.8
  41.8 0.5 multiply_cosine_fusion.1
  42.3 24.8 %all-to-all-done.1 = bf16[8,4,32,8,128]{4,3,2,1,0:T(8,128)(2,1)S(1)} async-done(((bf16[8,4,32,8,128]{4,3,2,1,0:T(8,128)(2,1)}), bf16[8,4,32,8,128]{4,3,2,1,0:T(8,128)(2,1)S(1)}, u32[]{:S(2)}, u32[]{:S(2)}) %all-to-all-start.1) | async-done | bytes 2097184 | tf_op jit(solution)/shard_map/all_to_all | solution.py:72
  67.1 0.5 multiply_reduce_fusion
  67.7 2.5 %convert_element_type.78 = f32[8,4,32,8,128]{4,3,2,1,0:T(8,128)} convert(bf16[8,4,32,8,128]{4,3,2,1,0:T(8,128)(2,1)S(1)} %all-to-all-done.1) | non-fusion elementwise | flops 1048576 | bytes 6291456 | tf_op jit(solution)/shard_map/convert_element_type | solution.py:74
  70.2 31.7 %all-gather.2.cloned.1.call-done = bf16[648,4096]{1,0:T(8,128)(2,1)} async-done(((bf16[648,128]{1,0:T(8,128)(2,1)}), bf16[648,4096]{1,0:T(8,128)(2,1)}) %all-gather.2.cloned.1.call-update) | async-done | bytes 5308432 | tf_op jit(solution)/shard_map/all_gather | solution.py:64
  101.9 0.8 slice_convert_fusion
  102.8 5.6 %fusion.7 = f32[256,640]{1,0:T(8,128)S(1)} fusion(bf16[648,4096]{1,0:T(8,128)(2,1)} %all-gather.2.cloned.1.call-done, f32[256,4096]{1,0:T(8,128)} %bitcast.75, f32[4096]{0:T(1024)S(1)} %bitcast.80, f32[256]{0:T(256)S(1)} %rsqrt.11), kind=kOutput, calls=%fused_computation.10 | convolution fusion | flops 1345323008 | bytes 10109952 | tf_op jit(solution)/shard_map/dot_general | solution.py:81
  108.5 0.6 fusion.28
  109.1 0.2 reshape.397
  109.2 0.5 subtract_convert_fusion
  109.7 0.4 pad_maximum_fusion
  110.1 0.2 convert_element_type.70
  110.4 2.5 %gather_fusion = bf16[544,8,128]{2,1,0:T(8,128)(2,1)S(1)} fusion(bf16[32,8,128]{2,1,0:T(8,128)(2,1)S(1)} %fusion.34, s32[1024]{0:T(1024)S(1)} %pad_clamp_fusion), kind=kCustom, calls=%fused_computation | custom fusion | bytes 2230400 | tf_op jit(solution)/shard_map/jit(_take)/gather | solution.py:100
  112.9 0.5 select_n.119
  113.5 0.5 broadcast.374
  114.0 1.7 reduce.4
  115.7 1.9 reshape.420
  117.6 9.7 %all-to-all-start.2 = ((bf16[32,2,10752]{2,1,0:T(2,128)(2,1)}), bf16[32,2,10752]{2,1,0:T(2,128)(2,1)}, u32[]{:S(2)}, u32[]{:S(2)}) async-start(bf16[32,2,10752]{2,1,0:T(2,128)(2,1)} %reshape.420), calls=%async_computation.2 | async-start | bytes 2752512 | tf_op jit(solution)/shard_map/all_to_all | solution.py:103
  127.4 0.2 iota_add_fusion
  127.8 4.4 %compare_and_fusion = pred[256,4352]{0,1:T(8,128)(4,1)} fusion(s32[256]{0:T(256)S(1)} %get-tuple-element.29, s32[256]{0:T(256)S(1)} %get-tuple-element.16, s32[4352]{0:T(1024)S(1)} %add.184, s32[4352]{0:T(1024)S(1)} %convert_reduce_fusion), kind=kLoop, calls=%fused_computation.12 | loop fusion | flops 3342336 | bytes 1150976 | tf_op jit(solution)/shard_map/and | solution.py:121
  132.2 25.2 %all-to-all-done.2 = bf16[32,2,10752]{2,1,0:T(2,128)(2,1)} async-done(((bf16[32,2,10752]{2,1,0:T(2,128)(2,1)}), bf16[32,2,10752]{2,1,0:T(2,128)(2,1)}, u32[]{:S(2)}, u32[]{:S(2)}) %all-to-all-start.2) | async-done | bytes 1376288 | tf_op jit(solution)/shard_map/all_to_all | solution.py:103
  157.4 7.8 %reshape.421 = bf16[32,1,21504]{2,1,0:T(2,128)(2,1)S(1)} reshape(bf16[32,2,10752]{2,1,0:T(2,128)(2,1)} %all-to-all-done.2) | data formatting | bytes 2752512
  165.3 0.4 copy.68
  165.7 1.1 copy-done.1
  167.0 0.3 collective-permute-start
  167.8 0.2 add_reduce_fusion
  168.1 0.2 fusion.9
  168.2 0.7 reduce.5
  168.9 0.7 reshape.422
  169.6 5.4 %all-to-all-start.3 = ((bf16[32,2,1024]{2,1,0:T(2,128)(2,1)}), bf16[32,2,1024]{2,1,0:T(2,128)(2,1)S(1)}, u32[]{:S(2)}, u32[]{:S(2)}) async-start(bf16[32,2,1024]{2,1,0:T(2,128)(2,1)} %reshape.422), calls=%async_computation.3 | async-start | bytes 262144 | tf_op jit(solution)/shard_map/all_to_all | solution.py:163
  175.0 0.2 fusion.35
  175.2 1.0 slice.51
  176.2 0.2 reshape.401
  176.4 9.6 %all-to-all-done.3 = bf16[32,2,1024]{2,1,0:T(2,128)(2,1)S(1)} async-done(((bf16[32,2,1024]{2,1,0:T(2,128)(2,1)}), bf16[32,2,1024]{2,1,0:T(2,128)(2,1)S(1)}, u32[]{:S(2)}, u32[]{:S(2)}) %all-to-all-start.3) | async-done | bytes 131104 | tf_op jit(solution)/shard_map/all_to_all | solution.py:163
  186.0 0.2 fusion.21
  186.2 0.6 copy.60
  186.9 1.2 broadcast_select_fusion.1
  188.1 8.6 %fusion.22 = f32[4352,256,4]{1,0,2:T(8,128)} fusion(bf16[4352,128,1]{1,0,2:T(8,128)(2,1)S(1)} %bitcast.74, bf16[256,4,128]{2,1,0:T(4,128)(2,1)S(1)} %reshape.401), kind=kOutput, calls=%fused_computation.33 | convolution fusion | flops 1140850688 | bytes 19202048 | tf_op jit(solution)/shard_map/qhd,kd->hqk/dot_general | solution.py:126
  196.7 18.1 %fusion.49 = (f32[4,256]{1,0:T(4,128)S(1)}, bf16[4,256,4352]{1,2,0:T(8,128)(2,1)}) fusion(f32[4352,256,4]{1,0,2:T(8,128)} %fusion.22, pred[256,4352]{0,1:T(8,128)(4,1)S(1)} %copy-done.2), kind=kOutput, calls=%fused_computation.106 | output fusion | flops 35655936 | bytes 27856896 | tf_op jit(solution)/shard_map/sub | solution.py:131
  214.8 5.0 %fusion.18 = bf16[256,4,128]{0,2,1:T(8,128)(2,1)S(1)} fusion(bf16[4352,128,1]{1,0,2:T(8,128)(2,1)S(1)} %bitcast.76, bf16[4,256,4352]{1,2,0:T(8,128)(2,1)} %get-tuple-element.27, f32[256,4]{0,1:T(4,128)S(1)} %bitcast.85), kind=kOutput, calls=%fused_computation.24 | convolution fusion | flops 1141112832 | bytes 10293248 | tf_op jit(solution)/shard_map/hqk,kd->hqd/dot_general | solution.py:133
  219.7 0.8 copy.53
  (51 shorter events, 2.0 us)
Async XLA Ops:
  7.2 1.0 copy-start
  7.2 94.8 %all-gather.2.cloned.1.call-start = ((), (), s32[]{:S(2)}) async-start(), calls=%async_computation.4 | async-start | bytes 5474304 | tf_op jit(solution)/shard_map/all_gather | solution.py:64
  34.8 6.6 %copy-start.6 = (s32[8]{0:T(128)S(1)}, s32[8]{0:T(128)}, u32[]{:S(2)}) copy-start(s32[8]{0:T(128)} %param.11) | copy-start | bytes 100
  34.8 6.8 %copy-start.5 = (s32[544]{0:T(1024)S(1)}, s32[544]{0:T(1024)}, u32[]{:S(2)}) copy-start(s32[544]{0:T(1024)} %constant.153) | copy-start | bytes 6532
  36.6 30.5 %all-to-all-start.1 = ((bf16[8,4,32,8,128]{4,3,2,1,0:T(8,128)(2,1)}), bf16[8,4,32,8,128]{4,3,2,1,0:T(8,128)(2,1)S(1)}, u32[]{:S(2)}, u32[]{:S(2)}) async-start(bf16[8,4,32,8,128]{4,3,2,1,0:T(8,128)(2,1)} %broadcast_in_dim.67), calls=%async_computation.1 | async-start | bytes 4194304 | tf_op jit(solution)/shard_map/all_to_all | solution.py:72
  117.6 39.8 %all-to-all-start.2 = ((bf16[32,2,10752]{2,1,0:T(2,128)(2,1)}), bf16[32,2,10752]{2,1,0:T(2,128)(2,1)}, u32[]{:S(2)}, u32[]{:S(2)}) async-start(bf16[32,2,10752]{2,1,0:T(2,128)(2,1)} %reshape.420), calls=%async_computation.2 | async-start | bytes 2752512 | tf_op jit(solution)/shard_map/all_to_all | solution.py:103
  165.7 1.1 copy-start.1
  165.7 1.6 copy-start.4
  167.0 19.9 %collective-permute-start = (bf16[32,17,8,128]{3,2,1,0:T(8,128)(2,1)S(1)}, bf16[32,17,8,128]{3,2,1,0:T(8,128)(2,1)S(1)}, u32[]{:S(2)}, u32[]{:S(2)}) collective-permute-start(bf16[32,17,8,128]{3,2,1,0:T(8,128)(2,1)S(1)} %bitcast.71), channel_id=1, source_target_pairs={{0,32},{32,0},{64,96},{96,64},{128,160},{160,128},{192,224},{224,1... | collective-permute-start | bytes 3342344 | tf_op jit(solution)/shard_map/ppermute | solution.py:106
  169.6 16.3 %all-to-all-start.3 = ((bf16[32,2,1024]{2,1,0:T(2,128)(2,1)}), bf16[32,2,1024]{2,1,0:T(2,128)(2,1)S(1)}, u32[]{:S(2)}, u32[]{:S(2)}) async-start(bf16[32,2,1024]{2,1,0:T(2,128)(2,1)} %reshape.422), calls=%async_computation.3 | async-start | bytes 262144 | tf_op jit(solution)/shard_map/all_to_all | solution.py:163
  188.1 8.6 %copy-start.2 = (pred[256,4352]{0,1:T(8,128)(4,1)S(1)}, pred[256,4352]{0,1:T(8,128)(4,1)}, u32[]{:S(2)}) copy-start(pred[256,4352]{0,1:T(8,128)(4,1)} %compare_and_fusion) | copy-start | bytes 3342340
  196.7 18.1 %copy-start.3 = (bf16[32,17,8,128]{3,2,1,0:T(8,128)(2,1)S(1)}, bf16[32,17,8,128]{3,2,1,0:T(8,128)(2,1)}, u32[]{:S(2)}) copy-start(bf16[32,17,8,128]{3,2,1,0:T(8,128)(2,1)} %get-tuple-element.19) | copy-start | bytes 3342340
Sparse Core Ops, SparseCore 0:
  11.0 90.8 all-gather.1

commit v4 on v3

--- a/solution.py
+++ b/solution.py
@@ -1,8 +1,10 @@
+import functools
 import math
 
 import jax
 import jax.numpy as jnp
 from jax import lax
+from jax.experimental import pallas as pl
 from jax.sharding import PartitionSpec as P
 
 D = 4096
@@ -39,6 +41,47 @@
         [leading * cos_part - trailing * sin_part, trailing * cos_part + leading * sin_part],
         axis=-1,
     )
+
+
+def attention_body(scale, q_ref, k_ref, v_ref, qseg_ref, qidx_ref, kseg_ref, kidx_ref, o_ref):
+    scores = lax.dot_general(
+        q_ref[...], k_ref[...], (((1,), (1,)), ((), ())), preferred_element_type=jnp.float32
+    ) * scale
+    allowed = (kseg_ref[...] == qseg_ref[...]) & (kidx_ref[...] <= qidx_ref[...])
+    scores = jnp.where(allowed, scores, masked_out)
+    row_max = jnp.max(scores, axis=1, keepdims=True)
+    weights = jnp.where(allowed, jnp.exp(scores - row_max), 0.0)
+    totals = jnp.sum(weights, axis=1, keepdims=True)
+    mixed = jnp.dot(weights.astype(jnp.bfloat16), v_ref[...], preferred_element_type=jnp.float32)
+    o_ref[...] = (mixed / totals).astype(o_ref.dtype)
+
+
+def segment_attention(queries, key_rows, value_rows, q_segment, q_index, k_segment, k_index, head_size, row_chunk=64):
+    tokens, cols = queries.shape
+    heads = cols // head_size
+    window = key_rows.shape[0]
+    chunks = tokens // row_chunk
+    flops = 4 * tokens * window * head_size * heads
+    return pl.pallas_call(
+        functools.partial(attention_body, 1.0 / math.sqrt(head_size)),
+        grid=(heads, chunks),
+        in_specs=[
+            pl.BlockSpec((row_chunk, head_size), lambda h, r: (r, h)),
+            pl.BlockSpec((window, head_size), lambda h, r: (0, 0)),
+            pl.BlockSpec((window, head_size), lambda h, r: (0, 0)),
+            pl.BlockSpec((row_chunk, 1), lambda h, r: (r, 0)),
+            pl.BlockSpec((row_chunk, 1), lambda h, r: (r, 0)),
+            pl.BlockSpec((1, window), lambda h, r: (0, 0)),
+            pl.BlockSpec((1, window), lambda h, r: (0, 0)),
+        ],
+        out_specs=pl.BlockSpec((row_chunk, head_size), lambda h, r: (r, h)),
+        out_shape=jax.ShapeDtypeStruct((tokens, cols), jnp.bfloat16),
+        cost_estimate=pl.CostEstimate(
+            flops=flops, transcendentals=tokens * window * heads,
+            bytes_accessed=2 * (2 * tokens * cols + 2 * window * head_size) + 8 * (tokens + window),
+        ),
+    )(queries, key_rows, value_rows, q_segment.reshape(tokens, 1), q_index.reshape(tokens, 1),
+      k_segment.reshape(1, window), k_index.reshape(1, window))
 
 
 def local(hidden_in, norm_gain, query_proj, kv_proj, prompt_lengths, cache_slot):
@@ -118,26 +161,9 @@
         (window_first + block_range) * block_tokens + source_range * sub + sub_range
     ).reshape(window)
     key_segment, unused_places = token_places(prompt_lengths, key_index)
-    allowed = (key_segment[None, :] == segment_own[:, None]) & (
-        key_index[None, :] <= token_index[:, None]
-    )
-    score_scale = 1.0 / math.sqrt(HD)
-    scores = (
-        jnp.einsum("qhd,kd->hqk", queries, key_rows, preferred_element_type=jnp.float32)
-        * score_scale
-    )
-    scores = jnp.where(allowed[None], scores, masked_out)
-    row_max = jnp.max(scores, axis=2, keepdims=True)
-    weights = jnp.where(allowed[None], jnp.exp(scores - row_max), 0.0)
-    totals = jnp.sum(weights, axis=2)
-    mixed = jnp.einsum(
-        "hqk,kd->hqd", weights.astype(jnp.bfloat16), value_rows, preferred_element_type=jnp.float32
-    )
-    attention = (
-        (mixed / totals[..., None])
-        .astype(jnp.bfloat16)
-        .transpose(1, 0, 2)
-        .reshape(block_tokens, query_cols)
+    attention = segment_attention(
+        queries.reshape(block_tokens, query_cols), key_rows, value_rows,
+        segment_own, token_index, key_segment, key_index, HD,
     )
 
     cache_cols = lax.dynamic_index_in_dim(

time: 228 us -> 218 us (0.956)
  Pallas kernels: 0 us -> 21.6 us
  other arithmetic: 35 us -> 13.6 us
  matrix products: 19.5 us -> 5.98 us
    pallas_call x0 -> x1, Pallas kernels: none -> 21.6 us  [segment_attention(): pl.pallas_call(functools.partial(attention_body, 1.0 / math.sqrt(head_siz...]
    sub x1 -> x0, other arithmetic: 18.1 us -> none  [local(): weights = jnp.where(allowed[None], jnp.exp(scores - row_max), 0.0)]
    dot_general x2 -> x0, matrix products: 13.6 us -> none  [the longest x1 8.61 us: local(): jnp.einsum('qhd,kd->hqk', queries, key_rows, preferred_element_type=jnp.f...]
    and x1 -> x0, other arithmetic: 4.36 us -> none  [local(): (key_segment[None, :] == segment_own[:, None]) & (key_index[None, :] <= t...]
    all_to_all x1, waiting for transfers between devices: 25.2 us -> 29.5 us  [local(): arrived = lax.all_to_all(parcel, 'gy', 0, 0, tiled=True)]
    all_to_all x1, waiting for transfers between devices: 9.57 us -> 6.77 us  [local(): lax.all_to_all(outgoing, 'gy', split_axis=0, concat_axis=0, tiled=True)]
    unnamed x23 -> x18, local copies, waits for them, and re-layouts: 14.6 us -> 13.6 us
where the time goes in v4:
time: 218 us; the launch traced here: 217 us
  waiting for transfers between devices  92.4 us (42%)
  local copies, waits for them, and re-layouts  25.1 us (12%)
  blocking collectives  23.8 us (11%)
  Pallas kernels  21.6 us (10%)
  starting transfers between devices  20.2 us (9%)
  between operations  14.3 us (7%)
  other arithmetic  13.6 us (6%)
  matrix products  5.98 us (3%)
    all_gather x1, waiting for transfers between devices, local(): gathered = lax.all_gather(stacked, 'gy', axis=1, tiled=True)  31.3 us
    all_to_all x1, waiting for transfers between devices, local(): arrived = lax.all_to_all(parcel, 'gy', 0, 0, tiled=True)  29.5 us
    all_to_all x1, waiting for transfers between devices, local(): rows_here = lax.all_to_all(spread, 'gx', 0, 0, tiled=True)  24.8 us
    all_to_all x1, blocking collectives, local(): pieces = lax.all_to_all(pieces, 'gy', 1, 1, tiled=True)  23.8 us
    pallas_call x1, Pallas kernels, segment_attention(): pl.pallas_call(functools.partial(attention_body, 1.0 / math.sqrt(head_siz...  21.6 us
    unnamed x18, local copies, waits for them, and re-layouts  13.6 us
    all_to_all x1, starting transfers between devices, local(): arrived = lax.all_to_all(parcel, 'gy', 0, 0, tiled=True)  9.81 us
    all_to_all x1, waiting for transfers between devices, local(): lax.all_to_all(outgoing, 'gy', split_axis=0, concat_axis=0, tiled=True)  6.77 us
  transfers between devices with their start and end apart: 5, of which 4 were waited for; matrix products, arithmetic and copies ran while one was open for 7% of the time, Pallas kernels for 0%

profile of v4, /device:TPU:2, one launch (start us, length us, event | category | flops | bytes accessed | tf_op | source)
XLA Modules:
  0.0 216.9 jit_solution(10004821409573456801)
XLA Ops:
  7.2 0.9 copy-done
  8.2 1.7 maximum_maximum_fusion
  10.0 1.0 copy.27
  11.0 23.8 %all_to_all.34 = bf16[4,32,8,128]{3,2,0,1:T(8,128)(2,1)S(1)} all-to-all(bf16[4,32,8,128]{3,2,0,1:T(8,128)(2,1)S(1)} %copy.27), channel_id=1, replica_groups=mesh['gx'=8,'gy'=32] {'gy'}, dimensions={1} | all-to-all | bytes 524288 | tf_op jit(solution)/shard_map/all_to_all | solution.py:113
  34.8 1.8 broadcast_in_dim.48
  36.7 5.0 %all-to-all-start.1 = ((bf16[8,4,32,8,128]{4,3,2,1,0:T(8,128)(2,1)}), bf16[8,4,32,8,128]{4,3,2,1,0:T(8,128)(2,1)S(1)}, u32[]{:S(2)}, u32[]{:S(2)}) async-start(bf16[8,4,32,8,128]{4,3,2,1,0:T(8,128)(2,1)} %broadcast_in_dim.48), calls=%async_computation.1 | async-start | bytes 4194304 | tf_op jit(solution)/shard_map/all_to_all | solution.py:115
  41.6 0.2 reduce-window.8
  42.1 0.5 multiply_cosine_fusion.1
  42.6 24.8 %all-to-all-done.1 = bf16[8,4,32,8,128]{4,3,2,1,0:T(8,128)(2,1)S(1)} async-done(((bf16[8,4,32,8,128]{4,3,2,1,0:T(8,128)(2,1)}), bf16[8,4,32,8,128]{4,3,2,1,0:T(8,128)(2,1)S(1)}, u32[]{:S(2)}, u32[]{:S(2)}) %all-to-all-start.1) | async-done | bytes 2097184 | tf_op jit(solution)/shard_map/all_to_all | solution.py:115
  67.3 0.5 multiply_reduce_fusion
  68.0 2.5 %convert_element_type.69 = f32[8,4,32,8,128]{4,3,2,1,0:T(8,128)} convert(bf16[8,4,32,8,128]{4,3,2,1,0:T(8,128)(2,1)S(1)} %all-to-all-done.1) | non-fusion elementwise | flops 1048576 | bytes 6291456 | tf_op jit(solution)/shard_map/convert_element_type | solution.py:117
  70.5 31.3 %all-gather.2.cloned.1.call-done = bf16[648,4096]{1,0:T(8,128)(2,1)} async-done(((bf16[648,128]{1,0:T(8,128)(2,1)}), bf16[648,4096]{1,0:T(8,128)(2,1)}) %all-gather.2.cloned.1.call-update) | async-done | bytes 5308432 | tf_op jit(solution)/shard_map/all_gather | solution.py:107
  101.8 0.8 slice_convert_fusion
  102.7 5.6 %fusion = f32[256,640]{1,0:T(8,128)S(1)} fusion(bf16[648,4096]{1,0:T(8,128)(2,1)} %all-gather.2.cloned.1.call-done, f32[256,4096]{1,0:T(8,128)} %bitcast.49, f32[4096]{0:T(1024)S(1)} %bitcast.54, f32[256]{0:T(256)S(1)} %rsqrt.11), kind=kOutput, calls=%fused_computation.1 | convolution fusion | flops 1345323008 | bytes 10109952 | tf_op jit(solution)/shard_map/dot_general | solution.py:124
  108.4 0.6 fusion.10
  109.0 2.5 %gather_fusion = bf16[544,8,128]{2,1,0:T(8,128)(2,1)S(1)} fusion(bf16[32,8,128]{2,1,0:T(8,128)(2,1)S(1)} %fusion.16, s32[1024]{0:T(1024)S(1)} %pad_clamp_fusion), kind=kCustom, calls=%fused_computation | custom fusion | bytes 2230400 | tf_op jit(solution)/shard_map/jit(_take)/gather | solution.py:143
  111.5 0.5 select_n.111
  112.1 0.2 reshape.352
  112.3 0.5 subtract_convert_fusion
  112.7 0.4 pad_maximum_fusion
  113.1 0.2 convert_element_type.61
  113.4 0.5 broadcast.337
  113.9 1.7 reduce.4
  115.6 1.9 reshape.375
  117.5 9.8 %all-to-all-start.2 = ((bf16[32,2,10752]{2,1,0:T(2,128)(2,1)}), bf16[32,2,10752]{2,1,0:T(2,128)(2,1)}, u32[]{:S(2)}, u32[]{:S(2)}) async-start(bf16[32,2,10752]{2,1,0:T(2,128)(2,1)} %reshape.375), calls=%async_computation.2 | async-start | bytes 2752512 | tf_op jit(solution)/shard_map/all_to_all | solution.py:146
  127.4 0.2 iota_add_fusion
  127.9 29.5 %all-to-all-done.2 = bf16[32,2,10752]{2,1,0:T(2,128)(2,1)} async-done(((bf16[32,2,10752]{2,1,0:T(2,128)(2,1)}), bf16[32,2,10752]{2,1,0:T(2,128)(2,1)}, u32[]{:S(2)}, u32[]{:S(2)}) %all-to-all-start.2) | async-done | bytes 1376288 | tf_op jit(solution)/shard_map/all_to_all | solution.py:146
  157.4 7.8 %reshape.376 = bf16[32,1,21504]{2,1,0:T(2,128)(2,1)S(1)} reshape(bf16[32,2,10752]{2,1,0:T(2,128)(2,1)} %all-to-all-done.2) | data formatting | bytes 2752512
  165.3 0.4 copy.45
  165.8 0.1 copy.38
  166.0 0.8 copy-done.1
  167.1 0.2 add_reduce_fusion
  167.4 0.7 iota_add_fusion.1.qidx_ref
  168.1 0.2 fusion.2
  168.3 0.7 reduce.5
  169.0 0.7 reshape.377
  169.7 5.4 %all-to-all-start.3 = ((bf16[32,2,1024]{2,1,0:T(2,128)(2,1)}), bf16[32,2,1024]{2,1,0:T(2,128)(2,1)S(1)}, u32[]{:S(2)}, u32[]{:S(2)}) async-start(bf16[32,2,1024]{2,1,0:T(2,128)(2,1)} %reshape.377), calls=%async_computation.3 | async-start | bytes 262144 | tf_op jit(solution)/shard_map/all_to_all | solution.py:189
  175.1 0.2 fusion.17
  175.3 0.8 add.215.kidx_ref
  176.0 0.8 copy.30.qseg_ref
  176.8 0.6 reshape.360.kseg_ref
  177.4 1.0 slice.50
  178.4 0.8 reshape_reshape.7.q_ref
  179.2 6.8 %all-to-all-done.3 = bf16[32,2,1024]{2,1,0:T(2,128)(2,1)S(1)} async-done(((bf16[32,2,1024]{2,1,0:T(2,128)(2,1)}), bf16[32,2,1024]{2,1,0:T(2,128)(2,1)S(1)}, u32[]{:S(2)}, u32[]{:S(2)}) %all-to-all-start.3) | async-done | bytes 131104 | tf_op jit(solution)/shard_map/all_to_all | solution.py:189
  186.1 0.2 fusion.5
  186.3 0.6 copy.39
  187.0 1.5 broadcast_select_fusion
  188.5 21.6 %shard_map.86 = bf16[256,512]{1,0:T(8,128)(2,1)} custom-call(bf16[256,512]{1,0:T(8,128)(2,1)} %reshape_reshape.7.q_ref, bf16[4352,128]{1,0:T(8,128)(2,1)} %bitcast.51, bf16[4352,128]{1,0:T(8,128)(2,1)} %bitcast.50, s32[256,1]{1,0:T(8,128)} %copy.30.qseg_ref, s32[256,1]{1,0:T(8,128)} %iota_add_fusion.1.qidx_ref, s32[1,4352]{1,0:T(1,128)} %reshape.360.kseg_ref, ...), custom_call_target="tpu_custom_call" | custom-call | flops 2281701376 | bytes 2789376 | tf_op jit(solution)/shard_map/pallas_call | solution.py:65
  (47 shorter events, 1.8 us)
Async XLA Ops:
  7.2 1.0 copy-start
  7.2 94.6 %all-gather.2.cloned.1.call-start = ((), (), s32[]{:S(2)}) async-start(), calls=%async_computation.4 | async-start | bytes 5474304 | tf_op jit(solution)/shard_map/all_gather | solution.py:107
  36.7 5.0 %copy-start.4 = (s32[8]{0:T(128)S(1)}, s32[8]{0:T(128)}, u32[]{:S(2)}) copy-start(s32[8]{0:T(128)} %param.11) | copy-start | bytes 100
  36.7 5.2 %copy-start.3 = (s32[544]{0:T(1024)S(1)}, s32[544]{0:T(1024)}, u32[]{:S(2)}) copy-start(s32[544]{0:T(1024)} %constant.147) | copy-start | bytes 6532
  36.7 30.7 %all-to-all-start.1 = ((bf16[8,4,32,8,128]{4,3,2,1,0:T(8,128)(2,1)}), bf16[8,4,32,8,128]{4,3,2,1,0:T(8,128)(2,1)S(1)}, u32[]{:S(2)}, u32[]{:S(2)}) async-start(bf16[8,4,32,8,128]{4,3,2,1,0:T(8,128)(2,1)} %broadcast_in_dim.48), calls=%async_computation.1 | async-start | bytes 4194304 | tf_op jit(solution)/shard_map/all_to_all | solution.py:115
  117.5 10.3 %copy-start.2 = (s32[512]{0:T(512)S(1)}, s32[512]{0:T(512)}, u32[]{:S(2)}) copy-start(s32[512]{0:T(512)} %param.12) | copy-start | bytes 6148
  117.5 39.9 %all-to-all-start.2 = ((bf16[32,2,10752]{2,1,0:T(2,128)(2,1)}), bf16[32,2,10752]{2,1,0:T(2,128)(2,1)}, u32[]{:S(2)}, u32[]{:S(2)}) async-start(bf16[32,2,10752]{2,1,0:T(2,128)(2,1)} %reshape.375), calls=%async_computation.2 | async-start | bytes 2752512 | tf_op jit(solution)/shard_map/all_to_all | solution.py:146
  165.7 1.1 copy-start.1
  166.8 20.1 %collective-permute-start = (bf16[32,17,8,128]{3,2,1,0:T(8,128)(2,1)S(1)}, bf16[32,17,8,128]{3,2,1,0:T(8,128)(2,1)S(1)}, u32[]{:S(2)}, u32[]{:S(2)}) collective-permute-start(bf16[32,17,8,128]{3,2,1,0:T(8,128)(2,1)S(1)} %bitcast.46), channel_id=1, source_target_pairs={{0,32},{32,0},{64,96},{96,64},{128,160},{160,128},{192,224},{224,1... | collective-permute-start | bytes 3342344 | tf_op jit(solution)/shard_map/ppermute | solution.py:149
  169.7 16.3 %all-to-all-start.3 = ((bf16[32,2,1024]{2,1,0:T(2,128)(2,1)}), bf16[32,2,1024]{2,1,0:T(2,128)(2,1)S(1)}, u32[]{:S(2)}, u32[]{:S(2)}) async-start(bf16[32,2,1024]{2,1,0:T(2,128)(2,1)} %reshape.377), calls=%async_computation.3 | async-start | bytes 262144 | tf_op jit(solution)/shard_map/all_to_all | solution.py:189
Sparse Core Ops, SparseCore 0:
  11.0 90.7 all-gather.1

commit v5 on v4

--- a/solution.py
+++ b/solution.py
@@ -43,38 +43,40 @@
     )
 
 
-def attention_body(scale, q_ref, k_ref, v_ref, qseg_ref, qidx_ref, kseg_ref, kidx_ref, o_ref):
-    scores = lax.dot_general(
-        q_ref[...], k_ref[...], (((1,), (1,)), ((), ())), preferred_element_type=jnp.float32
-    ) * scale
+def attention_body(scale, heads, head_size, q_ref, k_ref, v_ref, qseg_ref, qidx_ref, kseg_ref, kidx_ref, o_ref):
     allowed = (kseg_ref[...] == qseg_ref[...]) & (kidx_ref[...] <= qidx_ref[...])
-    scores = jnp.where(allowed, scores, masked_out)
-    row_max = jnp.max(scores, axis=1, keepdims=True)
-    weights = jnp.where(allowed, jnp.exp(scores - row_max), 0.0)
-    totals = jnp.sum(weights, axis=1, keepdims=True)
-    mixed = jnp.dot(weights.astype(jnp.bfloat16), v_ref[...], preferred_element_type=jnp.float32)
-    o_ref[...] = (mixed / totals).astype(o_ref.dtype)
+    for h in range(heads):
+        columns = slice(h * head_size, (h + 1) * head_size)
+        scores = lax.dot_general(
+            q_ref[:, columns], k_ref[...], (((1,), (1,)), ((), ())),
+            preferred_element_type=jnp.float32,
+        ) * scale
+        scores = jnp.where(allowed, scores, masked_out)
+        row_max = jnp.max(scores, axis=1, keepdims=True)
+        weights = jnp.exp(scores - row_max)
+        totals = jnp.sum(weights, axis=1, keepdims=True)
+        mixed = jnp.dot(weights.astype(jnp.bfloat16), v_ref[...], preferred_element_type=jnp.float32)
+        o_ref[:, columns] = (mixed / totals).astype(o_ref.dtype)
 
 
 def segment_attention(queries, key_rows, value_rows, q_segment, q_index, k_segment, k_index, head_size, row_chunk=64):
     tokens, cols = queries.shape
     heads = cols // head_size
     window = key_rows.shape[0]
-    chunks = tokens // row_chunk
     flops = 4 * tokens * window * head_size * heads
     return pl.pallas_call(
-        functools.partial(attention_body, 1.0 / math.sqrt(head_size)),
-        grid=(heads, chunks),
+        functools.partial(attention_body, 1.0 / math.sqrt(head_size), heads, head_size),
+        grid=(tokens // row_chunk,),
         in_specs=[
-            pl.BlockSpec((row_chunk, head_size), lambda h, r: (r, h)),
-            pl.BlockSpec((window, head_size), lambda h, r: (0, 0)),
-            pl.BlockSpec((window, head_size), lambda h, r: (0, 0)),
-            pl.BlockSpec((row_chunk, 1), lambda h, r: (r, 0)),
-            pl.BlockSpec((row_chunk, 1), lambda h, r: (r, 0)),
-            pl.BlockSpec((1, window), lambda h, r: (0, 0)),
-            pl.BlockSpec((1, window), lambda h, r: (0, 0)),
+            pl.BlockSpec((row_chunk, cols), lambda r: (r, 0)),
+            pl.BlockSpec((window, head_size), lambda r: (0, 0)),
+            pl.BlockSpec((window, head_size), lambda r: (0, 0)),
+            pl.BlockSpec((row_chunk, 1), lambda r: (r, 0)),
+            pl.BlockSpec((row_chunk, 1), lambda r: (r, 0)),
+            pl.BlockSpec((1, window), lambda r: (0, 0)),
+            pl.BlockSpec((1, window), lambda r: (0, 0)),
         ],
-        out_specs=pl.BlockSpec((row_chunk, head_size), lambda h, r: (r, h)),
+        out_specs=pl.BlockSpec((row_chunk, cols), lambda r: (r, 0)),
         out_shape=jax.ShapeDtypeStruct((tokens, cols), jnp.bfloat16),
         cost_estimate=pl.CostEstimate(
             flops=flops, transcendentals=tokens * window * heads,
@@ -133,19 +135,20 @@
     rotated = rotate(half_raw[:, None, :], my_places)[:, 0, :]
     mine = jnp.where(is_key, rotated, half_raw).astype(jnp.bfloat16)
 
-    window_blocks = min(count_gy, MOST // block_tokens + 1)
+    needed_blocks = MOST // block_tokens + 1
+    window_blocks = min(count_gy, -(-needed_blocks * sub // 16) * 16 // sub)
     window = window_blocks * block_tokens
     first_blocks = [min(max(b - (window_blocks - 1), 0), count_gy - window_blocks) for b in range(count_gy)]
     chosen = jnp.asarray(
         [[f + w for w in range(window_blocks)] for f in first_blocks], dtype=jnp.int32
     )
     strided = mine.reshape(count_gy, sub, HD)
-    kv_parcel = jnp.take(strided, chosen, axis=0).reshape(count_gy, window_blocks * sub * HD)
-    q_parcel = queries.reshape(count_gy, sub * query_cols)
+    kv_parcel = jnp.take(strided, chosen, axis=0).reshape(count_gy, window_blocks * sub, HD)
+    q_parcel = queries.reshape(count_gy, sub * heads_here, HD)
     parcel = jnp.concatenate([q_parcel, kv_parcel], axis=1)
     arrived = lax.all_to_all(parcel, "gy", 0, 0, tiled=True)
-    queries = arrived[:, : sub * query_cols].reshape(block_tokens, heads_here, HD)
-    mine_window = arrived[:, sub * query_cols :].reshape(count_gy, window_blocks, sub, HD)
+    queries = arrived[:, : sub * heads_here].reshape(block_tokens, query_cols)
+    mine_window = arrived[:, sub * heads_here :]
     other_window = lax.ppermute(mine_window, "gx", [(p, p ^ 1) for p in range(count_gx)])
     key_rows = jnp.where(is_key, mine_window, other_window).reshape(window, HD)
     value_rows = jnp.where(is_key, other_window, mine_window).reshape(window, HD)
@@ -162,12 +165,12 @@
     ).reshape(window)
     key_segment, unused_places = token_places(prompt_lengths, key_index)
     attention = segment_attention(
-        queries.reshape(block_tokens, query_cols), key_rows, value_rows,
+        queries, key_rows, value_rows,
         segment_own, token_index, key_segment, key_index, HD,
     )
 
     cache_cols = lax.dynamic_index_in_dim(
-        mine_window, where_gy - window_first, 1, keepdims=False
+        mine_window.reshape(count_gy, window_blocks, sub, HD), where_gy - window_first, 1, keepdims=False
     ).reshape(block_tokens, HD)
     pages_dev = PAGES_DEV
     page_len = block_tokens // pages_dev

time: 218 us -> 197 us (0.904)
  local copies, waits for them, and re-layouts: 25.1 us -> 12.2 us
  Pallas kernels: 21.6 us -> 16.6 us
  waiting for transfers between devices: 92.4 us -> 88.6 us
    unnamed x18 -> x11, local copies, waits for them, and re-layouts: 13.6 us -> 2.37 us
    all_to_all x1, waiting for transfers between devices: 6.77 us -> 0.01 us  [local(): lax.all_to_all(outgoing, 'gy', split_axis=0, concat_axis=0, tiled=True)]
    pallas_call x1, Pallas kernels: 21.6 us -> 16.6 us  [segment_attention(): pl.pallas_call(functools.partial(attention_body, 1.0 / math.sqrt(head_siz...]
  transfers between devices with their start and end apart: 5 -> 5, of which waited for: 4 -> 4; matrix products, arithmetic and copies ran while one was open for 7% -> 6% of each run, Pallas kernels for 0% -> 8%
where the time goes in v5:
time: 197 us; the launch traced here: 196 us
  waiting for transfers between devices  88.6 us (45%)
  blocking collectives  23.8 us (12%)
  starting transfers between devices  20.3 us (10%)
  Pallas kernels  16.6 us (8%)
  between operations  14.3 us (7%)
  other arithmetic  14.2 us (7%)
  local copies, waits for them, and re-layouts  12.2 us (6%)
  matrix products  5.98 us (3%)
    all_to_all x1, waiting for transfers between devices, local(): arrived = lax.all_to_all(parcel, 'gy', 0, 0, tiled=True)  31.4 us
    all_gather x1, waiting for transfers between devices, local(): gathered = lax.all_gather(stacked, 'gy', axis=1, tiled=True)  31.3 us
    all_to_all x1, waiting for transfers between devices, local(): rows_here = lax.all_to_all(spread, 'gx', 0, 0, tiled=True)  24.8 us
    all_to_all x1, blocking collectives, local(): pieces = lax.all_to_all(pieces, 'gy', 1, 1, tiled=True)  23.8 us
    pallas_call x1, Pallas kernels, segment_attention(): pl.pallas_call(functools.partial(attention_body, 1.0 / math.sqrt(head_siz...  16.6 us
    all_to_all x1, starting transfers between devices, local(): arrived = lax.all_to_all(parcel, 'gy', 0, 0, tiled=True)  9.56 us
    dot_general x1, matrix products, local(): lax.dot_general(normed, weights_full, contract, preferred_element_type=jn...  5.61 us
    all_to_all x1, starting transfers between devices, local(): lax.all_to_all(outgoing, 'gy', split_axis=0, concat_axis=0, tiled=True)  5.61 us
  transfers between devices with their start and end apart: 5, of which 4 were waited for; matrix products, arithmetic and copies ran while one was open for 6% of the time, Pallas kernels for 8%

profile of v5, /device:TPU:2, one launch (start us, length us, event | category | flops | bytes accessed | tf_op | source)
XLA Modules:
  0.0 195.9 jit_solution(5406878574691123376)
XLA Ops:
  7.2 0.9 copy-done
  8.2 1.7 maximum_maximum_fusion
  10.0 1.0 copy.25
  11.0 23.8 %all_to_all.27 = bf16[4,32,8,128]{3,2,0,1:T(8,128)(2,1)S(1)} all-to-all(bf16[4,32,8,128]{3,2,0,1:T(8,128)(2,1)S(1)} %copy.25), channel_id=1, replica_groups=mesh['gx'=8,'gy'=32] {'gy'}, dimensions={1} | all-to-all | bytes 524288 | tf_op jit(solution)/shard_map/all_to_all | solution.py:115
  34.8 1.8 broadcast_in_dim.52
  36.7 5.0 %all-to-all-start.1 = ((bf16[8,4,32,8,128]{4,3,2,1,0:T(8,128)(2,1)}), bf16[8,4,32,8,128]{4,3,2,1,0:T(8,128)(2,1)S(1)}, u32[]{:S(2)}, u32[]{:S(2)}) async-start(bf16[8,4,32,8,128]{4,3,2,1,0:T(8,128)(2,1)} %broadcast_in_dim.52), calls=%async_computation.1 | async-start | bytes 4194304 | tf_op jit(solution)/shard_map/all_to_all | solution.py:117
  41.6 0.2 reduce-window.8
  41.9 0.1 convert_reduce_fusion.2
  42.0 0.1 select_reduce_fusion
  42.0 0.5 multiply_cosine_fusion.1
  42.6 24.8 %all-to-all-done.1 = bf16[8,4,32,8,128]{4,3,2,1,0:T(8,128)(2,1)S(1)} async-done(((bf16[8,4,32,8,128]{4,3,2,1,0:T(8,128)(2,1)}), bf16[8,4,32,8,128]{4,3,2,1,0:T(8,128)(2,1)S(1)}, u32[]{:S(2)}, u32[]{:S(2)}) %all-to-all-start.1) | async-done | bytes 2097184 | tf_op jit(solution)/shard_map/all_to_all | solution.py:117
  67.3 0.5 multiply_reduce_fusion
  67.9 0.1 rsqrt.11
  68.0 2.5 %convert_element_type.65 = f32[8,4,32,8,128]{4,3,2,1,0:T(8,128)} convert(bf16[8,4,32,8,128]{4,3,2,1,0:T(8,128)(2,1)S(1)} %all-to-all-done.1) | non-fusion elementwise | flops 1048576 | bytes 6291456 | tf_op jit(solution)/shard_map/convert_element_type | solution.py:119
  70.5 31.3 %all-gather.2.cloned.1.call-done = bf16[648,4096]{1,0:T(8,128)(2,1)} async-done(((bf16[648,128]{1,0:T(8,128)(2,1)}), bf16[648,4096]{1,0:T(8,128)(2,1)}) %all-gather.2.cloned.1.call-update) | async-done | bytes 5308432 | tf_op jit(solution)/shard_map/all_gather | solution.py:109
  101.8 0.8 slice_convert_fusion
  102.7 5.6 %fusion = f32[256,640]{1,0:T(8,128)S(1)} fusion(bf16[648,4096]{1,0:T(8,128)(2,1)} %all-gather.2.cloned.1.call-done, f32[256,4096]{1,0:T(8,128)} %bitcast.41, f32[4096]{0:T(1024)S(1)} %bitcast.48, f32[256]{0:T(256)S(1)} %rsqrt.11), kind=kOutput, calls=%fused_computation.1 | convolution fusion | flops 1345323008 | bytes 10109952 | tf_op jit(solution)/shard_map/dot_general | solution.py:126
  108.4 0.6 fusion.10
  108.9 0.2 reshape.353
  109.1 0.1 fusion.16
  109.2 2.3 %gather_fusion = bf16[576,8,128]{2,1,0:T(8,128)(2,1)S(1)} fusion(bf16[32,8,128]{2,1,0:T(8,128)(2,1)S(1)} %fusion.16, s32[1024]{0:T(1024)S(1)} %pad_clamp_fusion), kind=kCustom, calls=%fused_computation | custom fusion | bytes 2361600 | tf_op jit(solution)/shard_map/jit(_take)/gather | solution.py:146
  111.6 0.5 subtract_convert_fusion
  112.1 1.3 pad_maximum_fusion
  113.4 9.6 %all-to-all-start.2 = ((bf16[32,176,128]{2,1,0:T(8,128)(2,1)}), bf16[32,176,128]{2,1,0:T(8,128)(2,1)S(1)}, u32[]{:S(2)}, u32[]{:S(2)}) async-start(bf16[32,176,128]{2,1,0:T(8,128)(2,1)} %pad_maximum_fusion), calls=%async_computation.2 | async-start | bytes 2883584 | tf_op jit(solution)/shard_map/all_to_all | solution.py:149
  123.1 31.4 %all-to-all-done.2 = bf16[32,176,128]{2,1,0:T(8,128)(2,1)S(1)} async-done(((bf16[32,176,128]{2,1,0:T(8,128)(2,1)}), bf16[32,176,128]{2,1,0:T(8,128)(2,1)S(1)}, u32[]{:S(2)}, u32[]{:S(2)}) %all-to-all-start.2) | async-done | bytes 1441824 | tf_op jit(solution)/shard_map/all_to_all | solution.py:149
  154.5 0.1 collective-permute-start
  154.6 0.2 iota_add_fusion
  154.8 0.1 add.214
  155.1 0.1 convert_reduce_fusion.1
  155.4 0.2 add_reduce_fusion
  155.6 0.2 fusion.17
  155.8 0.7 iota_add_fusion.1.qidx_ref
  156.5 1.1 collective-permute-done
  157.6 2.9 %broadcast_select_fusion = (bf16[32,144,128]{2,1,0:T(8,128)(2,1)}, bf16[32,144,128]{2,1,0:T(8,128)(2,1)}, bf16[32,18,8,128]{3,2,1,0:T(8,128)(2,1)S(1)}) fusion(bf16[32,144,128]{2,1,0:T(8,128)(2,1)} %collective-permute-done, pred[]{:T(512)S(6)} %eq.79, bf16[32,176,128]{2,1,0:T(8,128)(2,1)S(1)} %all-to-all-done.2), kind=kLoop, calls=%fused_computation.11 | loop fusion | flops 1179648 | bytes 5898241 | tf_op jit(solution)/shard_map/jit(_where)/select_n | solution.py:154
  160.6 0.2 fusion.2
  160.8 0.5 broadcast.338
  161.3 0.7 reduce.4
  161.9 0.7 reshape.377
  162.7 5.6 %all-to-all-start.3 = ((bf16[32,2,1024]{2,1,0:T(2,128)(2,1)}), bf16[32,2,1024]{2,1,0:T(2,128)(2,1)S(1)}, u32[]{:S(2)}, u32[]{:S(2)}) async-start(bf16[32,2,1024]{2,1,0:T(2,128)(2,1)} %reshape.377), calls=%async_computation.3 | async-start | bytes 262144 | tf_op jit(solution)/shard_map/all_to_all | solution.py:192
  168.3 0.1 convert_reduce_fusion
  168.4 0.8 add.215.kidx_ref
  169.2 0.8 copy.27.qseg_ref
  170.0 0.6 reshape.361.kseg_ref
  170.6 0.9 reshape.357.q_ref
  171.5 16.6 %shard_map.86 = bf16[256,512]{1,0:T(8,128)(2,1)} custom-call(bf16[256,512]{1,0:T(8,128)(2,1)} %reshape.357.q_ref, bf16[4608,128]{1,0:T(8,128)(2,1)} %bitcast.43, bf16[4608,128]{1,0:T(8,128)(2,1)} %bitcast.42, s32[256,1]{1,0:T(8,128)} %copy.27.qseg_ref, s32[256,1]{1,0:T(8,128)} %iota_add_fusion.1.qidx_ref, s32[1,4608]{1,0:T(1,128)} %reshape.361.kseg_ref, ...), custom_call_target="tpu_custom_call" | custom-call | flops 2415919104 | bytes 2922496 | tf_op jit(solution)/shard_map/pallas_call | solution.py:67
  188.1 0.1 reshape.378
  188.2 0.2 fusion.5
  188.4 0.6 copy.34
  (37 shorter events, 0.9 us)
Async XLA Ops:
  7.2 1.0 copy-start
  7.2 94.6 %all-gather.2.cloned.1.call-start = ((), (), s32[]{:S(2)}) async-start(), calls=%async_computation.4 | async-start | bytes 5474304 | tf_op jit(solution)/shard_map/all_gather | solution.py:109
  36.7 5.0 %copy-start.3 = (s32[8]{0:T(128)S(1)}, s32[8]{0:T(128)}, u32[]{:S(2)}) copy-start(s32[8]{0:T(128)} %param.11) | copy-start | bytes 100
  36.7 5.2 %copy-start.2 = (s32[576]{0:T(1024)S(1)}, s32[576]{0:T(1024)}, u32[]{:S(2)}) copy-start(s32[576]{0:T(1024)} %constant.149) | copy-start | bytes 6916
  36.7 30.7 %all-to-all-start.1 = ((bf16[8,4,32,8,128]{4,3,2,1,0:T(8,128)(2,1)}), bf16[8,4,32,8,128]{4,3,2,1,0:T(8,128)(2,1)S(1)}, u32[]{:S(2)}, u32[]{:S(2)}) async-start(bf16[8,4,32,8,128]{4,3,2,1,0:T(8,128)(2,1)} %broadcast_in_dim.52), calls=%async_computation.1 | async-start | bytes 4194304 | tf_op jit(solution)/shard_map/all_to_all | solution.py:117
  113.4 41.0 %all-to-all-start.2 = ((bf16[32,176,128]{2,1,0:T(8,128)(2,1)}), bf16[32,176,128]{2,1,0:T(8,128)(2,1)S(1)}, u32[]{:S(2)}, u32[]{:S(2)}) async-start(bf16[32,176,128]{2,1,0:T(8,128)(2,1)} %pad_maximum_fusion), calls=%async_computation.2 | async-start | bytes 2883584 | tf_op jit(solution)/shard_map/all_to_all | solution.py:149
  123.0 32.0 %copy-start.1 = (s32[512]{0:T(512)S(1)}, s32[512]{0:T(512)}, u32[]{:S(2)}) copy-start(s32[512]{0:T(512)} %param.12) | copy-start | bytes 6148
  154.5 3.1 %collective-permute-start = (bf16[32,144,128]{2,1,0:T(8,128)(2,1)S(1)}, bf16[32,144,128]{2,1,0:T(8,128)(2,1)}, u32[]{:S(2)}, u32[]{:S(2)}) collective-permute-start(bf16[32,144,128]{2,1,0:T(8,128)(2,1)S(1)} %slice.51), channel_id=1, source_target_pairs={{0,32},{32,0},{64,96},{96,64},{128,160},{160,128},{192,224},{224,1... | collective-permute-start | bytes 3538952 | tf_op jit(solution)/shard_map/ppermute | solution.py:152
  162.7 25.4 %all-to-all-start.3 = ((bf16[32,2,1024]{2,1,0:T(2,128)(2,1)}), bf16[32,2,1024]{2,1,0:T(2,128)(2,1)S(1)}, u32[]{:S(2)}, u32[]{:S(2)}) async-start(bf16[32,2,1024]{2,1,0:T(2,128)(2,1)} %reshape.377), calls=%async_computation.3 | async-start | bytes 262144 | tf_op jit(solution)/shard_map/all_to_all | solution.py:192
Sparse Core Ops, SparseCore 0:
  11.0 90.7 all-gather.1

commit v6 on v5

--- a/solution.py
+++ b/solution.py
@@ -105,11 +105,12 @@
     gain_rows = jnp.concatenate(
         [norm_gain[None, :], jnp.zeros((7, local_feats), norm_gain.dtype)], axis=0
     )
-    stacked = jnp.concatenate([query_proj, kv_rows, gain_rows], axis=0)
-    gathered = lax.all_gather(stacked, "gy", axis=1, tiled=True)
-    weight_rows = query_cols + HD
-    weights_full = gathered[:weight_rows]
-    gain_full = gathered[weight_rows]
+    kv_stack = jnp.concatenate([kv_rows, gain_rows], axis=0)
+    kv_spread = jnp.broadcast_to(kv_stack[None], (count_gy,) + kv_stack.shape)
+    kv_arrived = lax.all_to_all(kv_spread, "gy", 0, 0, tiled=True)
+    kv_weights = kv_arrived[:, :HD]
+    gain_full = kv_arrived[:, HD].reshape(features)
+    query_weights = lax.all_gather(query_proj, "gy", axis=1, tiled=True)
 
     pieces = hidden_in.reshape(blocks_per_slab, count_gy, sub, local_feats)
     pieces = lax.all_to_all(pieces, "gy", 1, 1, tiled=True)
@@ -123,15 +124,14 @@
         * gain_full.astype(jnp.float32)[None, :]
     ).astype(jnp.bfloat16)
     contract = (((1,), (1,)), ((), ()))
-    projected = lax.dot_general(normed, weights_full, contract, preferred_element_type=jnp.float32)
+    half_raw = lax.dot_general(
+        normed.reshape(block_tokens, count_gy, local_feats), kv_weights,
+        (((1, 2), (0, 2)), ((), ())), preferred_element_type=jnp.float32,
+    )
 
     order = jnp.arange(block_tokens, dtype=jnp.int32)
     my_tokens = (order // sub) * block_tokens + where_gy * sub + order % sub
     unused_segment, my_places = token_places(prompt_lengths, my_tokens)
-    queries = rotate(
-        projected[:, :query_cols].reshape(block_tokens, heads_here, HD), my_places
-    ).astype(jnp.bfloat16)
-    half_raw = projected[:, query_cols:]
     rotated = rotate(half_raw[:, None, :], my_places)[:, 0, :]
     mine = jnp.where(is_key, rotated, half_raw).astype(jnp.bfloat16)
 
@@ -144,11 +144,12 @@
     )
     strided = mine.reshape(count_gy, sub, HD)
     kv_parcel = jnp.take(strided, chosen, axis=0).reshape(count_gy, window_blocks * sub, HD)
-    q_parcel = queries.reshape(count_gy, sub * heads_here, HD)
-    parcel = jnp.concatenate([q_parcel, kv_parcel], axis=1)
-    arrived = lax.all_to_all(parcel, "gy", 0, 0, tiled=True)
-    queries = arrived[:, : sub * heads_here].reshape(block_tokens, query_cols)
-    mine_window = arrived[:, sub * heads_here :]
+    mine_window = lax.all_to_all(kv_parcel, "gy", 0, 0, tiled=True)
+    projected = lax.dot_general(normed, query_weights, contract, preferred_element_type=jnp.float32)
+    queries = rotate(projected.reshape(block_tokens, heads_here, HD), my_places).astype(jnp.bfloat16)
+    queries = lax.all_to_all(
+        queries.reshape(count_gy, sub * heads_here, HD), "gy", 0, 0, tiled=True
+    ).reshape(block_tokens, query_cols)
     other_window = lax.ppermute(mine_window, "gx", [(p, p ^ 1) for p in range(count_gx)])
     key_rows = jnp.where(is_key, mine_window, other_window).reshape(window, HD)
     value_rows = jnp.where(is_key, other_window, mine_window).reshape(window, HD)

time: 197 us -> 218 us (1.11)
  blocking collectives: 23.8 us -> 0 us
  local copies, waits for them, and re-layouts: 12.2 us -> 27.6 us
  starting transfers between devices: 20.3 us -> 35.3 us
  other arithmetic: 14.2 us -> 23.4 us
  waiting for transfers between devices: 88.6 us -> 92.6 us
    all_gather x1, waiting for transfers between devices: 31.3 us -> 0.02 us  [local(): query_weights = lax.all_gather(query_proj, 'gy', axis=1, tiled=True)]
    all_to_all x1 -> x4, waiting for transfers between devices: 31.4 us -> 61.3 us  [the longest x1 30.2 us: local(): kv_arrived = lax.all_to_all(kv_spread, 'gy', 0, 0, tiled=True)]
    all_to_all x1 -> x0, blocking collectives: 23.8 us -> none  [local(): pieces = lax.all_to_all(pieces, 'gy', 1, 1, tiled=True)]
    all_to_all x1 -> x4, starting transfers between devices: 9.56 us -> 24.4 us  [the longest x1 11.5 us: local(): pieces = lax.all_to_all(pieces, 'gy', 1, 1, tiled=True)]
    all_to_all x1, waiting for transfers between devices: 0.01 us -> 5.79 us  [local(): lax.all_to_all(outgoing, 'gy', split_axis=0, concat_axis=0, tiled=True)]
    mul x1, other arithmetic: 0.85 us -> 4.03 us  [local(): widened * lax.rsqrt(squares / features + epsilon)[:, None]]
    convert_element_type x0 -> x2, local copies, waits for them, and re-layouts: none -> 2.93 us  [the longest x1 2.82 us: local(): normed = (widened * lax.rsqrt(squares / features + epsilon)[:, None] * ga...]
    eq x2, local copies, waits for them, and re-layouts: 0.15 us -> 2.74 us  [local(): same_owner = owners[:, :, None] == owners[:, None, :]]
  transfers between devices with their start and end apart: 5 -> 8, of which waited for: 4 -> 6; matrix products, arithmetic and copies ran while one was open for 6% -> 25% of each run, Pallas kernels for 8% -> 0%
where the time goes in v6:
time: 218 us; the launch traced here: 216 us
  waiting for transfers between devices  92.6 us (42%)
  starting transfers between devices  35.3 us (16%)
  local copies, waits for them, and re-layouts  27.6 us (13%)
  other arithmetic  23.4 us (11%)
  Pallas kernels  16.6 us (8%)
  between operations  14.4 us (7%)
  matrix products  6.22 us (3%)
    all_to_all x1, waiting for transfers between devices, local(): kv_arrived = lax.all_to_all(kv_spread, 'gy', 0, 0, tiled=True)  30.2 us
    all_to_all x1, waiting for transfers between devices, local(): rows_here = lax.all_to_all(spread, 'gx', 0, 0, tiled=True)  24.7 us
    pallas_call x1, Pallas kernels, segment_attention(): pl.pallas_call(functools.partial(attention_body, 1.0 / math.sqrt(head_siz...  16.6 us
    all_to_all x1, waiting for transfers between devices, local(): mine_window = lax.all_to_all(kv_parcel, 'gy', 0, 0, tiled=True)  14.5 us
    all_to_all x1, waiting for transfers between devices, local(): pieces = lax.all_to_all(pieces, 'gy', 1, 1, tiled=True)  11.6 us
    all_to_all x1, starting transfers between devices, local(): pieces = lax.all_to_all(pieces, 'gy', 1, 1, tiled=True)  11.5 us
    all_to_all x1, starting transfers between devices, local(): lax.all_to_all(outgoing, 'gy', split_axis=0, concat_axis=0, tiled=True)  5.8 us
    all_to_all x1, waiting for transfers between devices, local(): lax.all_to_all(outgoing, 'gy', split_axis=0, concat_axis=0, tiled=True)  5.79 us
  transfers between devices with their start and end apart: 8, of which 6 were waited for; matrix products, arithmetic and copies ran while one was open for 25% of the time, Pallas kernels for 0%

profile of v6, /device:TPU:2, one launch (start us, length us, event | category | flops | bytes accessed | tf_op | source)
XLA Modules:
  0.0 216.2 jit_solution(10363449798157012431)
XLA Ops:
  7.2 1.7 copy.43
  8.9 11.5 %all-to-all-start = ((bf16[4,32,8,128]{3,2,0,1:T(8,128)(2,1)}), bf16[4,32,8,128]{3,2,0,1:T(8,128)(2,1)S(1)}, u32[]{:S(2)}, u32[]{:S(2)}) async-start(bf16[4,32,8,128]{3,2,0,1:T(8,128)(2,1)} %copy.43), calls=%async_computation | async-start | bytes 524288 | tf_op jit(solution)/shard_map/all_to_all | solution.py:116
  20.5 0.7 maximum_maximum_fusion
  21.3 11.6 %all-to-all-done = bf16[4,32,8,128]{3,2,0,1:T(8,128)(2,1)S(1)} async-done(((bf16[4,32,8,128]{3,2,0,1:T(8,128)(2,1)}), bf16[4,32,8,128]{3,2,0,1:T(8,128)(2,1)S(1)}, u32[]{:S(2)}, u32[]{:S(2)}) %all-to-all-start) | async-done | bytes 262176 | tf_op jit(solution)/shard_map/all_to_all | solution.py:116
  32.9 1.1 broadcast_in_dim.57
  34.0 4.4 %all-to-all-start.2 = ((bf16[32,136,128]{2,1,0:T(8,128)(2,1)}), bf16[32,136,128]{2,1,0:T(8,128)(2,1)S(1)}, u32[]{:S(2)}, u32[]{:S(2)}) async-start(bf16[32,136,128]{2,1,0:T(8,128)(2,1)} %broadcast_in_dim.57), calls=%async_computation.2 | async-start | bytes 2228224 | tf_op jit(solution)/shard_map/all_to_all | solution.py:110
  38.4 0.7 all-gather.2.cloned.1.call-update
  39.1 30.2 %all-to-all-done.2 = bf16[32,136,128]{2,1,0:T(8,128)(2,1)S(1)} async-done(((bf16[32,136,128]{2,1,0:T(8,128)(2,1)}), bf16[32,136,128]{2,1,0:T(8,128)(2,1)S(1)}, u32[]{:S(2)}, u32[]{:S(2)}) %all-to-all-start.2) | async-done | bytes 1114144 | tf_op jit(solution)/shard_map/all_to_all | solution.py:110
  69.3 1.7 broadcast_in_dim.54
  71.0 5.1 %all-to-all-start.1 = ((bf16[8,4,32,8,128]{4,3,1,2,0:T(8,128)(2,1)}), bf16[8,4,32,8,128]{4,3,1,2,0:T(8,128)(2,1)S(1)}, u32[]{:S(2)}, u32[]{:S(2)}) async-start(bf16[8,4,32,8,128]{4,3,1,2,0:T(8,128)(2,1)} %broadcast_in_dim.54), calls=%async_computation.1 | async-start | bytes 4194304 | tf_op jit(solution)/shard_map/all_to_all | solution.py:118
  77.0 24.7 %all-to-all-done.1 = bf16[8,4,32,8,128]{4,3,1,2,0:T(8,128)(2,1)S(1)} async-done(((bf16[8,4,32,8,128]{4,3,1,2,0:T(8,128)(2,1)}), bf16[8,4,32,8,128]{4,3,1,2,0:T(8,128)(2,1)S(1)}, u32[]{:S(2)}, u32[]{:S(2)}) %all-to-all-start.1) | async-done | bytes 2097184 | tf_op jit(solution)/shard_map/all_to_all | solution.py:118
  101.8 1.1 multiply_reduce_fusion
  103.0 0.8 copy_convert_fusion
  104.3 0.9 fusion.4
  105.7 3.0 %gather_fusion = bf16[576,8,128]{2,1,0:T(8,128)(2,1)} fusion(bf16[32,8,128]{2,1,0:T(8,128)(2,1)S(1)} %bitcast.49, s32[1024]{0:T(1024)S(1)} %pad_clamp_fusion), kind=kCustom, calls=%fused_computation | custom fusion | bytes 2361600 | tf_op jit(solution)/shard_map/jit(_take)/gather | solution.py:146
  108.7 4.7 %all-to-all-start.4 = ((bf16[32,144,128]{2,1,0:T(8,128)(2,1)}), bf16[32,144,128]{2,1,0:T(8,128)(2,1)S(1)}, u32[]{:S(2)}, u32[]{:S(2)}) async-start(bf16[32,144,128]{2,1,0:T(8,128)(2,1)} %bitcast.51), calls=%async_computation.4 | async-start | bytes 2359296 | tf_op jit(solution)/shard_map/all_to_all | solution.py:147
  113.5 0.9 iota_add_fusion
  114.4 1.7 add.215
  116.1 1.3 add_select_fusion
  117.4 1.4 eq.83
  118.8 1.4 copy.50
  120.2 1.5 convert_reduce_fusion.1
  121.7 1.4 copy.52
  123.0 1.4 broadcast_in_dim.114
  124.4 1.5 add_reduce_fusion
  125.9 0.9 fusion.18
  126.8 0.7 iota_add_fusion.1.qidx_ref
  127.9 1.6 multiply_cosine_fusion.1
  129.6 4.0 %fusion.3 = bf16[8,4,8,32,128]{4,3,2,1,0:T(8,128)(2,1)} fusion(f32[32,128]{1,0:T(8,128)S(1)} %bitcast.59, f32[8,4,8]{2,1,0:T(4,128)} %copy-done.4, bf16[8,4,32,8,128]{4,3,1,2,0:T(8,128)(2,1)S(1)} %all-to-all-done.1), kind=kLoop, calls=%fused_computation.9 | loop fusion | flops 4194304 | bytes 4211712 | tf_op jit(solution)/shard_map/mul | solution.py:123
  133.6 2.8 %reshape.405 = bf16[256,4096,1]{1,0,2:T(8,128)(2,1)S(1)} reshape(bf16[8,4,8,32,128]{4,3,2,1,0:T(8,128)(2,1)} %fusion.3) | data formatting | bytes 4194304 | tf_op jit(solution)/shard_map/convert_element_type | solution.py:125
  136.4 14.5 %all-to-all-done.4 = bf16[32,144,128]{2,1,0:T(8,128)(2,1)S(1)} async-done(((bf16[32,144,128]{2,1,0:T(8,128)(2,1)}), bf16[32,144,128]{2,1,0:T(8,128)(2,1)S(1)}, u32[]{:S(2)}, u32[]{:S(2)}) %all-to-all-start.4) | async-done | bytes 1179680 | tf_op jit(solution)/shard_map/all_to_all | solution.py:147
  151.5 1.5 reshape_reshape.4
  153.0 1.7 fusion.2
  155.2 2.2 reduce.4
  157.3 1.6 reshape.409
  159.0 5.8 %all-to-all-start.5 = ((bf16[32,2,1024]{2,1,0:T(2,128)(2,1)}), bf16[32,2,1024]{2,1,0:T(2,128)(2,1)}, u32[]{:S(2)}, u32[]{:S(2)}) async-start(bf16[32,2,1024]{2,1,0:T(2,128)(2,1)} %reshape.409), calls=%async_computation.5 | async-start | bytes 262144 | tf_op jit(solution)/shard_map/all_to_all | solution.py:193
  164.8 3.5 %fusion.30 = f32[256,4,128]{0,2,1:T(8,128)S(1)} fusion(bf16[256,4096,1]{1,0,2:T(8,128)(2,1)S(1)} %reshape.405, bf16[4,128,4096]{2,1,0:T(8,128)(2,1)} %bitcast.65), kind=kOutput, calls=%fused_computation.89 | convolution fusion | flops 1073741824 | bytes 6815744 | tf_op jit(solution)/shard_map/dot_general | solution.py:148
  168.9 0.9 pad_maximum_fusion
  169.7 5.8 %all-to-all-done.5 = bf16[32,2,1024]{2,1,0:T(2,128)(2,1)} async-done(((bf16[32,2,1024]{2,1,0:T(2,128)(2,1)}), bf16[32,2,1024]{2,1,0:T(2,128)(2,1)}, u32[]{:S(2)}, u32[]{:S(2)}) %all-to-all-start.5) | async-done | bytes 131104 | tf_op jit(solution)/shard_map/all_to_all | solution.py:193
  175.5 3.9 %all-to-all-start.3 = ((bf16[32,32,128]{2,1,0:T(8,128)(2,1)}), bf16[32,32,128]{2,1,0:T(8,128)(2,1)S(1)}, u32[]{:S(2)}, u32[]{:S(2)}) async-start(bf16[32,32,128]{2,1,0:T(8,128)(2,1)} %pad_maximum_fusion), calls=%async_computation.3 | async-start | bytes 524288 | tf_op jit(solution)/shard_map/all_to_all | solution.py:150
  179.6 0.8 add.216.kidx_ref
  180.3 0.8 copy.49.qseg_ref
  181.7 1.4 reshape.410
  183.3 0.6 copy.56
  184.0 2.8 %broadcast_select_fusion = (bf16[32,144,128]{2,1,0:T(8,128)(2,1)}, bf16[32,144,128]{2,1,0:T(8,128)(2,1)}) fusion(bf16[32,144,128]{2,1,0:T(8,128)(2,1)} %collective-permute-done, bf16[32,144,128]{2,1,0:T(8,128)(2,1)S(1)} %all-to-all-done.4, pred[]{:T(512)S(6)} %eq.79), kind=kLoop, calls=%fused_computation.13 | loop fusion | flops 1179648 | bytes 4718593 | tf_op jit(solution)/shard_map/jit(_where)/select_n | solution.py:155
  186.8 5.1 %all-to-all-done.3 = bf16[32,32,128]{2,1,0:T(8,128)(2,1)S(1)} async-done(((bf16[32,32,128]{2,1,0:T(8,128)(2,1)}), bf16[32,32,128]{2,1,0:T(8,128)(2,1)S(1)}, u32[]{:S(2)}, u32[]{:S(2)}) %all-to-all-start.3) | async-done | bytes 262176 | tf_op jit(solution)/shard_map/all_to_all | solution.py:150
  191.9 0.9 reshape.385.q_ref
  192.7 16.6 %shard_map.86 = bf16[256,512]{1,0:T(8,128)(2,1)} custom-call(bf16[256,512]{1,0:T(8,128)(2,1)} %reshape.385.q_ref, bf16[4608,128]{1,0:T(8,128)(2,1)} %bitcast.53, bf16[4608,128]{1,0:T(8,128)(2,1)} %bitcast.52, s32[256,1]{1,0:T(8,128)} %copy.49.qseg_ref, s32[256,1]{1,0:T(8,128)} %iota_add_fusion.1.qidx_ref, s32[1,4608]{1,0:T(1,128)} %reshape.390.kseg_ref, ...), custom_call_target="tpu_custom_call" | custom-call | flops 2415919104 | bytes 2922496 | tf_op jit(solution)/shard_map/pallas_call | solution.py:67
  (66 shorter events, 5.3 us)
Async XLA Ops:
  7.2 13.3 %copy-start = (bf16[1024,128]{1,0:T(8,128)(2,1)S(1)}, bf16[1024,128]{1,0:T(8,128)(2,1)}, u32[]{:S(2)}) copy-start(bf16[1024,128]{1,0:T(8,128)(2,1)} %param.10) | copy-start | bytes 786436
  8.9 23.9 %all-to-all-start = ((bf16[4,32,8,128]{3,2,0,1:T(8,128)(2,1)}), bf16[4,32,8,128]{3,2,0,1:T(8,128)(2,1)S(1)}, u32[]{:S(2)}, u32[]{:S(2)}) async-start(bf16[4,32,8,128]{3,2,0,1:T(8,128)(2,1)} %copy.43), calls=%async_computation | async-start | bytes 524288 | tf_op jit(solution)/shard_map/all_to_all | solution.py:116
  34.0 35.3 %all-to-all-start.2 = ((bf16[32,136,128]{2,1,0:T(8,128)(2,1)}), bf16[32,136,128]{2,1,0:T(8,128)(2,1)S(1)}, u32[]{:S(2)}, u32[]{:S(2)}) async-start(bf16[32,136,128]{2,1,0:T(8,128)(2,1)} %broadcast_in_dim.57), calls=%async_computation.2 | async-start | bytes 2228224 | tf_op jit(solution)/shard_map/all_to_all | solution.py:110
  38.4 126.4 %all-gather.2.cloned.1.call-start = ((), (), s32[]{:S(2)}) async-start(), calls=%async_computation.6 | async-start | bytes 4325376 | tf_op jit(solution)/shard_map/all_gather | solution.py:113
  71.0 5.1 %copy-start.14 = (s32[8]{0:T(128)S(1)}, s32[8]{0:T(128)}, u32[]{:S(2)}) copy-start(s32[8]{0:T(128)} %param.11) | copy-start | bytes 100
  71.0 5.3 %copy-start.8 = (s32[576]{0:T(1024)S(1)}, s32[576]{0:T(1024)}, u32[]{:S(2)}) copy-start(s32[576]{0:T(1024)} %constant.149) | copy-start | bytes 6916
  71.0 30.8 %all-to-all-start.1 = ((bf16[8,4,32,8,128]{4,3,1,2,0:T(8,128)(2,1)}), bf16[8,4,32,8,128]{4,3,1,2,0:T(8,128)(2,1)S(1)}, u32[]{:S(2)}, u32[]{:S(2)}) async-start(bf16[8,4,32,8,128]{4,3,1,2,0:T(8,128)(2,1)} %broadcast_in_dim.54), calls=%async_computation.1 | async-start | bytes 4194304 | tf_op jit(solution)/shard_map/all_to_all | solution.py:118
  76.2 0.8 copy-start.11
  76.3 28.9 %copy-start.9 = (f32[64]{0:T(128)}, f32[64]{0:T(128)S(1)}, u32[]{:S(2)}) copy-start(f32[64]{0:T(128)S(1)} %multiply_power_fusion) | copy-start | bytes 772
  77.0 28.2 %copy-start.6 = (f32[256]{0:T(256)}, f32[256]{0:T(256)S(1)}, u32[]{:S(2)}) copy-start(f32[256]{0:T(256)S(1)} %subtract_convert_fusion.1) | copy-start | bytes 3076
  102.9 0.9 copy-start.4
  108.7 42.2 %all-to-all-start.4 = ((bf16[32,144,128]{2,1,0:T(8,128)(2,1)}), bf16[32,144,128]{2,1,0:T(8,128)(2,1)S(1)}, u32[]{:S(2)}, u32[]{:S(2)}) async-start(bf16[32,144,128]{2,1,0:T(8,128)(2,1)} %bitcast.51), calls=%async_computation.4 | async-start | bytes 2359296 | tf_op jit(solution)/shard_map/all_to_all | solution.py:147
  133.6 19.5 %copy-start.10 = (s32[16]{0:T(128)S(1)}, s32[16]{0:T(128)}, u32[]{:S(2)}) copy-start(s32[16]{0:T(128)} %add_reduce_fusion) | copy-start | bytes 196
  150.9 33.1 %collective-permute-start = (bf16[32,144,128]{2,1,0:T(8,128)(2,1)S(1)}, bf16[32,144,128]{2,1,0:T(8,128)(2,1)}, u32[]{:S(2)}, u32[]{:S(2)}) collective-permute-start(bf16[32,144,128]{2,1,0:T(8,128)(2,1)S(1)} %all-to-all-done.4), channel_id=1, source_target_pairs={{0,32},{32,0},{64,96},{96,64},{128,160},{160,128},{192,224},{224,1... | collective-permute-start | bytes 3538952 | tf_op jit(solution)/shard_map/ppermute | solution.py:153
  159.0 16.5 %all-to-all-start.5 = ((bf16[32,2,1024]{2,1,0:T(2,128)(2,1)}), bf16[32,2,1024]{2,1,0:T(2,128)(2,1)}, u32[]{:S(2)}, u32[]{:S(2)}) async-start(bf16[32,2,1024]{2,1,0:T(2,128)(2,1)} %reshape.409), calls=%async_computation.5 | async-start | bytes 262144 | tf_op jit(solution)/shard_map/all_to_all | solution.py:193
  164.8 3.6 %copy-start.2 = (f32[256,64]{0,1:T(8,128)S(1)}, f32[256,64]{0,1:T(8,128)}, u32[]{:S(2)}) copy-start(f32[256,64]{0,1:T(8,128)} %get-tuple-element.12) | copy-start | bytes 196612
  164.8 3.6 %copy-start.3 = (f32[256,64]{0,1:T(8,128)S(1)}, f32[256,64]{0,1:T(8,128)}, u32[]{:S(2)}) copy-start(f32[256,64]{0,1:T(8,128)} %get-tuple-element.13) | copy-start | bytes 196612
  168.3 11.1 %copy-start.5 = (s32[4608]{0:T(1024)S(1)}, s32[4608]{0:T(1024)}, u32[]{:S(2)}) copy-start(s32[4608]{0:T(1024)} %add.215) | copy-start | bytes 55300
  168.4 11.1 %copy-start.12 = (s32[8,1]{0,1:T(1,128)S(1)}, s32[8,1]{0,1:T(1,128)}, u32[]{:S(2)}) copy-start(s32[8,1]{0,1:T(1,128)} %copy-done.11) | copy-start | bytes 100
  168.4 11.2 %copy-start.1 = (s32[32,18,8]{2,1,0:T(8,128)S(1)}, s32[32,18,8]{2,1,0:T(8,128)}, u32[]{:S(2)}) copy-start(s32[32,18,8]{2,1,0:T(8,128)} %iota_add_fusion) | copy-start | bytes 55300
  168.4 11.9 %copy-start.7 = (s32[256]{0:T(256)S(1)}, s32[256]{0:T(256)}, u32[]{:S(2)}) copy-start(s32[256]{0:T(256)} %get-tuple-element.4) | copy-start | bytes 3076
  168.4 14.7 %copy-start.13 = (s32[16]{0:T(128)S(1)}, s32[16]{0:T(128)}, u32[]{:S(2)}) copy-start(s32[16]{0:T(128)} %fusion.29) | copy-start | bytes 196
  175.5 16.3 %all-to-all-start.3 = ((bf16[32,32,128]{2,1,0:T(8,128)(2,1)}), bf16[32,32,128]{2,1,0:T(8,128)(2,1)S(1)}, u32[]{:S(2)}, u32[]{:S(2)}) async-start(bf16[32,32,128]{2,1,0:T(8,128)(2,1)} %pad_maximum_fusion), calls=%async_computation.3 | async-start | bytes 524288 | tf_op jit(solution)/shard_map/all_to_all | solution.py:150
Sparse Core Ops, SparseCore 0:
  41.7 105.6 all-gather.1

commit v7 on v5

--- a/solution.py
+++ b/solution.py
@@ -18,6 +18,8 @@
 epsilon = 1e-06
 rope_base = 5000000.0
 masked_out = -1e30
+GX = ("x", "core")
+GY = ("y", "z")
 
 
 def token_places(prompt_lengths, token_index):
@@ -87,10 +89,10 @@
 
 
 def local(hidden_in, norm_gain, query_proj, kv_proj, prompt_lengths, cache_slot):
-    count_gx = lax.axis_size("gx")
-    count_gy = lax.axis_size("gy")
-    where_gx = lax.axis_index("gx")
-    where_gy = lax.axis_index("gy")
+    count_gx = lax.axis_size(GX)
+    count_gy = lax.axis_size(GY)
+    where_gx = lax.axis_index(GX)
+    where_gy = lax.axis_index(GY)
     local_rows, local_feats = hidden_in.shape
     features = local_feats * count_gy
     block_tokens = local_rows * count_gx // count_gy
@@ -106,15 +108,16 @@
         [norm_gain[None, :], jnp.zeros((7, local_feats), norm_gain.dtype)], axis=0
     )
     stacked = jnp.concatenate([query_proj, kv_rows, gain_rows], axis=0)
-    gathered = lax.all_gather(stacked, "gy", axis=1, tiled=True)
+    gathered = lax.all_gather(stacked, "z", axis=1, tiled=True)
+    gathered = lax.all_gather(gathered, "y", axis=1, tiled=True)
     weight_rows = query_cols + HD
     weights_full = gathered[:weight_rows]
     gain_full = gathered[weight_rows]
 
     pieces = hidden_in.reshape(blocks_per_slab, count_gy, sub, local_feats)
-    pieces = lax.all_to_all(pieces, "gy", 1, 1, tiled=True)
+    pieces = lax.all_to_all(pieces, GY, 1, 1, tiled=True)
     spread = jnp.broadcast_to(pieces[None], (count_gx,) + pieces.shape)
-    rows_here = lax.all_to_all(spread, "gx", 0, 0, tiled=True)
+    rows_here = lax.all_to_all(spread, GX, 0, 0, tiled=True)
     rows_here = rows_here.transpose(0, 1, 3, 2, 4).reshape(block_tokens, features)
     widened = rows_here.astype(jnp.float32)
     squares = jnp.sum(widened * widened, axis=1)
@@ -146,10 +149,10 @@
     kv_parcel = jnp.take(strided, chosen, axis=0).reshape(count_gy, window_blocks * sub, HD)
     q_parcel = queries.reshape(count_gy, sub * heads_here, HD)
     parcel = jnp.concatenate([q_parcel, kv_parcel], axis=1)
-    arrived = lax.all_to_all(parcel, "gy", 0, 0, tiled=True)
+    arrived = lax.all_to_all(parcel, GY, 0, 0, tiled=True)
     queries = arrived[:, : sub * heads_here].reshape(block_tokens, query_cols)
     mine_window = arrived[:, sub * heads_here :]
-    other_window = lax.ppermute(mine_window, "gx", [(p, p ^ 1) for p in range(count_gx)])
+    other_window = lax.ppermute(mine_window, GX, [(p, p ^ 1) for p in range(count_gx)])
     key_rows = jnp.where(is_key, mine_window, other_window).reshape(window, HD)
     value_rows = jnp.where(is_key, other_window, mine_window).reshape(window, HD)
 
@@ -189,7 +192,7 @@
     slot_range = jnp.arange(slots_all, dtype=jnp.int32)
     send_map = (slot_range[:, None] == target[None, :]).astype(jnp.bfloat16)
     outgoing = jnp.dot(send_map, my_pages, preferred_element_type=jnp.float32).astype(jnp.bfloat16)
-    incoming = lax.all_to_all(outgoing, "gy", split_axis=0, concat_axis=0, tiled=True)
+    incoming = lax.all_to_all(outgoing, GY, split_axis=0, concat_axis=0, tiled=True)
     wanted = where_gy * pages_dev + page_range
     matches = cache_slot[None, :] == wanted[:, None]
     page_ids = jnp.arange(cache_slot.shape[0], dtype=jnp.int32)
@@ -203,10 +206,12 @@
 
 
 def solution(mesh):
+    parts = mesh.devices.reshape(4, 2, 4, 8)
+    split_mesh = jax.sharding.Mesh(parts, ("x", "core", "y", "z"))
     return jax.shard_map(
         local,
-        mesh=mesh,
-        in_specs=(P("gx", "gy"), P("gy"), P("gx", "gy"), P(None, "gy"), P(), P()),
-        out_specs=(P("gy", "gx"), P("gy", None, "gx")),
+        mesh=split_mesh,
+        in_specs=(P(GX, GY), P(GY), P(GX, GY), P(None, GY), P(), P()),
+        out_specs=(P(GY, GX), P(GY, None, GX)),
         check_vma=False,
     )

time: 197 us -> 216 us (1.096)
  waiting for transfers between devices: 88.6 us -> 114 us
  blocking collectives: 23.8 us -> 18.4 us
    all_gather x1 -> x2, waiting for transfers between devices: 31.3 us -> 51.5 us  [the longest x1 44.5 us: local(): gathered = lax.all_gather(stacked, 'z', axis=1, tiled=True)]
    all_to_all x1, blocking collectives: 23.8 us -> 18.4 us  [local(): pieces = lax.all_to_all(pieces, GY, 1, 1, tiled=True)]
    all_to_all x3, waiting for transfers between devices: 56.1 us -> 61.2 us  [the longest x1 36.5 us: local(): arrived = lax.all_to_all(parcel, GY, 0, 0, tiled=True)]
  transfers between devices with their start and end apart: 5 -> 6, of which waited for: 4 -> 5; matrix products, arithmetic and copies ran while one was open for 6% -> 5% of each run, Pallas kernels for 8% -> 8%
where the time goes in v7:
time: 216 us; the launch traced here: 214 us
  waiting for transfers between devices  114 us (53%)
  starting transfers between devices  19.6 us (9%)
  blocking collectives  18.4 us (9%)
  Pallas kernels  16.6 us (8%)
  between operations  14.3 us (7%)
  other arithmetic  14.2 us (7%)
  local copies, waits for them, and re-layouts  11.2 us (5%)
  matrix products  5.97 us (3%)
    all_gather x1, waiting for transfers between devices, local(): gathered = lax.all_gather(stacked, 'z', axis=1, tiled=True)  44.5 us
    all_to_all x1, waiting for transfers between devices, local(): arrived = lax.all_to_all(parcel, GY, 0, 0, tiled=True)  36.5 us
    all_to_all x1, waiting for transfers between devices, local(): rows_here = lax.all_to_all(spread, GX, 0, 0, tiled=True)  24.8 us
    all_to_all x1, blocking collectives, local(): pieces = lax.all_to_all(pieces, GY, 1, 1, tiled=True)  18.4 us
    pallas_call x1, Pallas kernels, segment_attention(): pl.pallas_call(functools.partial(attention_body, 1.0 / math.sqrt(head_siz...  16.6 us
    all_to_all x1, starting transfers between devices, local(): arrived = lax.all_to_all(parcel, GY, 0, 0, tiled=True)  8.98 us
    all_gather x1, waiting for transfers between devices, local(): gathered = lax.all_gather(gathered, 'y', axis=1, tiled=True)  6.96 us
    dot_general x1, matrix products, local(): lax.dot_general(normed, weights_full, contract, preferred_element_type=jn...  5.61 us
  transfers between devices with their start and end apart: 6, of which 5 were waited for; matrix products, arithmetic and copies ran while one was open for 5% of the time, Pallas kernels for 8%

profile of v7, /device:TPU:2, one launch (start us, length us, event | category | flops | bytes accessed | tf_op | source)
XLA Modules:
  0.0 214.2 jit_solution(11535349115029592531)
XLA Ops:
  7.2 0.9 copy-done
  8.2 1.7 maximum_maximum_fusion
  10.0 44.5 %all-gather.3.cloned.1.call-done = bf16[648,1024]{1,0:T(8,128)(2,1)} async-done(((bf16[648,128]{1,0:T(8,128)(2,1)}), bf16[648,1024]{1,0:T(8,128)(2,1)}) %all-gather.3.cloned.1.call-update) | async-done | bytes 1327120 | tf_op jit(solution)/shard_map/all_gather | solution.py:111
  54.6 18.4 %all_to_all.27 = bf16[4,32,8,128]{3,2,0,1:T(8,128)(2,1)S(1)} all-to-all(bf16[4,32,8,128]{3,2,0,1:T(8,128)(2,1)S(1)} %copy.25), channel_id=1, replica_groups=mesh['x'=4,'core'=2,'y'=4,'z'=8] {'y','z'}, dimensions={1} | all-to-all | bytes 524288 | tf_op jit(solution)/shard_map/all_to_all | solution.py:118
  73.1 1.8 broadcast_in_dim.52
  74.9 4.9 %all-to-all-start.1 = ((bf16[8,4,32,8,128]{4,3,2,1,0:T(8,128)(2,1)}), bf16[8,4,32,8,128]{4,3,2,1,0:T(8,128)(2,1)S(1)}, u32[]{:S(2)}, u32[]{:S(2)}) async-start(bf16[8,4,32,8,128]{4,3,2,1,0:T(8,128)(2,1)} %broadcast_in_dim.52), calls=%async_computation.1 | async-start | bytes 4194304 | tf_op jit(solution)/shard_map/all_to_all | solution.py:120
  79.9 0.2 reduce-window.8
  80.1 0.1 convert_reduce_fusion.2
  80.2 0.1 select_reduce_fusion
  80.3 0.5 multiply_cosine_fusion.1
  80.8 24.8 %all-to-all-done.1 = bf16[8,4,32,8,128]{4,3,2,1,0:T(8,128)(2,1)S(1)} async-done(((bf16[8,4,32,8,128]{4,3,2,1,0:T(8,128)(2,1)}), bf16[8,4,32,8,128]{4,3,2,1,0:T(8,128)(2,1)S(1)}, u32[]{:S(2)}, u32[]{:S(2)}) %all-to-all-start.1) | async-done | bytes 2097184 | tf_op jit(solution)/shard_map/all_to_all | solution.py:120
  105.6 0.5 multiply_reduce_fusion
  106.1 0.1 rsqrt.11
  106.2 2.5 %convert_element_type.65 = f32[8,4,32,8,128]{4,3,2,1,0:T(8,128)} convert(bf16[8,4,32,8,128]{4,3,2,1,0:T(8,128)(2,1)S(1)} %all-to-all-done.1) | non-fusion elementwise | flops 1048576 | bytes 6291456 | tf_op jit(solution)/shard_map/convert_element_type | solution.py:122
  108.7 7.0 %all-gather.5.cloned.1.call-done = bf16[648,4096]{1,0:T(8,128)(2,1)} async-done(((bf16[648,1024]{1,0:T(8,128)(2,1)}), bf16[648,4096]{1,0:T(8,128)(2,1)}) %all-gather.5.cloned.1.call-update) | async-done | bytes 5308432 | tf_op jit(solution)/shard_map/all_gather | solution.py:112
  115.7 0.8 slice_convert_fusion
  116.5 5.6 %fusion = f32[256,640]{1,0:T(8,128)S(1)} fusion(bf16[648,4096]{1,0:T(8,128)(2,1)} %all-gather.5.cloned.1.call-done, f32[256,4096]{1,0:T(8,128)} %bitcast.41, f32[4096]{0:T(1024)S(1)} %bitcast.48, f32[256]{0:T(256)S(1)} %rsqrt.11), kind=kOutput, calls=%fused_computation.1 | convolution fusion | flops 1345323008 | bytes 10109952 | tf_op jit(solution)/shard_map/dot_general | solution.py:129
  122.2 0.6 fusion.10
  122.8 0.2 reshape.353
  123.0 0.1 fusion.16
  123.1 2.3 %gather_fusion = bf16[576,8,128]{2,1,0:T(8,128)(2,1)S(1)} fusion(bf16[32,8,128]{2,1,0:T(8,128)(2,1)S(1)} %fusion.16, s32[1024]{0:T(1024)S(1)} %pad_clamp_fusion), kind=kCustom, calls=%fused_computation | custom fusion | bytes 2361600 | tf_op jit(solution)/shard_map/jit(_take)/gather | solution.py:149
  125.4 0.5 subtract_convert_fusion
  125.9 1.3 pad_maximum_fusion
  127.2 9.0 %all-to-all-start.2 = ((bf16[32,176,128]{2,1,0:T(8,128)(2,1)}), bf16[32,176,128]{2,1,0:T(8,128)(2,1)S(1)}, u32[]{:S(2)}, u32[]{:S(2)}) async-start(bf16[32,176,128]{2,1,0:T(8,128)(2,1)} %pad_maximum_fusion), calls=%async_computation.2 | async-start | bytes 2883584 | tf_op jit(solution)/shard_map/all_to_all | solution.py:152
  136.4 36.5 %all-to-all-done.2 = bf16[32,176,128]{2,1,0:T(8,128)(2,1)S(1)} async-done(((bf16[32,176,128]{2,1,0:T(8,128)(2,1)}), bf16[32,176,128]{2,1,0:T(8,128)(2,1)S(1)}, u32[]{:S(2)}, u32[]{:S(2)}) %all-to-all-start.2) | async-done | bytes 1441824 | tf_op jit(solution)/shard_map/all_to_all | solution.py:152
  172.9 0.1 collective-permute-start
  173.0 0.2 iota_add_fusion
  173.2 0.1 add.222
  173.5 0.1 convert_reduce_fusion.1
  173.8 0.2 add_reduce_fusion
  174.0 0.2 fusion.17
  174.2 0.7 iota_add_fusion.1.qidx_ref
  174.9 1.1 collective-permute-done
  176.0 2.9 %broadcast_select_fusion = (bf16[32,144,128]{2,1,0:T(8,128)(2,1)}, bf16[32,144,128]{2,1,0:T(8,128)(2,1)}, bf16[32,18,8,128]{3,2,1,0:T(8,128)(2,1)S(1)}) fusion(bf16[32,144,128]{2,1,0:T(8,128)(2,1)} %collective-permute-done, pred[]{:T(512)S(6)} %eq.79, bf16[32,176,128]{2,1,0:T(8,128)(2,1)S(1)} %all-to-all-done.2), kind=kLoop, calls=%fused_computation.11 | loop fusion | flops 1179648 | bytes 5898241 | tf_op jit(solution)/shard_map/jit(_where)/select_n | solution.py:157
  178.9 0.2 fusion.2
  179.1 0.5 broadcast.338
  179.6 0.7 reduce.4
  180.3 0.7 reshape.377
  181.0 5.6 %all-to-all-start.3 = ((bf16[32,2,1024]{2,1,0:T(2,128)(2,1)}), bf16[32,2,1024]{2,1,0:T(2,128)(2,1)S(1)}, u32[]{:S(2)}, u32[]{:S(2)}) async-start(bf16[32,2,1024]{2,1,0:T(2,128)(2,1)} %reshape.377), calls=%async_computation.3 | async-start | bytes 262144 | tf_op jit(solution)/shard_map/all_to_all | solution.py:195
  186.6 0.1 convert_reduce_fusion
  186.7 0.8 add.223.kidx_ref
  187.5 0.8 copy.27.qseg_ref
  188.3 0.6 reshape.361.kseg_ref
  188.9 0.9 reshape.357.q_ref
  189.8 16.6 %shard_map.86 = bf16[256,512]{1,0:T(8,128)(2,1)} custom-call(bf16[256,512]{1,0:T(8,128)(2,1)} %reshape.357.q_ref, bf16[4608,128]{1,0:T(8,128)(2,1)} %bitcast.43, bf16[4608,128]{1,0:T(8,128)(2,1)} %bitcast.42, s32[256,1]{1,0:T(8,128)} %copy.27.qseg_ref, s32[256,1]{1,0:T(8,128)} %iota_add_fusion.1.qidx_ref, s32[1,4608]{1,0:T(1,128)} %reshape.361.kseg_ref, ...), custom_call_target="tpu_custom_call" | custom-call | flops 2415919104 | bytes 2922496 | tf_op jit(solution)/shard_map/pallas_call | solution.py:69
  206.4 0.1 reshape.378
  206.5 0.2 fusion.5
  206.7 0.6 copy.34
  (42 shorter events, 1.0 us)
Async XLA Ops:
  7.2 1.0 copy-start
  7.2 47.4 %copy-start.1 = (bf16[1024,128]{1,0:T(8,128)(2,1)S(1)}, bf16[1024,128]{1,0:T(8,128)(2,1)}, u32[]{:S(2)}) copy-start(bf16[1024,128]{1,0:T(8,128)(2,1)} %param.7) | copy-start | bytes 786436
  7.2 47.3 %all-gather.3.cloned.1.call-start = ((), (), s32[]{:S(2)}) async-start(), calls=%async_computation.4 | async-start | bytes 1492992 | tf_op jit(solution)/shard_map/all_gather | solution.py:111
  10.0 105.7 %all-gather.5.cloned.1.call-start = ((), (), s32[]{:S(2)}) async-start(), calls=%async_computation.5 | async-start | bytes 6635520 | tf_op jit(solution)/shard_map/all_gather | solution.py:112
  74.9 4.9 %copy-start.4 = (s32[8]{0:T(128)S(1)}, s32[8]{0:T(128)}, u32[]{:S(2)}) copy-start(s32[8]{0:T(128)} %param.11) | copy-start | bytes 100
  74.9 5.2 %copy-start.3 = (s32[576]{0:T(1024)S(1)}, s32[576]{0:T(1024)}, u32[]{:S(2)}) copy-start(s32[576]{0:T(1024)} %constant.158) | copy-start | bytes 6916
  74.9 30.7 %all-to-all-start.1 = ((bf16[8,4,32,8,128]{4,3,2,1,0:T(8,128)(2,1)}), bf16[8,4,32,8,128]{4,3,2,1,0:T(8,128)(2,1)S(1)}, u32[]{:S(2)}, u32[]{:S(2)}) async-start(bf16[8,4,32,8,128]{4,3,2,1,0:T(8,128)(2,1)} %broadcast_in_dim.52), calls=%async_computation.1 | async-start | bytes 4194304 | tf_op jit(solution)/shard_map/all_to_all | solution.py:120
  127.2 45.6 %all-to-all-start.2 = ((bf16[32,176,128]{2,1,0:T(8,128)(2,1)}), bf16[32,176,128]{2,1,0:T(8,128)(2,1)S(1)}, u32[]{:S(2)}, u32[]{:S(2)}) async-start(bf16[32,176,128]{2,1,0:T(8,128)(2,1)} %pad_maximum_fusion), calls=%async_computation.2 | async-start | bytes 2883584 | tf_op jit(solution)/shard_map/all_to_all | solution.py:152
  136.2 37.1 %copy-start.2 = (s32[512]{0:T(512)S(1)}, s32[512]{0:T(512)}, u32[]{:S(2)}) copy-start(s32[512]{0:T(512)} %param.12) | copy-start | bytes 6148
  172.9 3.1 %collective-permute-start = (bf16[32,144,128]{2,1,0:T(8,128)(2,1)S(1)}, bf16[32,144,128]{2,1,0:T(8,128)(2,1)}, u32[]{:S(2)}, u32[]{:S(2)}) collective-permute-start(bf16[32,144,128]{2,1,0:T(8,128)(2,1)S(1)} %slice.51), channel_id=1, source_target_pairs={{0,32},{32,0},{64,96},{96,64},{128,160},{160,128},{192,224},{224,1... | collective-permute-start | bytes 3538952 | tf_op jit(solution)/shard_map/ppermute | solution.py:155
  181.0 25.4 %all-to-all-start.3 = ((bf16[32,2,1024]{2,1,0:T(2,128)(2,1)}), bf16[32,2,1024]{2,1,0:T(2,128)(2,1)S(1)}, u32[]{:S(2)}, u32[]{:S(2)}) async-start(bf16[32,2,1024]{2,1,0:T(2,128)(2,1)} %reshape.377), calls=%async_computation.3 | async-start | bytes 262144 | tf_op jit(solution)/shard_map/all_to_all | solution.py:195
Sparse Core Ops, SparseCore 0:
  10.3 44.2 all-gather.2
  56.3 59.2 all-gather.4

commit v8 on v5

--- a/solution.py
+++ b/solution.py
@@ -5,6 +5,7 @@
 import jax.numpy as jnp
 from jax import lax
 from jax.experimental import pallas as pl
+from jax.experimental.pallas import tpu as pltpu
 from jax.sharding import PartitionSpec as P
 
 D = 4096
@@ -43,8 +44,7 @@
     )
 
 
-def attention_body(scale, heads, head_size, q_ref, k_ref, v_ref, qseg_ref, qidx_ref, kseg_ref, kidx_ref, o_ref):
-    allowed = (kseg_ref[...] == qseg_ref[...]) & (kidx_ref[...] <= qidx_ref[...])
+def attention_heads(scale, heads, head_size, q_ref, k_ref, v_ref, allowed, o_ref):
     for h in range(heads):
         columns = slice(h * head_size, (h + 1) * head_size)
         scores = lax.dot_general(
@@ -59,30 +59,47 @@
         o_ref[:, columns] = (mixed / totals).astype(o_ref.dtype)
 
 
-def segment_attention(queries, key_rows, value_rows, q_segment, q_index, k_segment, k_index, head_size, row_chunk=64):
+def attention_body(scale, heads, head_size, flag_ref, q_ref, a_ref, b_ref, qseg_ref, qidx_ref, kseg_ref, kidx_ref, o_ref):
+    allowed = (kseg_ref[...] == qseg_ref[...]) & (kidx_ref[...] <= qidx_ref[...])
+
+    @pl.when(flag_ref[0] == 1)
+    def _():
+        attention_heads(scale, heads, head_size, q_ref, a_ref, b_ref, allowed, o_ref)
+
+    @pl.when(flag_ref[0] != 1)
+    def _():
+        attention_heads(scale, heads, head_size, q_ref, b_ref, a_ref, allowed, o_ref)
+
+
+def segment_attention(a_is_key, queries, a_rows, b_rows, q_segment, q_index, k_segment, k_index, head_size, row_chunk=128):
     tokens, cols = queries.shape
     heads = cols // head_size
-    window = key_rows.shape[0]
+    window = a_rows.shape[0]
     flops = 4 * tokens * window * head_size * heads
+    grid_spec = pltpu.PrefetchScalarGridSpec(
+        num_scalar_prefetch=1,
+        grid=(tokens // row_chunk,),
+        in_specs=[
+            pl.BlockSpec((row_chunk, cols), lambda r, f: (r, 0)),
+            pl.BlockSpec((window, head_size), lambda r, f: (0, 0)),
+            pl.BlockSpec((window, head_size), lambda r, f: (0, 0)),
+            pl.BlockSpec((row_chunk, 1), lambda r, f: (r, 0)),
+            pl.BlockSpec((row_chunk, 1), lambda r, f: (r, 0)),
+            pl.BlockSpec((1, window), lambda r, f: (0, 0)),
+            pl.BlockSpec((1, window), lambda r, f: (0, 0)),
+        ],
+        out_specs=pl.BlockSpec((row_chunk, cols), lambda r, f: (r, 0)),
+    )
     return pl.pallas_call(
         functools.partial(attention_body, 1.0 / math.sqrt(head_size), heads, head_size),
-        grid=(tokens // row_chunk,),
-        in_specs=[
-            pl.BlockSpec((row_chunk, cols), lambda r: (r, 0)),
-            pl.BlockSpec((window, head_size), lambda r: (0, 0)),
-            pl.BlockSpec((window, head_size), lambda r: (0, 0)),
-            pl.BlockSpec((row_chunk, 1), lambda r: (r, 0)),
-            pl.BlockSpec((row_chunk, 1), lambda r: (r, 0)),
-            pl.BlockSpec((1, window), lambda r: (0, 0)),
-            pl.BlockSpec((1, window), lambda r: (0, 0)),
-        ],
-        out_specs=pl.BlockSpec((row_chunk, cols), lambda r: (r, 0)),
+        grid_spec=grid_spec,
         out_shape=jax.ShapeDtypeStruct((tokens, cols), jnp.bfloat16),
         cost_estimate=pl.CostEstimate(
             flops=flops, transcendentals=tokens * window * heads,
             bytes_accessed=2 * (2 * tokens * cols + 2 * window * head_size) + 8 * (tokens + window),
         ),
-    )(queries, key_rows, value_rows, q_segment.reshape(tokens, 1), q_index.reshape(tokens, 1),
+    )(a_is_key.astype(jnp.int32).reshape(1), queries, a_rows, b_rows,
+      q_segment.reshape(tokens, 1), q_index.reshape(tokens, 1),
       k_segment.reshape(1, window), k_index.reshape(1, window))
 
 
@@ -150,8 +167,6 @@
     queries = arrived[:, : sub * heads_here].reshape(block_tokens, query_cols)
     mine_window = arrived[:, sub * heads_here :]
     other_window = lax.ppermute(mine_window, "gx", [(p, p ^ 1) for p in range(count_gx)])
-    key_rows = jnp.where(is_key, mine_window, other_window).reshape(window, HD)
-    value_rows = jnp.where(is_key, other_window, mine_window).reshape(window, HD)
 
     first_query = where_gy * block_tokens
     token_index = first_query + order
@@ -165,7 +180,7 @@
     ).reshape(window)
     key_segment, unused_places = token_places(prompt_lengths, key_index)
     attention = segment_attention(
-        queries, key_rows, value_rows,
+        is_key, queries, mine_window.reshape(window, HD), other_window.reshape(window, HD),
         segment_own, token_index, key_segment, key_index, HD,
     )
 

time: 197 us -> 196 us (level)
  waiting for transfers between devices: 88.6 us -> 94.8 us
  Pallas kernels: 16.6 us -> 12.1 us
  other arithmetic: 14.2 us -> 11.2 us
    all_to_all x1, waiting for transfers between devices: 0.01 us -> 7.5 us  [local(): lax.all_to_all(outgoing, 'gy', split_axis=0, concat_axis=0, tiled=True)]
    pallas_call x1, Pallas kernels: 16.6 us -> 12.1 us  [segment_attention(): pl.pallas_call(functools.partial(attention_body, 1.0 / math.sqrt(head_siz...]
    select_n x1 -> x0, other arithmetic: 2.95 us -> none  [local(): jnp.where(is_key, other_window, mine_window).reshape(window, HD)]
  transfers between devices with their start and end apart: 5 -> 5, of which waited for: 4 -> 4; matrix products, arithmetic and copies ran while one was open for 6% -> 8% of each run, Pallas kernels for 8% -> 0%
where the time goes in v8:
time: 196 us
  waiting for transfers between devices  94.8 us (48%)
  blocking collectives  23.8 us (12%)
  starting transfers between devices  20.3 us (10%)
  between operations  14.3 us (7%)
  local copies, waits for them, and re-layouts  13.4 us (7%)
  Pallas kernels  12.1 us (6%)
  other arithmetic  11.2 us (6%)
  matrix products  5.97 us (3%)
    all_gather x1, waiting for transfers between devices, local(): gathered = lax.all_gather(stacked, 'gy', axis=1, tiled=True)  31.3 us
    all_to_all x1, waiting for transfers between devices, local(): arrived = lax.all_to_all(parcel, 'gy', 0, 0, tiled=True)  31.2 us
    all_to_all x1, waiting for transfers between devices, local(): rows_here = lax.all_to_all(spread, 'gx', 0, 0, tiled=True)  24.8 us
    all_to_all x1, blocking collectives, local(): pieces = lax.all_to_all(pieces, 'gy', 1, 1, tiled=True)  23.8 us
    pallas_call x1, Pallas kernels, segment_attention(): pl.pallas_call(functools.partial(attention_body, 1.0 / math.sqrt(head_siz...  12.1 us
    all_to_all x1, starting transfers between devices, local(): arrived = lax.all_to_all(parcel, 'gy', 0, 0, tiled=True)  9.69 us
    all_to_all x1, waiting for transfers between devices, local(): lax.all_to_all(outgoing, 'gy', split_axis=0, concat_axis=0, tiled=True)  7.5 us
    dot_general x1, matrix products, local(): lax.dot_general(normed, weights_full, contract, preferred_element_type=jn...  5.61 us
  transfers between devices with their start and end apart: 5, of which 4 were waited for; matrix products, arithmetic and copies ran while one was open for 8% of the time, Pallas kernels for 0%

profile of v8, /device:TPU:2, one launch (start us, length us, event | category | flops | bytes accessed | tf_op | source)
XLA Modules:
  0.0 195.8 jit_solution(8928098788344087415)
XLA Ops:
  7.2 0.9 copy-done
  8.2 1.7 maximum_maximum_fusion
  10.0 1.0 copy.25
  11.0 23.8 %all_to_all.27 = bf16[4,32,8,128]{3,2,0,1:T(8,128)(2,1)S(1)} all-to-all(bf16[4,32,8,128]{3,2,0,1:T(8,128)(2,1)S(1)} %copy.25), channel_id=1, replica_groups=mesh['gx'=8,'gy'=32] {'gy'}, dimensions={1} | all-to-all | bytes 524288 | tf_op jit(solution)/shard_map/all_to_all | solution.py:132
  34.8 1.8 broadcast_in_dim.52
  36.7 5.0 %all-to-all-start.1 = ((bf16[8,4,32,8,128]{4,3,2,1,0:T(8,128)(2,1)}), bf16[8,4,32,8,128]{4,3,2,1,0:T(8,128)(2,1)S(1)}, u32[]{:S(2)}, u32[]{:S(2)}) async-start(bf16[8,4,32,8,128]{4,3,2,1,0:T(8,128)(2,1)} %broadcast_in_dim.52), calls=%async_computation.1 | async-start | bytes 4194304 | tf_op jit(solution)/shard_map/all_to_all | solution.py:134
  41.6 0.2 reduce-window.8
  41.9 0.1 convert_reduce_fusion.2
  42.0 0.1 select_reduce_fusion
  42.1 0.5 multiply_cosine_fusion.1
  42.6 24.8 %all-to-all-done.1 = bf16[8,4,32,8,128]{4,3,2,1,0:T(8,128)(2,1)S(1)} async-done(((bf16[8,4,32,8,128]{4,3,2,1,0:T(8,128)(2,1)}), bf16[8,4,32,8,128]{4,3,2,1,0:T(8,128)(2,1)S(1)}, u32[]{:S(2)}, u32[]{:S(2)}) %all-to-all-start.1) | async-done | bytes 2097184 | tf_op jit(solution)/shard_map/all_to_all | solution.py:134
  67.3 0.5 multiply_reduce_fusion
  67.9 0.1 rsqrt.11
  68.0 2.5 %convert_element_type.66 = f32[8,4,32,8,128]{4,3,2,1,0:T(8,128)} convert(bf16[8,4,32,8,128]{4,3,2,1,0:T(8,128)(2,1)S(1)} %all-to-all-done.1) | non-fusion elementwise | flops 1048576 | bytes 6291456 | tf_op jit(solution)/shard_map/convert_element_type | solution.py:136
  70.5 31.3 %all-gather.2.cloned.1.call-done = bf16[648,4096]{1,0:T(8,128)(2,1)} async-done(((bf16[648,128]{1,0:T(8,128)(2,1)}), bf16[648,4096]{1,0:T(8,128)(2,1)}) %all-gather.2.cloned.1.call-update) | async-done | bytes 5308432 | tf_op jit(solution)/shard_map/all_gather | solution.py:126
  101.8 0.8 slice_convert_fusion
  102.7 5.6 %fusion = f32[256,640]{1,0:T(8,128)S(1)} fusion(bf16[648,4096]{1,0:T(8,128)(2,1)} %all-gather.2.cloned.1.call-done, f32[256,4096]{1,0:T(8,128)} %bitcast.42, f32[4096]{0:T(1024)S(1)} %bitcast.47, f32[256]{0:T(256)S(1)} %rsqrt.11), kind=kOutput, calls=%fused_computation.1 | convolution fusion | flops 1345323008 | bytes 10109952 | tf_op jit(solution)/shard_map/dot_general | solution.py:143
  108.4 0.6 fusion.10
  108.9 0.2 reshape.360
  109.1 0.1 fusion.16
  109.2 2.3 %gather_fusion = bf16[576,8,128]{2,1,0:T(8,128)(2,1)S(1)} fusion(bf16[32,8,128]{2,1,0:T(8,128)(2,1)S(1)} %fusion.16, s32[1024]{0:T(1024)S(1)} %pad_clamp_fusion), kind=kCustom, calls=%fused_computation | custom fusion | bytes 2361600 | tf_op jit(solution)/shard_map/jit(_take)/gather | solution.py:163
  111.6 0.5 subtract_convert_fusion
  112.1 1.3 pad_maximum_fusion
  113.4 9.7 %all-to-all-start.2 = ((bf16[32,176,128]{2,1,0:T(8,128)(2,1)}), bf16[32,176,128]{2,1,0:T(8,128)(2,1)S(1)}, u32[]{:S(2)}, u32[]{:S(2)}) async-start(bf16[32,176,128]{2,1,0:T(8,128)(2,1)} %pad_maximum_fusion), calls=%async_computation.2 | async-start | bytes 2883584 | tf_op jit(solution)/shard_map/all_to_all | solution.py:166
  123.2 0.2 iota_add_fusion
  123.4 31.2 %all-to-all-done.2 = bf16[32,176,128]{2,1,0:T(8,128)(2,1)S(1)} async-done(((bf16[32,176,128]{2,1,0:T(8,128)(2,1)}), bf16[32,176,128]{2,1,0:T(8,128)(2,1)S(1)}, u32[]{:S(2)}, u32[]{:S(2)}) %all-to-all-start.2) | async-done | bytes 1441824 | tf_op jit(solution)/shard_map/all_to_all | solution.py:166
  154.6 1.3 slice_bitcast_fusion.1
  155.9 0.1 add.214
  156.2 0.1 convert_reduce_fusion.1
  156.4 0.1 broadcast_in_dim.107
  156.5 0.2 add_reduce_fusion
  156.7 0.1 convert_reduce_fusion
  156.8 0.7 iota_add_fusion.1.qidx_ref
  157.5 0.2 fusion.2
  157.7 0.5 broadcast.338
  158.2 0.7 reduce.4
  158.9 0.7 reshape.386
  159.6 5.6 %all-to-all-start.3 = ((bf16[32,2,1024]{2,1,0:T(2,128)(2,1)}), bf16[32,2,1024]{2,1,0:T(2,128)(2,1)S(1)}, u32[]{:S(2)}, u32[]{:S(2)}) async-start(bf16[32,2,1024]{2,1,0:T(2,128)(2,1)} %reshape.386), calls=%async_computation.3 | async-start | bytes 262144 | tf_op jit(solution)/shard_map/all_to_all | solution.py:207
  165.2 0.2 fusion.17
  165.4 0.8 add.215.kidx_ref
  166.2 0.8 copy.27.qseg_ref
  167.0 0.6 reshape.368.kseg_ref
  167.6 0.9 reshape.364.q_ref
  168.5 7.5 %all-to-all-done.3 = bf16[32,2,1024]{2,1,0:T(2,128)(2,1)S(1)} async-done(((bf16[32,2,1024]{2,1,0:T(2,128)(2,1)}), bf16[32,2,1024]{2,1,0:T(2,128)(2,1)S(1)}, u32[]{:S(2)}, u32[]{:S(2)}) %all-to-all-start.3) | async-done | bytes 131104 | tf_op jit(solution)/shard_map/all_to_all | solution.py:207
  176.0 0.1 reshape.387
  176.1 0.2 fusion.5
  176.3 0.6 copy.34
  176.9 12.1 %shard_map.86 = bf16[256,512]{1,0:T(8,128)(2,1)} custom-call(s32[1]{0:T(128)} %bitcast.flag_ref, bf16[256,512]{1,0:T(8,128)(2,1)} %reshape.364.q_ref, bf16[4608,128]{1,0:T(8,128)(2,1)} %bitcast.14.a_ref, bf16[4608,128]{1,0:T(8,128)(2,1)} %bitcast.15.b_ref, s32[256,1]{1,0:T(8,128)} %copy.27.qseg_ref, s32[256,1]{1,0:T(8,128)} %iota_add_fusion.1.qidx_ref, ...), custom_call_target="tpu_custom_call" | custom-call | flops 2415919104 | bytes 2922496 | tf_op jit(solution)/shard_map/pallas_call | solution.py:93
  (36 shorter events, 0.7 us)
Async XLA Ops:
  7.2 1.0 copy-start
  7.2 94.6 %all-gather.2.cloned.1.call-start = ((), (), s32[]{:S(2)}) async-start(), calls=%async_computation.4 | async-start | bytes 5474304 | tf_op jit(solution)/shard_map/all_gather | solution.py:126
  36.7 5.0 %copy-start.3 = (s32[8]{0:T(128)S(1)}, s32[8]{0:T(128)}, u32[]{:S(2)}) copy-start(s32[8]{0:T(128)} %param.11) | copy-start | bytes 100
  36.7 5.2 %copy-start.2 = (s32[576]{0:T(1024)S(1)}, s32[576]{0:T(1024)}, u32[]{:S(2)}) copy-start(s32[576]{0:T(1024)} %constant.149) | copy-start | bytes 6916
  36.7 30.7 %all-to-all-start.1 = ((bf16[8,4,32,8,128]{4,3,2,1,0:T(8,128)(2,1)}), bf16[8,4,32,8,128]{4,3,2,1,0:T(8,128)(2,1)S(1)}, u32[]{:S(2)}, u32[]{:S(2)}) async-start(bf16[8,4,32,8,128]{4,3,2,1,0:T(8,128)(2,1)} %broadcast_in_dim.52), calls=%async_computation.1 | async-start | bytes 4194304 | tf_op jit(solution)/shard_map/all_to_all | solution.py:134
  113.4 9.7 %copy-start.1 = (s32[512]{0:T(512)S(1)}, s32[512]{0:T(512)}, u32[]{:S(2)}) copy-start(s32[512]{0:T(512)} %param.12) | copy-start | bytes 6148
  113.4 41.2 %all-to-all-start.2 = ((bf16[32,176,128]{2,1,0:T(8,128)(2,1)}), bf16[32,176,128]{2,1,0:T(8,128)(2,1)S(1)}, u32[]{:S(2)}, u32[]{:S(2)}) async-start(bf16[32,176,128]{2,1,0:T(8,128)(2,1)} %pad_maximum_fusion), calls=%async_computation.2 | async-start | bytes 2883584 | tf_op jit(solution)/shard_map/all_to_all | solution.py:166
  155.9 21.1 %collective-permute-start = (bf16[32,144,128]{2,1,0:T(8,128)(2,1)}, bf16[32,144,128]{2,1,0:T(8,128)(2,1)}, u32[]{:S(2)}, u32[]{:S(2)}) collective-permute-start(bf16[32,144,128]{2,1,0:T(8,128)(2,1)} %get-tuple-element.7), channel_id=1, source_target_pairs={{0,32},{32,0},{64,96},{96,64},{128,160},{160,128},{192,224},{224,1... | collective-permute-start | bytes 3538952 | tf_op jit(solution)/shard_map/ppermute | solution.py:169
  159.6 16.4 %all-to-all-start.3 = ((bf16[32,2,1024]{2,1,0:T(2,128)(2,1)}), bf16[32,2,1024]{2,1,0:T(2,128)(2,1)S(1)}, u32[]{:S(2)}, u32[]{:S(2)}) async-start(bf16[32,2,1024]{2,1,0:T(2,128)(2,1)} %reshape.386), calls=%async_computation.3 | async-start | bytes 262144 | tf_op jit(solution)/shard_map/all_to_all | solution.py:207
Sparse Core Ops, SparseCore 0:
  11.0 90.7 all-gather.1

commit v9 on v8

--- a/solution.py
+++ b/solution.py
@@ -8,9 +8,7 @@
 from jax.experimental.pallas import tpu as pltpu
 from jax.sharding import PartitionSpec as P
 
-D = 4096
-H = 32
-KVH = 4
+
 HD = 128
 PAGES_DEV = 16
 MOST = 4096
@@ -111,7 +109,6 @@
     local_rows, local_feats = hidden_in.shape
     features = local_feats * count_gy
     block_tokens = local_rows * count_gx // count_gy
-    all_tokens = block_tokens * count_gy
     blocks_per_slab = local_rows // block_tokens
     sub = block_tokens // count_gy
     heads_here = query_proj.shape[0] // HD
@@ -144,7 +141,7 @@
 
     order = jnp.arange(block_tokens, dtype=jnp.int32)
     my_tokens = (order // sub) * block_tokens + where_gy * sub + order % sub
-    unused_segment, my_places = token_places(prompt_lengths, my_tokens)
+    _, my_places = token_places(prompt_lengths, my_tokens)
     queries = rotate(
         projected[:, :query_cols].reshape(block_tokens, heads_here, HD), my_places
     ).astype(jnp.bfloat16)

time: 196 us -> 196 us (level)
  no operation moved by 1% of the time
where the time goes in v9:
time: 196 us
  waiting for transfers between devices  94.8 us (48%)
  blocking collectives  23.8 us (12%)
  starting transfers between devices  20.3 us (10%)
  between operations  14.3 us (7%)
  local copies, waits for them, and re-layouts  13.4 us (7%)
  Pallas kernels  12.1 us (6%)
  other arithmetic  11.2 us (6%)
  matrix products  5.97 us (3%)
    all_gather x1, waiting for transfers between devices, local(): gathered = lax.all_gather(stacked, 'gy', axis=1, tiled=True)  31.3 us
    all_to_all x1, waiting for transfers between devices, local(): arrived = lax.all_to_all(parcel, 'gy', 0, 0, tiled=True)  31.2 us
    all_to_all x1, waiting for transfers between devices, local(): rows_here = lax.all_to_all(spread, 'gx', 0, 0, tiled=True)  24.8 us
    all_to_all x1, blocking collectives, local(): pieces = lax.all_to_all(pieces, 'gy', 1, 1, tiled=True)  23.8 us
    pallas_call x1, Pallas kernels, segment_attention(): pl.pallas_call(functools.partial(attention_body, 1.0 / math.sqrt(head_siz...  12.1 us
    all_to_all x1, starting transfers between devices, local(): arrived = lax.all_to_all(parcel, 'gy', 0, 0, tiled=True)  9.69 us
    all_to_all x1, waiting for transfers between devices, local(): lax.all_to_all(outgoing, 'gy', split_axis=0, concat_axis=0, tiled=True)  7.5 us
    dot_general x1, matrix products, local(): lax.dot_general(normed, weights_full, contract, preferred_element_type=jn...  5.61 us
  transfers between devices with their start and end apart: 5, of which 4 were waited for; matrix products, arithmetic and copies ran while one was open for 8% of the time, Pallas kernels for 0%

profile of v9, /device:TPU:2, one launch (start us, length us, event | category | flops | bytes accessed | tf_op | source)
XLA Modules:
  0.0 195.8 jit_solution(8928098788344087415)
XLA Ops:
  7.2 0.9 copy-done
  8.2 1.7 maximum_maximum_fusion
  10.0 1.0 copy.25
  11.0 23.8 %all_to_all.27 = bf16[4,32,8,128]{3,2,0,1:T(8,128)(2,1)S(1)} all-to-all(bf16[4,32,8,128]{3,2,0,1:T(8,128)(2,1)S(1)} %copy.25), channel_id=1, replica_groups=mesh['gx'=8,'gy'=32] {'gy'}, dimensions={1} | all-to-all | bytes 524288 | tf_op jit(solution)/shard_map/all_to_all | solution.py:129
  34.8 1.8 broadcast_in_dim.52
  36.7 5.0 %all-to-all-start.1 = ((bf16[8,4,32,8,128]{4,3,2,1,0:T(8,128)(2,1)}), bf16[8,4,32,8,128]{4,3,2,1,0:T(8,128)(2,1)S(1)}, u32[]{:S(2)}, u32[]{:S(2)}) async-start(bf16[8,4,32,8,128]{4,3,2,1,0:T(8,128)(2,1)} %broadcast_in_dim.52), calls=%async_computation.1 | async-start | bytes 4194304 | tf_op jit(solution)/shard_map/all_to_all | solution.py:131
  41.6 0.2 reduce-window.8
  41.9 0.1 convert_reduce_fusion.2
  42.0 0.1 select_reduce_fusion
  42.1 0.5 multiply_cosine_fusion.1
  42.6 24.8 %all-to-all-done.1 = bf16[8,4,32,8,128]{4,3,2,1,0:T(8,128)(2,1)S(1)} async-done(((bf16[8,4,32,8,128]{4,3,2,1,0:T(8,128)(2,1)}), bf16[8,4,32,8,128]{4,3,2,1,0:T(8,128)(2,1)S(1)}, u32[]{:S(2)}, u32[]{:S(2)}) %all-to-all-start.1) | async-done | bytes 2097184 | tf_op jit(solution)/shard_map/all_to_all | solution.py:131
  67.3 0.5 multiply_reduce_fusion
  67.9 0.1 rsqrt.11
  68.0 2.5 %convert_element_type.66 = f32[8,4,32,8,128]{4,3,2,1,0:T(8,128)} convert(bf16[8,4,32,8,128]{4,3,2,1,0:T(8,128)(2,1)S(1)} %all-to-all-done.1) | non-fusion elementwise | flops 1048576 | bytes 6291456 | tf_op jit(solution)/shard_map/convert_element_type | solution.py:133
  70.5 31.3 %all-gather.2.cloned.1.call-done = bf16[648,4096]{1,0:T(8,128)(2,1)} async-done(((bf16[648,128]{1,0:T(8,128)(2,1)}), bf16[648,4096]{1,0:T(8,128)(2,1)}) %all-gather.2.cloned.1.call-update) | async-done | bytes 5308432 | tf_op jit(solution)/shard_map/all_gather | solution.py:123
  101.8 0.8 slice_convert_fusion
  102.7 5.6 %fusion = f32[256,640]{1,0:T(8,128)S(1)} fusion(bf16[648,4096]{1,0:T(8,128)(2,1)} %all-gather.2.cloned.1.call-done, f32[256,4096]{1,0:T(8,128)} %bitcast.42, f32[4096]{0:T(1024)S(1)} %bitcast.47, f32[256]{0:T(256)S(1)} %rsqrt.11), kind=kOutput, calls=%fused_computation.1 | convolution fusion | flops 1345323008 | bytes 10109952 | tf_op jit(solution)/shard_map/dot_general | solution.py:140
  108.4 0.6 fusion.10
  108.9 0.2 reshape.360
  109.1 0.1 fusion.16
  109.2 2.3 %gather_fusion = bf16[576,8,128]{2,1,0:T(8,128)(2,1)S(1)} fusion(bf16[32,8,128]{2,1,0:T(8,128)(2,1)S(1)} %fusion.16, s32[1024]{0:T(1024)S(1)} %pad_clamp_fusion), kind=kCustom, calls=%fused_computation | custom fusion | bytes 2361600 | tf_op jit(solution)/shard_map/jit(_take)/gather | solution.py:160
  111.6 0.5 subtract_convert_fusion
  112.1 1.3 pad_maximum_fusion
  113.4 9.7 %all-to-all-start.2 = ((bf16[32,176,128]{2,1,0:T(8,128)(2,1)}), bf16[32,176,128]{2,1,0:T(8,128)(2,1)S(1)}, u32[]{:S(2)}, u32[]{:S(2)}) async-start(bf16[32,176,128]{2,1,0:T(8,128)(2,1)} %pad_maximum_fusion), calls=%async_computation.2 | async-start | bytes 2883584 | tf_op jit(solution)/shard_map/all_to_all | solution.py:163
  123.2 0.2 iota_add_fusion
  123.4 31.2 %all-to-all-done.2 = bf16[32,176,128]{2,1,0:T(8,128)(2,1)S(1)} async-done(((bf16[32,176,128]{2,1,0:T(8,128)(2,1)}), bf16[32,176,128]{2,1,0:T(8,128)(2,1)S(1)}, u32[]{:S(2)}, u32[]{:S(2)}) %all-to-all-start.2) | async-done | bytes 1441824 | tf_op jit(solution)/shard_map/all_to_all | solution.py:163
  154.6 1.3 slice_bitcast_fusion.1
  155.9 0.1 add.214
  156.2 0.1 convert_reduce_fusion.1
  156.4 0.1 broadcast_in_dim.107
  156.5 0.2 add_reduce_fusion
  156.7 0.1 convert_reduce_fusion
  156.8 0.7 iota_add_fusion.1.qidx_ref
  157.5 0.2 fusion.2
  157.7 0.5 broadcast.338
  158.2 0.7 reduce.4
  158.9 0.7 reshape.386
  159.6 5.6 %all-to-all-start.3 = ((bf16[32,2,1024]{2,1,0:T(2,128)(2,1)}), bf16[32,2,1024]{2,1,0:T(2,128)(2,1)S(1)}, u32[]{:S(2)}, u32[]{:S(2)}) async-start(bf16[32,2,1024]{2,1,0:T(2,128)(2,1)} %reshape.386), calls=%async_computation.3 | async-start | bytes 262144 | tf_op jit(solution)/shard_map/all_to_all | solution.py:204
  165.2 0.2 fusion.17
  165.4 0.8 add.215.kidx_ref
  166.2 0.8 copy.27.qseg_ref
  167.0 0.6 reshape.368.kseg_ref
  167.6 0.9 reshape.364.q_ref
  168.5 7.5 %all-to-all-done.3 = bf16[32,2,1024]{2,1,0:T(2,128)(2,1)S(1)} async-done(((bf16[32,2,1024]{2,1,0:T(2,128)(2,1)}), bf16[32,2,1024]{2,1,0:T(2,128)(2,1)S(1)}, u32[]{:S(2)}, u32[]{:S(2)}) %all-to-all-start.3) | async-done | bytes 131104 | tf_op jit(solution)/shard_map/all_to_all | solution.py:204
  176.0 0.1 reshape.387
  176.1 0.2 fusion.5
  176.3 0.6 copy.34
  176.9 12.1 %shard_map.86 = bf16[256,512]{1,0:T(8,128)(2,1)} custom-call(s32[1]{0:T(128)} %bitcast.flag_ref, bf16[256,512]{1,0:T(8,128)(2,1)} %reshape.364.q_ref, bf16[4608,128]{1,0:T(8,128)(2,1)} %bitcast.14.a_ref, bf16[4608,128]{1,0:T(8,128)(2,1)} %bitcast.15.b_ref, s32[256,1]{1,0:T(8,128)} %copy.27.qseg_ref, s32[256,1]{1,0:T(8,128)} %iota_add_fusion.1.qidx_ref, ...), custom_call_target="tpu_custom_call" | custom-call | flops 2415919104 | bytes 2922496 | tf_op jit(solution)/shard_map/pallas_call | solution.py:91
  (36 shorter events, 0.7 us)
Async XLA Ops:
  7.2 1.0 copy-start
  7.2 94.6 %all-gather.2.cloned.1.call-start = ((), (), s32[]{:S(2)}) async-start(), calls=%async_computation.4 | async-start | bytes 5474304 | tf_op jit(solution)/shard_map/all_gather | solution.py:123
  36.7 5.0 %copy-start.3 = (s32[8]{0:T(128)S(1)}, s32[8]{0:T(128)}, u32[]{:S(2)}) copy-start(s32[8]{0:T(128)} %param.11) | copy-start | bytes 100
  36.7 5.2 %copy-start.2 = (s32[576]{0:T(1024)S(1)}, s32[576]{0:T(1024)}, u32[]{:S(2)}) copy-start(s32[576]{0:T(1024)} %constant.149) | copy-start | bytes 6916
  36.7 30.7 %all-to-all-start.1 = ((bf16[8,4,32,8,128]{4,3,2,1,0:T(8,128)(2,1)}), bf16[8,4,32,8,128]{4,3,2,1,0:T(8,128)(2,1)S(1)}, u32[]{:S(2)}, u32[]{:S(2)}) async-start(bf16[8,4,32,8,128]{4,3,2,1,0:T(8,128)(2,1)} %broadcast_in_dim.52), calls=%async_computation.1 | async-start | bytes 4194304 | tf_op jit(solution)/shard_map/all_to_all | solution.py:131
  113.4 9.7 %copy-start.1 = (s32[512]{0:T(512)S(1)}, s32[512]{0:T(512)}, u32[]{:S(2)}) copy-start(s32[512]{0:T(512)} %param.12) | copy-start | bytes 6148
  113.4 41.2 %all-to-all-start.2 = ((bf16[32,176,128]{2,1,0:T(8,128)(2,1)}), bf16[32,176,128]{2,1,0:T(8,128)(2,1)S(1)}, u32[]{:S(2)}, u32[]{:S(2)}) async-start(bf16[32,176,128]{2,1,0:T(8,128)(2,1)} %pad_maximum_fusion), calls=%async_computation.2 | async-start | bytes 2883584 | tf_op jit(solution)/shard_map/all_to_all | solution.py:163
  155.9 21.1 %collective-permute-start = (bf16[32,144,128]{2,1,0:T(8,128)(2,1)}, bf16[32,144,128]{2,1,0:T(8,128)(2,1)}, u32[]{:S(2)}, u32[]{:S(2)}) collective-permute-start(bf16[32,144,128]{2,1,0:T(8,128)(2,1)} %get-tuple-element.7), channel_id=1, source_target_pairs={{0,32},{32,0},{64,96},{96,64},{128,160},{160,128},{192,224},{224,1... | collective-permute-start | bytes 3538952 | tf_op jit(solution)/shard_map/ppermute | solution.py:166
  159.6 16.4 %all-to-all-start.3 = ((bf16[32,2,1024]{2,1,0:T(2,128)(2,1)}), bf16[32,2,1024]{2,1,0:T(2,128)(2,1)S(1)}, u32[]{:S(2)}, u32[]{:S(2)}) async-start(bf16[32,2,1024]{2,1,0:T(2,128)(2,1)} %reshape.386), calls=%async_computation.3 | async-start | bytes 262144 | tf_op jit(solution)/shard_map/all_to_all | solution.py:204
Sparse Core Ops, SparseCore 0:
  11.0 90.7 all-gather.1
